TPU v7x, 256 devices: a whole 4x4x8 slice. The times are simulated.
256 devices in a mesh: ka: 16 (over z, y_lo), band: 8 (over x, y_hi), ga: 2 (over core).
Axes of the slice: x: 4, y: 4 (y_hi: 2, y_lo: 2; y = y_hi * 2 + y_lo), z: 8, core: 2. Of those that a mesh axis runs over, the one named last changes fastest.
Arguments:
- pair_density: bfloat16 [8, 256, 8, 2048], P(None, ('ka', 'band')), may hold values from -4 to 4
- valence_energy: float32 [8, 8], replicated, may hold values from -6 to -1
- conduction_energy: float32 [8, 256], replicated, may hold values from 0.5 to 12
- star_map: int32 [64], replicated, may hold values from 0 to 7, as said below
- op_of_k: int32 [64], replicated, may hold values from 0 to 47
- perm_lists: int32 [48, 2048], replicated, may hold values from 0 to 2047, as said below
- cond_top: int32 [64], replicated, may hold values from 128 to 256
Outputs:
- chi: float32 [1, 2048, 2048], P(None, ('band', 'ga'), 'ka')
Inputs may be any that keep to these rules, and one draw needn't show every extreme that they name: `star_map`: every irreducible point is named by at least one full-zone k-point. `perm_lists`: each row is a permutation of 0 .. 2047 that maps every aligned block of 128 slots onto itself.
All inputs are finite; a program needn't handle non-finite values.
Results may differ from a plain program's by a relative error of at most 0.0015.
Values may be sent and summed in bfloat16 or wider, within the bound.
No kernel may reach another device: no remote copies, remote signals or barrier semaphores. Data moves between devices by JAX's collectives and lax.ppermute only.
A program may use at most 128 MiB of HBM per device.

v0:
```python
import jax
import jax.numpy as jnp
from jax import lax
from jax.sharding import PartitionSpec as P

NG = 2048
GB = 128
KI = 8
KF = 64
NF = 1


freq_step = 2.0


def rotate_batch(picked, perm_rows):
    k_count = picked.shape[0]
    blocks = NG // GB
    local = perm_rows.reshape(k_count, blocks, GB) - (jnp.arange(blocks) * GB)[None, :, None]
    onehot = (local[..., None] == jnp.arange(GB)[None, None, None, :]).astype(jnp.bfloat16)
    shaped = picked.reshape(k_count, -1, blocks, GB)
    moved = jnp.einsum("krbi,kboi->krbo", shaped, onehot, preferred_element_type=jnp.float32)
    return moved.astype(jnp.bfloat16).reshape(picked.shape)


def on_device(
    pair_density, valence_energy, conduction_energy, star_map, op_of_k, perm_lists, cond_top
):
    ka_count = lax.axis_size("ka")
    band_count = lax.axis_size("band")
    ga_count = lax.axis_size("ga")
    ka_index = lax.axis_index("ka")
    band_index = lax.axis_index("band")
    ga_index = lax.axis_index("ga")
    k_local = KF // ka_count
    cond_piece = pair_density.shape[1]
    my_points = ka_index * k_local + jnp.arange(k_local)
    stars = jnp.take(star_map, my_points)
    tops = jnp.take(cond_top, my_points)
    whole = lax.all_gather(pair_density, "ka", axis=1, tiled=True)
    picked = jnp.take(whole, stars, axis=0)
    my_perms = jnp.take(perm_lists, jnp.take(op_of_k, my_points), axis=0)
    rotated = rotate_batch(picked, my_perms)
    cond_table = conduction_energy.reshape(KI, ka_count, band_count, cond_piece)
    cond_table = lax.dynamic_slice_in_dim(cond_table, band_index, 1, 2).reshape(
        KI, ka_count * cond_piece
    )
    cond_local = jnp.take(cond_table, stars, axis=0)
    val_local = jnp.take(valence_energy, stars, axis=0)
    band_global = (
        jnp.arange(ka_count)[:, None] * band_count + band_index
    ) * cond_piece + jnp.arange(cond_piece)[None, :]
    band_global = band_global.reshape(ka_count * cond_piece)
    mask = (band_global[None, :] < tops[:, None]).astype(jnp.float32)[None, :, :, None]
    omega = freq_step * jnp.arange(NF).astype(jnp.float32)
    omega_sq = (omega * omega)[:, None, None, None]
    diff = val_local[:, None, :] - cond_local[:, :, None]
    weight = 4.0 / KF * diff[None] / (diff[None] * diff[None] + omega_sq) * mask
    product = weight[..., None] * rotated[None].astype(jnp.float32)
    scaled_hi = product.astype(jnp.bfloat16)
    hi_back = lax.optimization_barrier(scaled_hi).astype(jnp.float32)
    scaled_lo = (product - hi_back).astype(jnp.bfloat16)
    pair_rows = rotated.shape[0] * rotated.shape[1] * rotated.shape[2]
    flat_scaled = jnp.stack(
        [scaled_hi.reshape(NF, pair_rows, NG), scaled_lo.reshape(NF, pair_rows, NG)]
    )
    flat = rotated.reshape(pair_rows, NG)
    slab = NG // (band_count * ga_count)
    row_part = flat.reshape(pair_rows, band_count, ga_count, slab)
    row_part = lax.dynamic_slice_in_dim(row_part, ga_index, 1, 2).reshape(
        pair_rows, band_count * slab
    )
    partial_value = jnp.einsum(
        "rg,sfrh->fgh", row_part, flat_scaled, preferred_element_type=jnp.float32
    )
    column_sums = lax.psum_scatter(partial_value, "ka", scatter_dimension=2, tiled=True)
    return lax.psum_scatter(column_sums, "band", scatter_dimension=1, tiled=True)


def solution(mesh):
    return jax.shard_map(
        on_device,
        mesh=mesh,
        in_specs=(P(None, ("ka", "band"), None, None), P(), P(), P(), P(), P(), P()),
        out_specs=P(None, ("band", "ga"), "ka"),
        check_vma=False,
    )
```

profile of v0, /device:TPU:22, one launch (start us, length us, event | category | flops | bytes accessed | tf_op | source)
XLA Modules:
  0.0 545.4 jit_solution(13602813167420612139)
XLA Ops:
  6.5 0.7 all-gather.2.cloned.1.call-update
  7.3 1.3 gather_fusion.6
  8.6 1.3 gather_fusion.5
  9.9 1.3 gather_fusion.4
  11.2 0.1 iota_add_fusion
  11.3 0.1 add.71
  11.4 0.8 copy.11
  12.3 1.2 gather_fusion
  13.6 0.6 gather_fusion.1
  14.2 0.1 compare_convert_fusion
  14.4 0.1 fusion.6
  14.5 0.1 mul.115
  14.6 0.6 gather_fusion.2
  15.2 0.1 fusion.7
  15.3 178.8 %all-gather.2.cloned.1.call-done = bf16[8,32,8,2048]{3,2,1,0:T(8,128)(2,1)} async-done(((bf16[8,2,8,2048]{3,2,1,0:T(8,128)(2,1)}), bf16[8,32,8,2048]{3,2,1,0:T(8,128)(2,1)}) %all-gather.2.cloned.1.call-update) | async-done | bytes 8388624 | tf_op jit(solution)/shard_map/all_gather | solution.py:40
  194.1 6.2 %gather_fusion.3 = bf16[4,32,8,2048]{3,2,1,0:T(8,128)(2,1)} fusion(bf16[8,32,8,2048]{3,2,1,0:T(8,128)(2,1)} %all-gather.2.cloned.1.call-done, s32[1024]{0:T(1024)S(1)} %pad_clamp_fusion.1), kind=kCustom, calls=%fused_computation.6 | custom fusion | bytes 8388624 | tf_op jit(solution)/shard_map/jit(_take)/gather | solution.py:41
  200.2 3.6 copy.20
  203.8 3.7 convert_bitcast_fusion
  207.5 6.4 %copy.16 = bf16[4,256,16,128]{3,1,0,2:T(8,128)(2,1)} copy(bf16[4,256,16,128]{1,3,2,0:T(8,128)(2,1)} %convert_bitcast_fusion) | data formatting | bytes 8388608 | tf_op jit(solution)/shard_map/convert_element_type | solution.py:23
  213.9 8.4 %copy.14 = f32[4,256,16,128]{3,2,1,0:T(8,128)} copy(bf16[4,256,16,128]{1,3,2,0:T(8,128)(2,1)} %convert_bitcast_fusion) | data formatting | bytes 12582912 | tf_op jit(solution)/shard_map/convert_element_type | solution.py:59
  222.3 9.3 %reshape.255 = f32[1,4,32,8,2048]{4,3,2,1,0:T(8,128)} reshape(f32[4,256,16,128]{3,2,1,0:T(8,128)} %copy.14) | data formatting | bytes 16777216 | tf_op jit(solution)/shard_map/convert_element_type | solution.py:59
  231.5 9.2 %reshape.254 = f32[1,1024,2048]{2,1,0:T(8,128)} reshape(f32[4,256,16,128]{3,2,1,0:T(8,128)} %copy.14) | data formatting | bytes 16777216 | tf_op jit(solution)/shard_map/convert_element_type | solution.py:59
  240.8 1.7 constant_dynamic-slice_fusion
  242.5 2.6 copy.17
  245.2 4.0 multiply_convert_fusion.1
  249.2 6.5 %subtract_convert_fusion = bf16[1,4,32,8,2048]{4,3,2,1,0:T(8,128)(2,1)} fusion(bf16[1,4,32,8,2048]{4,3,2,1,0:T(8,128)(2,1)S(1)} %multiply_convert_fusion.1, f32[1,4,32,8,2048]{4,3,2,1,0:T(8,128)} %reshape.255, f32[4,32,8]{2,1,0:T(8,128)S(1)} %fusion.6), kind=kLoop, calls=%fused_computation.8 | loop fusion | flops 8388608 | bytes 16781312 | tf_op jit(solution)/shard_map/convert_element_type | solution.py:62
  255.7 0.5 fusion
  256.2 7.4 %convert_reduce_fusion = bf16[1024,2048]{1,0:T(8,128)(2,1)} fusion(bf16[1,1,1024,2048]{3,2,1,0:T(8,128)(2,1)} %bitcast.31, bf16[1,1,1024,2048]{3,2,1,0:T(8,128)(2,1)S(1)} %fusion), kind=kLoop, calls=%fused_computation.7 | loop fusion | flops 18874368 | bytes 12582912 | tf_op jit(solution)/shard_map/rg,sfrh->fgh/reduce_sum | solution.py:73
  263.6 10.7 %convolution_bitcast_fusion = f32[1,1024,2048]{1,2,0:T(8,128)} fusion(bf16[1024,2048]{1,0:T(8,128)(2,1)} %convert_reduce_fusion, bf16[1024,1024]{0,1:T(8,128)(2,1)} %bitcast.35), kind=kOutput, calls=%fused_computation.11 | convolution fusion | flops 4294967296 | bytes 14680064 | tf_op jit(solution)/shard_map/rg,sfrh->fgh/dot_general | solution.py:73
  274.4 183.7 %reduce-scatter.3.cloned.1.call-done = f32[1,1024,128]{1,2,0:T(8,128)} async-done(((f32[1,1024,2048]{1,2,0:T(8,128)}), f32[1,1024,128]{1,2,0:T(8,128)}) %reduce-scatter.3.cloned.1.call-update) | async-done | bytes 524304 | tf_op jit(solution)/shard_map/reduce_scatter | solution.py:76
  458.1 79.3 %reduce-scatter.5.cloned.1.call-done = f32[1,128,128]{1,2,0:T(8,128)} async-done(((f32[1,1024,128]{1,2,0:T(8,128)}), f32[1,128,128]{1,2,0:T(8,128)}) %reduce-scatter.5.cloned.1.call-update) | async-done | bytes 65552 | tf_op jit(solution)/shard_map/reduce_scatter | solution.py:77
  537.3 1.6 copy.18
  (26 shorter events, 0.4 us)
Async XLA Ops:
  6.5 8.1 %copy-start = (s32[48,2048]{1,0:T(8,128)S(1)}, s32[48,2048]{1,0:T(8,128)}, u32[]{:S(2)}) copy-start(s32[48,2048]{1,0:T(8,128)} %param.14) | copy-start | bytes 1179652
  6.5 187.5 %all-gather.2.cloned.1.call-start = ((), (), s32[]{:S(2)}) async-start(), calls=%async_computation.2 | async-start | bytes 8912896 | tf_op jit(solution)/shard_map/all_gather | solution.py:40
  7.3 450.8 %reduce-scatter.3.cloned.1.call-start = ((), (), s32[]{:S(2)}) async-start(), calls=%async_computation.3 | async-start | bytes 8912896 | tf_op jit(solution)/shard_map/reduce_scatter | solution.py:76
  245.2 10.5 %slice-start = ((s8[8388608]{0:T(1024)(128)(4,1)}), s8[4194304]{0:T(1024)(128)(4,1)S(1)}, s32[]{:S(2)}) async-start(s8[8388608]{0:T(1024)(128)(4,1)} %bitcast.29), calls=%async_computation.5 | async-start | bytes 8388608
  249.2 6.5 %slice-start.1 = ((s8[8388608]{0:T(1024)(128)(4,1)}), s8[4194304]{0:T(1024)(128)(4,1)S(1)}, s32[]{:S(2)}) async-start(s8[8388608]{0:T(1024)(128)(4,1)} %bitcast.29), calls=%async_computation.6 | async-start | bytes 8388608
  274.3 264.6 %copy-start.1 = (s32[48,2048]{1,0:T(8,128)S(1)}, s32[48,2048]{1,0:T(8,128)}, u32[]{:S(2)}) copy-start(s32[48,2048]{1,0:T(8,128)} %param.14) | copy-start | bytes 1179652
  274.3 263.0 %reduce-scatter.5.cloned.1.call-start = ((), (), s32[]{:S(2)}) async-start(), calls=%async_computation.4 | async-start | bytes 589824 | tf_op jit(solution)/shard_map/reduce_scatter | solution.py:77
Sparse Core Ops, SparseCore 0:
  9.1 184.8 all-gather.1
  274.4 183.5 reduce-scatter.2
  461.9 75.3 reduce-scatter.4
where the time goes:
time: 549 us; the launch traced here: 545 us
  waiting for transfers between devices  442 us (81%)
  local copies, waits for them, and re-layouts  56.3 us (10%)
  other arithmetic  18.9 us (3%)
  matrix products  14.4 us (3%)
  between operations  13.3 us (2%)
    reduce_scatter x1, waiting for transfers between devices, on_device(): lax.psum_scatter(partial_value, 'ka', scatter_dimension=2, tiled=True)  184 us
    all_gather x1, waiting for transfers between devices, on_device(): whole = lax.all_gather(pair_density, 'ka', axis=1, tiled=True)  179 us
    reduce_scatter x1, waiting for transfers between devices, on_device(): lax.psum_scatter(column_sums, 'band', scatter_dimension=1, tiled=True)  79.3 us
    convert_element_type x3, local copies, waits for them, and re-layouts, on_device(): product = weight[..., None] * rotated[None].astype(jnp.float32)  26.9 us
  transfers between devices with their start and end apart: 3, of which 3 were waited for; matrix products, arithmetic and copies ran while one was open for 1% of the time, Pallas kernels for 0%

commit v1 on v0

v1 whole, which is shorter than its diff:
```python
import jax
import jax.numpy as jnp
from jax import lax
from jax.sharding import PartitionSpec as P

NG = 2048
GB = 128
KI = 8
KF = 64
NF = 1
NV = 8

BW = 512
NB = NG // BW
PAIR = ((0, 1), (2, 3), (0, 1), (0, 2), (0, 3), (1, 2), (1, 3), (2, 3))
LOCAL = (((0, 0), (1, 1)), ((0, 0), (1, 1))) + (((0, 1), (1, 0)),) * 6


freq_step = 2.0


def slab_perm(ka_count, band_count, ga_count):
    pieces = BW // GB
    pairs = []
    for i in range(ka_count):
        for j in range(band_count):
            for g in range(ga_count):
                row_block = PAIR[j][LOCAL[j][g][0]]
                col_block = PAIR[j][LOCAL[j][g][1]]
                r = row_block * pieces + i // pieces
                cs = col_block * pieces + i % pieces
                src = (i * band_count + j) * ga_count + g
                dst = (cs * band_count + r // ga_count) * ga_count + r % ga_count
                pairs.append((src, dst))
    return pairs


def on_device(
    pair_density, valence_energy, conduction_energy, star_map, op_of_k, perm_lists, cond_top
):
    ka_count = lax.axis_size("ka")
    band_count = lax.axis_size("band")
    ga_count = lax.axis_size("ga")
    assert (ka_count, band_count, ga_count) == (16, 8, 2)
    ka_index = lax.axis_index("ka")
    band_index = lax.axis_index("band")
    ga_index = lax.axis_index("ga")
    cond_piece = pair_density.shape[1]
    pair = jnp.asarray(PAIR, jnp.int32)
    local_tab = jnp.asarray(LOCAL, jnp.int32)

    blocked = pair_density.reshape(KI, cond_piece, NV, NB, BW)
    send = jnp.take(blocked, pair.reshape(-1), axis=3)
    send = send.reshape(KI, cond_piece, NV, band_count, 2, BW)
    send = jnp.moveaxis(send, 3, 0)
    recv = lax.all_to_all(send, "band", 0, 0, tiled=False)
    c_loc = band_count * cond_piece
    loc = jnp.moveaxis(recv, 0, 1).reshape(KI, c_loc, NV, 2, BW)

    picked = jnp.take(loc, star_map, axis=0)
    my_pair = pair[band_index]
    perm_blocks = perm_lists.reshape(perm_lists.shape[0], NB, BW)
    my_perm = jnp.take(jnp.take(perm_blocks, op_of_k, axis=0), my_pair, axis=1)
    subs = BW // GB
    local = my_perm.reshape(KF, 2 * subs, GB) - (
        my_pair.repeat(subs) * BW + (jnp.arange(2 * subs) % subs) * GB
    )[None, :, None]
    onehot = (local[..., None] == jnp.arange(GB)[None, None, None, :]).astype(jnp.bfloat16)
    shaped = picked.reshape(KF, c_loc * NV, 2 * subs, GB)
    rotated = jnp.einsum("krbi,kboi->krbo", shaped, onehot, preferred_element_type=jnp.float32)
    rotated = rotated.astype(jnp.bfloat16).reshape(KF, c_loc, NV, 2, BW)

    c_base = ka_index * c_loc
    cond_grp = lax.dynamic_slice_in_dim(conduction_energy, c_base, c_loc, axis=1)
    cond_local = jnp.take(cond_grp, star_map, axis=0)
    val_local = jnp.take(valence_energy, star_map, axis=0)
    band_global = c_base + jnp.arange(c_loc)
    mask = (band_global[None, :] < cond_top[:, None]).astype(jnp.float32)[None, :, :, None]
    omega = freq_step * jnp.arange(NF).astype(jnp.float32)
    omega_sq = (omega * omega)[:, None, None, None]
    diff = val_local[:, None, :] - cond_local[:, :, None]
    weight = 4.0 / KF * diff[None] / (diff[None] * diff[None] + omega_sq) * mask

    row_sel = local_tab[band_index, ga_index, 0]
    col_sel = local_tab[band_index, ga_index, 1]
    rot_row = lax.dynamic_index_in_dim(rotated, row_sel, axis=3, keepdims=False)
    rot_col = lax.dynamic_index_in_dim(rotated, col_sel, axis=3, keepdims=False)
    product = weight[..., None] * rot_col[None].astype(jnp.float32)
    scaled_hi = product.astype(jnp.bfloat16)
    hi_back = lax.optimization_barrier(scaled_hi).astype(jnp.float32)
    scaled_lo = (product - hi_back).astype(jnp.bfloat16)
    pair_rows = KF * c_loc * NV
    flat_scaled = jnp.stack(
        [scaled_hi.reshape(NF, pair_rows, BW), scaled_lo.reshape(NF, pair_rows, BW)]
    )
    partial_value = jnp.einsum(
        "rg,sfrh->fgh", rot_row.reshape(pair_rows, BW), flat_scaled,
        preferred_element_type=jnp.float32,
    )

    pieces = partial_value.reshape(NF, subs, GB, subs, GB).transpose(1, 3, 0, 2, 4)
    pieces = pieces.reshape(subs * subs, NF, GB, GB)
    got = lax.all_to_all(pieces, "ka", 0, 0, tiled=False)
    slab = got.sum(axis=0)
    return lax.ppermute(
        slab, ("ka", "band", "ga"), slab_perm(ka_count, band_count, ga_count)
    )


def solution(mesh):
    return jax.shard_map(
        on_device,
        mesh=mesh,
        in_specs=(P(None, ("ka", "band"), None, None), P(), P(), P(), P(), P(), P()),
        out_specs=P(None, ("band", "ga"), "ka"),
        check_vma=False,
    )
```

time: 549 us -> 352 us (0.64)
  waiting for transfers between devices: 442 us -> 18.9 us
  local copies, waits for them, and re-layouts: 56.3 us -> 167 us
  other arithmetic: 18.9 us -> 84.4 us
  blocking collectives: 0 us -> 36.9 us
  starting transfers between devices: 0.08 us -> 11.7 us
  matrix products: 14.4 us -> 25.3 us
  between operations: 13.3 us -> 3.78 us
    reduce_scatter x2 -> x0, waiting for transfers between devices: 263 us -> none  [the longest x1 184 us: on_device(): lax.psum_scatter(partial_value, 'ka', scatter_dimension=2, tiled=True)]
    all_gather x1 -> x0, waiting for transfers between devices: 179 us -> none  [on_device(): whole = lax.all_gather(pair_density, 'ka', axis=1, tiled=True)]
    gather x7 -> x10, local copies, waits for them, and re-layouts: 12.4 us -> 63.1 us  [the longest x3 58.7 us: on_device(): picked = jnp.take(loc, star_map, axis=0)]
    all_to_all x0 -> x1, blocking collectives: none -> 36.9 us  [on_device(): got = lax.all_to_all(pieces, 'ka', 0, 0, tiled=False)]
    reshape x1 -> x4, local copies, waits for them, and re-layouts: 0.07 us -> 26.9 us  [the longest x1 24.9 us: on_device(): rotated = rotated.astype(jnp.bfloat16).reshape(KF, c_loc, NV, 2, BW)]
    unnamed x10, local copies, waits for them, and re-layouts: 4.42 us -> 27 us
    convert_element_type x1, other arithmetic: 4.03 us -> 26.2 us  [on_device(): scaled_hi = product.astype(jnp.bfloat16)]
    convert_element_type x1, other arithmetic: 6.49 us -> 27.2 us  [on_device(): scaled_lo = (product - hi_back).astype(jnp.bfloat16)]
  transfers between devices with their start and end apart: 3 -> 2, of which waited for: 3 -> 2; matrix products, arithmetic and copies ran while one was open for 1% -> 4% of each run, Pallas kernels for 0% -> 0%
where the time goes in v1:
time: 352 us; the launch traced here: 348 us
  local copies, waits for them, and re-layouts  167 us (47%)
  other arithmetic  84.4 us (24%)
  blocking collectives  36.9 us (10%)
  matrix products  25.3 us (7%)
  waiting for transfers between devices  18.9 us (5%)
  starting transfers between devices  11.7 us (3%)
  between operations  3.78 us (1%)
    gather x3, local copies, waits for them, and re-layouts, on_device(): picked = jnp.take(loc, star_map, axis=0)  58.7 us
    all_to_all x1, blocking collectives, on_device(): got = lax.all_to_all(pieces, 'ka', 0, 0, tiled=False)  36.9 us
    convert_element_type x1, other arithmetic, on_device(): scaled_lo = (product - hi_back).astype(jnp.bfloat16)  27.2 us
    unnamed x10, local copies, waits for them, and re-layouts  27 us
    convert_element_type x1, other arithmetic, on_device(): scaled_hi = product.astype(jnp.bfloat16)  26.2 us
    reshape x1, local copies, waits for them, and re-layouts, on_device(): rotated = rotated.astype(jnp.bfloat16).reshape(KF, c_loc, NV, 2, BW)  24.9 us
    convert_element_type x1, local copies, waits for them, and re-layouts, on_device(): rotated = rotated.astype(jnp.bfloat16).reshape(KF, c_loc, NV, 2, BW)  22.9 us
    dynamic_slice x1, local copies, waits for them, and re-layouts, on_device(): rot_row = lax.dynamic_index_in_dim(rotated, row_sel, axis=3, keepdims=False)  20.9 us
  transfers between devices with their start and end apart: 2, of which 2 were waited for; matrix products, arithmetic and copies ran while one was open for 4% of the time, Pallas kernels for 0%

profile of v1, /device:TPU:22, one launch (start us, length us, event | category | flops | bytes accessed | tf_op | source)
XLA Modules:
  0.0 347.9 jit_solution(10553102851344910025)
XLA Ops:
  0.0 0.7 pad_clamp_fusion
  1.8 1.6 copy.43
  3.4 7.2 %all-to-all-start = ((bf16[8,8,2,8,2,512]{5,3,4,2,1,0:T(8,128)(2,1)}), bf16[8,8,2,8,2,512]{5,3,4,2,1,0:T(8,128)(2,1)}, u32[]{:S(2)}, u32[]{:S(2)}) async-start(bf16[8,8,2,8,2,512]{5,3,4,2,1,0:T(8,128)(2,1)} %copy.43), calls=%async_computation | async-start | bytes 4194304 | tf_op jit(solution)/shard_map/all_to_all | solution.py:56
  11.9 1.3 constant_dynamic-slice_fusion
  17.3 0.7 compare_convert_fusion
  18.1 0.8 constant_dynamic-slice_fusion.3
  19.5 1.3 gather_fusion
  20.8 1.3 reshape.327
  22.0 0.9 gather_fusion.2
  23.9 0.7 fusion.11
  27.7 10.3 %all-to-all-done = bf16[8,8,2,8,2,512]{5,3,4,2,1,0:T(8,128)(2,1)} async-done(((bf16[8,8,2,8,2,512]{5,3,4,2,1,0:T(8,128)(2,1)}), bf16[8,8,2,8,2,512]{5,3,4,2,1,0:T(8,128)(2,1)}, u32[]{:S(2)}, u32[]{:S(2)}) %all-to-all-start) | async-done | bytes 2097184 | tf_op jit(solution)/shard_map/all_to_all | solution.py:56
  38.0 1.8 copy.44
  39.8 7.6 %gather_fusion.5 = bf16[64,16,8,2,512]{4,2,3,1,0:T(8,128)(2,1)} fusion(bf16[8,16,8,2,512]{4,2,3,1,0:T(8,128)(2,1)S(1)} %bitcast.50, s32[1024]{0:T(1024)S(1)} %pad_clamp_fusion.3), kind=kCustom, calls=%fused_computation.5 | custom fusion | bytes 33554688 | tf_op jit(solution)/shard_map/jit(_take)/gather | solution.py:60
  47.3 24.2 %copy.45 = bf16[64,16,8,2,512]{4,3,2,1,0:T(2,128)(2,1)} copy(bf16[64,16,8,2,512]{4,2,3,1,0:T(8,128)(2,1)} %gather_fusion.5) | data formatting | bytes 33554432 | tf_op jit(solution)/shard_map/jit(_take)/gather | solution.py:60
  71.6 26.9 %gather.38 = bf16[64,128,8,128]{3,2,1,0:T(8,128)(2,1)} reshape(bf16[64,16,8,2,512]{4,3,2,1,0:T(2,128)(2,1)} %copy.45) | data formatting | bytes 33554432 | tf_op jit(solution)/shard_map/jit(_take)/gather | solution.py:60
  98.4 8.5 %broadcast_select_fusion = bf16[64,128,8,128]{3,2,1,0:T(8,128)(2,1)S(1)} fusion(bf16[64,128,8,128]{3,2,1,0:T(8,128)(2,1)} %gather.38, pred[64]{0:T(512)(128)(4,1)S(1)} %get-tuple-element.10), kind=kLoop, calls=%fused_computation.16 | loop fusion | flops 8388608 | bytes 33554496 | tf_op jit(solution)/shard_map/jit(_take)/select_n | solution.py:60
  107.0 15.8 %convert_bitcast_fusion = bf16[64,128,8,128]{1,3,2,0:T(8,128)(2,1)} fusion(bf16[64,128,8,128]{3,2,1,0:T(8,128)(2,1)S(1)} %broadcast_select_fusion, s32[64,8,128]{2,1,0:T(8,128)S(1)} %select_subtract_fusion), kind=kOutput, calls=%fused_computation.14 | convolution fusion | flops 2164260864 | bytes 33816576 | tf_op jit(solution)/shard_map/krbi,kboi->krbo/dot_general | solution.py:70
  122.8 22.9 %copy.47 = bf16[64,128,8,128]{3,2,1,0:T(8,128)(2,1)} copy(bf16[64,128,8,128]{1,3,2,0:T(8,128)(2,1)} %convert_bitcast_fusion) | data formatting | bytes 33554432 | tf_op jit(solution)/shard_map/convert_element_type | solution.py:71
  145.7 24.9 %reshape.331 = bf16[64,16,8,2,512]{4,3,2,1,0:T(2,128)(2,1)} reshape(bf16[64,128,8,128]{3,2,1,0:T(8,128)(2,1)} %copy.47) | data formatting | bytes 33554432 | tf_op jit(solution)/shard_map/reshape | solution.py:71
  170.6 20.9 %constant_dynamic-slice_fusion.1 = bf16[64,16,8,1,512]{4,3,2,1,0:T(2,128)(2,1)S(1)} fusion(bf16[64,16,8,2,512]{4,3,2,1,0:T(2,128)(2,1)} %reshape.331, s32[]{:T(128)S(6)} %select_n.132), kind=kLoop, calls=%fused_computation.42 | loop fusion | bytes 16777220 | tf_op jit(solution)/shard_map/jit(dynamic_index_in_dim)/dynamic_slice | solution.py:86
  191.5 4.8 %copy.53 = bf16[64,16,8,1,512]{4,2,3,1,0:T(8,128)(2,1)} copy(bf16[64,16,8,1,512]{4,3,2,1,0:T(2,128)(2,1)S(1)} %constant_dynamic-slice_fusion.1) | data formatting | bytes 16777216
  196.3 26.2 %fusion.5 = (bf16[1,64,16,8,512]{4,0,3,2,1:T(2,128)(2,1)}, f32[64,16,8,1,512]{4,3,2,1,0:T(1,128)S(1)}) fusion(f32[64,16,8]{2,1,0:T(8,128)S(1)} %fusion.8, bf16[64,16,8,2,512]{4,3,2,1,0:T(2,128)(2,1)} %reshape.331, s32[]{:T(128)S(6)} %select_n.131), kind=kLoop, calls=%fused_computation.17 | loop fusion | flops 12582912 | bytes 33587204 | tf_op jit(solution)/shard_map/convert_element_type | solution.py:89
  222.5 7.6 %copy.51 = f32[64,16,8,1,512]{4,2,3,1,0:T(8,128)} copy(f32[64,16,8,1,512]{4,3,2,1,0:T(1,128)S(1)} %get-tuple-element.6) | data formatting | bytes 33554432
  230.0 27.2 %subtract_convert_fusion = bf16[1,64,16,8,512]{4,0,3,2,1:T(2,128)(2,1)} fusion(bf16[1,64,16,8,512]{4,0,3,2,1:T(2,128)(2,1)} %get-tuple-element.5, f32[64,16,8,1,512]{4,3,2,1,0:T(1,128)S(1)} %get-tuple-element.6, f32[64,16,8]{2,1,0:T(8,128)S(1)} %fusion.8), kind=kLoop, calls=%fused_computation.11 | loop fusion | flops 16777216 | bytes 33587200 | tf_op jit(solution)/shard_map/convert_element_type | solution.py:91
  257.3 12.5 %copy.52 = bf16[1,64,16,8,512]{4,3,0,2,1:T(8,128)(2,1)} copy(bf16[1,64,16,8,512]{4,0,3,2,1:T(2,128)(2,1)} %subtract_convert_fusion) | data formatting | bytes 16777216
  269.7 1.2 copy-done.2
  271.0 4.0 %fusion.6 = bf16[1,1,8192,512]{3,2,1,0:T(8,128)(2,1)} fusion(f32[1,8192,512]{2,1,0:T(8,128)S(1)} %bitcast.51, f32[8192]{0:T(1024)S(1)} %mul.108), kind=kLoop, calls=%fused_computation.18 | loop fusion | flops 8388608 | bytes 25198592 | tf_op jit(solution)/shard_map/stack | solution.py:93
  275.0 12.1 %convert_reduce_fusion = bf16[8192,512]{1,0:T(8,128)(2,1)} fusion(bf16[1,1,8192,512]{3,2,1,0:T(8,128)(2,1)} %bitcast.52, bf16[1,1,8192,512]{3,2,1,0:T(8,128)(2,1)} %fusion.6), kind=kLoop, calls=%fused_computation.6 | loop fusion | flops 37748736 | bytes 25165824 | tf_op jit(solution)/shard_map/rg,sfrh->fgh/reduce_sum | solution.py:96
  287.0 9.5 %convolution_bitcast_fusion = f32[1,512,512]{1,2,0:T(8,128)S(1)} fusion(bf16[8192,512]{1,0:T(8,128)(2,1)} %convert_reduce_fusion, bf16[8192,512]{1,0:T(8,128)(2,1)} %bitcast.53), kind=kOutput, calls=%fused_computation.19 | convolution fusion | flops 4294967296 | bytes 17825792 | tf_op jit(solution)/shard_map/rg,sfrh->fgh/dot_general | solution.py:96
  297.3 36.9 %all_to_all.10 = f32[16,1,128,128]{3,2,1,0:T(8,128)S(1)} all-to-all(f32[16,1,128,128]{3,2,1,0:T(8,128)S(1)} %bitcast.55), channel_id=1, replica_groups=mesh['ka'=16,'band'=8,'ga'=2] {'ka'}, dimensions={0} | all-to-all | bytes 2097152 | tf_op jit(solution)/shard_map/all_to_all | solution.py:103
  334.2 4.5 %collective-permute-start = (f32[1,128,128]{2,1,0:T(8,128)S(1)}, f32[1,128,128]{2,1,0:T(8,128)S(1)}, u32[]{:S(2)}, u32[]{:S(2)}) collective-permute-start(f32[1,128,128]{2,1,0:T(8,128)S(1)} %bitcast.57), channel_id=1, source_target_pairs={{0,0},{1,68},{2,136},{3,204},{4,64},{5,4},{6,128},{7,8},{8,192},{9... | collective-permute-start | bytes 196616 | tf_op jit(solution)/shard_map/ppermute | solution.py:105
  338.7 8.6 %collective-permute-done = f32[1,128,128]{2,1,0:T(8,128)S(1)} collective-permute-done((f32[1,128,128]{2,1,0:T(8,128)S(1)}, f32[1,128,128]{2,1,0:T(8,128)S(1)}, u32[]{:S(2)}, u32[]{:S(2)}) %collective-permute-start) | collective-permute-done | bytes 65568 | tf_op jit(solution)/shard_map/ppermute | solution.py:105
  (36 shorter events, 9.0 us)
Async XLA Ops:
  0.0 1.1 copy-start
  3.4 34.6 %all-to-all-start = ((bf16[8,8,2,8,2,512]{5,3,4,2,1,0:T(8,128)(2,1)}), bf16[8,8,2,8,2,512]{5,3,4,2,1,0:T(8,128)(2,1)}, u32[]{:S(2)}, u32[]{:S(2)}) async-start(bf16[8,8,2,8,2,512]{5,3,4,2,1,0:T(8,128)(2,1)} %copy.43), calls=%async_computation | async-start | bytes 4194304 | tf_op jit(solution)/shard_map/all_to_all | solution.py:56
  257.3 13.7 %copy-start.2 = (f32[64,16,8,1,512]{4,2,3,1,0:T(8,128)S(1)}, f32[64,16,8,1,512]{4,2,3,1,0:T(8,128)}, u32[]{:S(2)}) copy-start(f32[64,16,8,1,512]{4,2,3,1,0:T(8,128)} %copy.51) | copy-start | bytes 50331652
  274.9 73.0 %copy-start.1 = (bf16[8,2,8,2048]{3,2,1,0:T(8,128)(2,1)S(1)}, bf16[8,2,8,2048]{3,2,1,0:T(8,128)(2,1)}, u32[]{:S(2)}) copy-start(bf16[8,2,8,2048]{3,2,1,0:T(8,128)(2,1)} %param.9) | copy-start | bytes 1572868
  334.2 13.1 %collective-permute-start = (f32[1,128,128]{2,1,0:T(8,128)S(1)}, f32[1,128,128]{2,1,0:T(8,128)S(1)}, u32[]{:S(2)}, u32[]{:S(2)}) collective-permute-start(f32[1,128,128]{2,1,0:T(8,128)S(1)} %bitcast.57), channel_id=1, source_target_pairs={{0,0},{1,68},{2,136},{3,204},{4,64},{5,4},{6,128},{7,8},{8,192},{9... | collective-permute-start | bytes 196616 | tf_op jit(solution)/shard_map/ppermute | solution.py:105

commit v2 on v1

v2 whole, which is shorter than its diff:
```python
import jax
import jax.numpy as jnp
from jax import lax
from jax.experimental import pallas as pl
from jax.experimental.pallas import tpu as pltpu
from jax.sharding import PartitionSpec as P

NG = 2048
GB = 128
KI = 8
KF = 64
NF = 1
NV = 8

BW = 512
NB = NG // BW
PAIR = ((0, 1), (2, 3), (0, 1), (0, 2), (0, 3), (1, 2), (1, 3), (2, 3))
LOCAL = (((0, 0), (1, 1)), ((0, 0), (1, 1))) + (((0, 1), (1, 0)),) * 6
BLOCKS = tuple(
    tuple((PAIR[j][LOCAL[j][g][0]], PAIR[j][LOCAL[j][g][1]]) for g in range(2))
    for j in range(len(PAIR))
)
KB = 4


freq_step = 2.0


def chi_kernel(star_ref, loc_ref, perm_ref, w_ref, out_ref):
    step = pl.program_id(0)

    @pl.when(step == 0)
    def _():
        out_ref[...] = jnp.zeros_like(out_ref)

    lane = lax.broadcasted_iota(jnp.int32, (GB, GB), 1)
    nt = (((1,), (1,)), ((), ()))
    for t in range(KB):
        x = loc_ref[star_ref[step * KB + t]]
        slots = perm_ref[t]
        parts = []
        for q in range(2 * BW // GB):
            onehot = jnp.where(slots[:, q : q + 1] == lane, 1.0, 0.0).astype(jnp.bfloat16)
            parts.append(
                lax.dot_general(
                    onehot, x[:, q * GB : (q + 1) * GB], nt,
                    preferred_element_type=jnp.float32,
                )
            )
        rot_t = jnp.concatenate(parts, axis=0)
        row_t = rot_t[:BW].astype(jnp.bfloat16)
        col_t = rot_t[BW:]
        lhs = jnp.concatenate([row_t, row_t], axis=1)
        for f in range(NF):
            product = col_t * w_ref[t, f : f + 1, :]
            scaled_hi = product.astype(jnp.bfloat16)
            scaled_lo = (product - scaled_hi.astype(jnp.float32)).astype(jnp.bfloat16)
            rhs = jnp.concatenate([scaled_hi, scaled_lo], axis=1)
            out_ref[f] += lax.dot_general(lhs, rhs, nt, preferred_element_type=jnp.float32)


def chi_block(star_map, loc, perm_t, weight_t):
    rows = loc.shape[1]
    return pl.pallas_call(
        chi_kernel,
        out_shape=jax.ShapeDtypeStruct((NF, BW, BW), jnp.float32),
        grid_spec=pltpu.PrefetchScalarGridSpec(
            num_scalar_prefetch=1,
            grid=(KF // KB,),
            in_specs=[
                pl.BlockSpec((KI, rows, 2 * BW), lambda st, sm: (0, 0, 0)),
                pl.BlockSpec((KB, GB, 2 * BW // GB), lambda st, sm: (st, 0, 0)),
                pl.BlockSpec((KB, NF, rows), lambda st, sm: (st, 0, 0)),
            ],
            out_specs=pl.BlockSpec((NF, BW, BW), lambda st, sm: (0, 0, 0)),
        ),
        compiler_params=pltpu.CompilerParams(dimension_semantics=("arbitrary",)),
    )(star_map, loc, perm_t, weight_t)


def slab_perm(ka_count, band_count, ga_count):
    pieces = BW // GB
    pairs = []
    for i in range(ka_count):
        for j in range(band_count):
            for g in range(ga_count):
                row_block, col_block = BLOCKS[j][g]
                r = row_block * pieces + i // pieces
                cs = col_block * pieces + i % pieces
                src = (i * band_count + j) * ga_count + g
                dst = (cs * band_count + r // ga_count) * ga_count + r % ga_count
                pairs.append((src, dst))
    return pairs


def on_device(
    pair_density, valence_energy, conduction_energy, star_map, op_of_k, perm_lists, cond_top
):
    ka_count = lax.axis_size("ka")
    band_count = lax.axis_size("band")
    ga_count = lax.axis_size("ga")
    assert (ka_count, band_count, ga_count) == (16, 8, 2)
    ka_index = lax.axis_index("ka")
    band_index = lax.axis_index("band")
    ga_index = lax.axis_index("ga")
    cond_piece = pair_density.shape[1]
    blocks = jnp.asarray(BLOCKS, jnp.int32)

    blocked = pair_density.reshape(KI, cond_piece, NV, NB, BW)
    send = jnp.take(blocked, blocks[:, ga_index].reshape(-1), axis=3)
    send = send.reshape(KI, cond_piece, NV, band_count, 2, BW)
    send = jnp.moveaxis(send, 3, 0)
    recv = lax.all_to_all(send, "band", 0, 0, tiled=False)
    c_loc = band_count * cond_piece
    loc = jnp.moveaxis(recv, 0, 1).reshape(KI, c_loc * NV, 2 * BW)

    c_base = ka_index * c_loc
    cond_grp = lax.dynamic_slice_in_dim(conduction_energy, c_base, c_loc, axis=1)
    cond_local = jnp.take(cond_grp, star_map, axis=0)
    val_local = jnp.take(valence_energy, star_map, axis=0)
    band_global = c_base + jnp.arange(c_loc)
    mask = (band_global[None, :] < cond_top[:, None]).astype(jnp.float32)[None, :, :, None]
    omega = freq_step * jnp.arange(NF).astype(jnp.float32)
    omega_sq = (omega * omega)[:, None, None, None]
    diff = val_local[:, None, :] - cond_local[:, :, None]
    weight = 4.0 / KF * diff[None] / (diff[None] * diff[None] + omega_sq) * mask
    weight_t = jnp.transpose(weight.reshape(NF, KF, c_loc * NV), (1, 0, 2))

    my_blocks = blocks[band_index, ga_index]
    perm_blocks = perm_lists.reshape(perm_lists.shape[0], NB, BW)
    my_perm = jnp.take(jnp.take(perm_blocks, op_of_k, axis=0), my_blocks, axis=1)
    subs = BW // GB
    local = my_perm.reshape(KF, 2 * subs, GB) - (
        my_blocks.repeat(subs) * BW + (jnp.arange(2 * subs) % subs) * GB
    )[None, :, None]
    perm_t = jnp.transpose(local, (0, 2, 1))
    partial_value = chi_block(star_map, loc, perm_t, weight_t)

    pieces = partial_value.reshape(NF, subs, GB, subs, GB).transpose(1, 3, 0, 2, 4)
    pieces = pieces.reshape(subs * subs, NF, GB, GB)
    got = lax.all_to_all(pieces, "ka", 0, 0, tiled=False)
    slab = got.sum(axis=0)
    return lax.ppermute(
        slab, ("ka", "band", "ga"), slab_perm(ka_count, band_count, ga_count)
    )


def solution(mesh):
    return jax.shard_map(
        on_device,
        mesh=mesh,
        in_specs=(P(None, ("ka", "band"), None, None), P(), P(), P(), P(), P(), P()),
        out_specs=P(None, ("band", "ga"), "ka"),
        check_vma=False,
    )
```

time: 352 us -> 132 us (0.38)
  local copies, waits for them, and re-layouts: 167 us -> 17.7 us
  other arithmetic: 84.4 us -> 7.75 us
  Pallas kernels: 0 us -> 34.8 us
  matrix products: 25.3 us -> 0 us
  between operations: 3.78 us -> 0.19 us
    convert_element_type x2 -> x0, other arithmetic: 53.4 us -> none  [the longest x1 27.2 us: on_device(): scaled_lo = (product - hi_back).astype(jnp.bfloat16)]
    gather x8 -> x7, local copies, waits for them, and re-layouts: 61.2 us -> 8.29 us  [the longest x2 3.85 us: on_device(): send = jnp.take(blocked, blocks[:, ga_index].reshape(-1), axis=3)]
    pallas_call x0 -> x1, Pallas kernels: none -> 34.8 us  [chi_block(): pl.pallas_call(chi_kernel, out_shape=jax.ShapeDtypeStruct((NF, BW, BW), j...]
    unnamed x10 -> x15, local copies, waits for them, and re-layouts: 27 us -> 0.66 us
    dot_general x2 -> x0, matrix products: 25.3 us -> none  [the longest x1 15.8 us: on_device(): jnp.einsum('krbi,kboi->krbo', shaped, onehot, preferred_element_type=jnp....]
    reshape x1 -> x0, local copies, waits for them, and re-layouts: 24.9 us -> none  [on_device(): rotated = rotated.astype(jnp.bfloat16).reshape(KF, c_loc, NV, 2, BW)]
    convert_element_type x2 -> x0, local copies, waits for them, and re-layouts: 23 us -> none  [the longest x1 22.9 us: on_device(): rotated = rotated.astype(jnp.bfloat16).reshape(KF, c_loc, NV, 2, BW)]
    dynamic_slice x2, local copies, waits for them, and re-layouts: 22.2 us -> 0.85 us  [on_device(): send = jnp.take(blocked, blocks[:, ga_index].reshape(-1), axis=3)]
  transfers between devices with their start and end apart: 2 -> 2, of which waited for: 2 -> 2; matrix products, arithmetic and copies ran while one was open for 4% -> 11% of each run, Pallas kernels for 0% -> 0%
where the time goes in v2:
time: 132 us; the launch traced here: 130 us
  blocking collectives  36.9 us (28%)
  Pallas kernels  34.8 us (26%)
  waiting for transfers between devices  21.1 us (16%)
  local copies, waits for them, and re-layouts  17.7 us (13%)
  starting transfers between devices  11.8 us (9%)
  other arithmetic  7.75 us (6%)
    all_to_all x1, blocking collectives, on_device(): got = lax.all_to_all(pieces, 'ka', 0, 0, tiled=False)  36.9 us
    pallas_call x1, Pallas kernels, chi_block(): pl.pallas_call(chi_kernel, out_shape=jax.ShapeDtypeStruct((NF, BW, BW), j...  34.8 us
    all_to_all x1, waiting for transfers between devices, on_device(): recv = lax.all_to_all(send, 'band', 0, 0, tiled=False)  12.5 us
    ppermute x1, waiting for transfers between devices, on_device(): lax.ppermute(slab, ('ka', 'band', 'ga'), slab_perm(ka_count, band_count,...  8.6 us
    all_to_all x1, starting transfers between devices, on_device(): recv = lax.all_to_all(send, 'band', 0, 0, tiled=False)  7.32 us
    transpose x1, other arithmetic, on_device(): perm_t = jnp.transpose(local, (0, 2, 1))  4.86 us
    ppermute x1, starting transfers between devices, on_device(): lax.ppermute(slab, ('ka', 'band', 'ga'), slab_perm(ka_count, band_count,...  4.48 us
    gather x2, local copies, waits for them, and re-layouts, on_device(): send = jnp.take(blocked, blocks[:, ga_index].reshape(-1), axis=3)  3.85 us
  transfers between devices with their start and end apart: 2, of which 2 were waited for; matrix products, arithmetic and copies ran while one was open for 11% of the time, Pallas kernels for 0%

profile of v2, /device:TPU:22, one launch (start us, length us, event | category | flops | bytes accessed | tf_op | source)
XLA Modules:
  0.0 130.2 jit_solution(3741257077237885533)
XLA Ops:
  0.0 0.8 constant_dynamic-slice_fusion.2
  0.9 0.1 copy.32
  1.1 2.0 %gather_fusion = bf16[16,8,2,8,512]{4,3,2,1,0:T(8,128)(2,1)} fusion(bf16[8,2,8,4,512]{4,2,3,1,0:T(8,128)(2,1)S(1)} %bitcast.29, s32[1024]{0:T(1024)S(1)} %pad_clamp_fusion.3), kind=kCustom, calls=%fused_computation | custom fusion | bytes 4194368 | tf_op jit(solution)/shard_map/jit(_take)/gather | solution.py:110
  3.1 1.8 %copy.33 = bf16[8,2,8,16,512]{4,2,3,1,0:T(8,128)(2,1)S(1)} copy(bf16[8,2,8,16,512]{4,2,1,0,3:T(8,128)(2,1)} %bitcast.32) | data formatting | bytes 4194304 | tf_op jit(solution)/shard_map/jit(_take)/gather | solution.py:110
  4.9 0.2 select_bitcast_fusion
  5.2 1.5 %copy.34 = bf16[8,8,2,8,2,512]{5,3,4,2,1,0:T(8,128)(2,1)} copy(bf16[8,8,2,8,2,512]{5,3,4,0,2,1:T(8,128)(2,1)S(1)} %select_bitcast_fusion) | data formatting | bytes 4194304 | tf_op jit(solution)/shard_map/transpose | solution.py:112
  6.8 7.3 %all-to-all-start = ((bf16[8,8,2,8,2,512]{5,3,4,2,1,0:T(8,128)(2,1)}), bf16[8,8,2,8,2,512]{5,3,4,2,1,0:T(8,128)(2,1)S(1)}, u32[]{:S(2)}, u32[]{:S(2)}) async-start(bf16[8,8,2,8,2,512]{5,3,4,2,1,0:T(8,128)(2,1)} %copy.34), calls=%async_computation | async-start | bytes 4194304 | tf_op jit(solution)/shard_map/all_to_all | solution.py:113
  14.1 0.7 compare_and_fusion.2
  14.9 0.6 gather_fusion.4
  15.5 0.6 gather_fusion.3
  16.3 0.7 bitcast_multiply_fusion
  17.0 0.1 broadcast_in_dim.73
  17.5 0.7 copy.41.w_ref
  18.2 0.3 reshape.240
  18.5 0.9 gather_fusion.1
  19.4 0.2 broadcast_select_fusion
  19.6 0.2 copy.36
  19.7 0.7 fusion.6
  20.4 0.6 gather_fusion.2
  21.0 0.2 copy.37
  21.2 0.2 gather.28
  21.4 2.6 %copy.38 = s32[64,8,128]{1,2,0:T(8,128)} copy(s32[64,8,128]{2,1,0:T(8,128)S(1)} %gather.28) | data formatting | bytes 524288 | tf_op jit(solution)/shard_map/jit(_take)/gather | solution.py:131
  24.0 4.9 %subtract_bitcast_fusion.perm_ref = s32[64,128,8]{2,1,0:T(8,128)} fusion(s32[64,8,128]{1,2,0:T(8,128)} %copy.38, s32[8]{0:T(128)S(1)} %fusion.4, pred[8]{0:T(512)(128)(4,1)S(1)} %broadcast_in_dim.73), kind=kLoop, calls=%fused_computation.5 | loop fusion | flops 131072 | bytes 524328 | tf_op jit(solution)/shard_map/transpose | solution.py:136
  28.9 12.5 %all-to-all-done = bf16[8,8,2,8,2,512]{5,3,4,2,1,0:T(8,128)(2,1)S(1)} async-done(((bf16[8,8,2,8,2,512]{5,3,4,2,1,0:T(8,128)(2,1)}), bf16[8,8,2,8,2,512]{5,3,4,2,1,0:T(8,128)(2,1)S(1)}, u32[]{:S(2)}, u32[]{:S(2)}) %all-to-all-start) | async-done | bytes 2097184 | tf_op jit(solution)/shard_map/all_to_all | solution.py:113
  41.5 1.6 %copy.35 = bf16[8,8,2,8,2,512]{5,3,4,2,1,0:T(8,128)(2,1)} copy(bf16[8,8,2,8,2,512]{5,3,4,2,0,1:T(8,128)(2,1)S(1)} %bitcast.31) | data formatting | bytes 4194304 | tf_op jit(solution)/shard_map/transpose | solution.py:115
  43.1 34.8 %shard_map.82 = f32[1,512,512]{2,1,0:T(8,128)} custom-call(s32[64]{0:T(128)} %star_ref.1, bf16[8,128,1024]{2,1,0:T(8,128)(2,1)} %bitcast.33, s32[64,128,8]{2,1,0:T(8,128)} %subtract_bitcast_fusion.perm_ref, f32[64,1,128]{2,1,0:T(1,128)} %copy.41.w_ref), custom_call_target="tpu_custom_call" | custom-call | tf_op jit(solution)/shard_map/pallas_call | solution.py:64
  77.9 1.6 %reshape.241 = f32[1,4,128,4,128]{4,3,2,1,0:T(4,128)S(1)} reshape(f32[1,512,512]{2,1,0:T(8,128)} %shard_map.82) | data formatting | bytes 2097152 | tf_op jit(solution)/shard_map/reshape | solution.py:139
  79.5 0.1 copy.42
  79.6 36.9 %all_to_all.10 = f32[16,1,128,128]{3,2,1,0:T(8,128)S(1)} all-to-all(f32[16,1,128,128]{3,2,1,0:T(8,128)S(1)} %bitcast.34), channel_id=1, replica_groups=mesh['ka'=16,'band'=8,'ga'=2] {'ka'}, dimensions={0} | all-to-all | bytes 2097152 | tf_op jit(solution)/shard_map/all_to_all | solution.py:141
  116.5 4.5 %collective-permute-start = (f32[1,128,128]{2,1,0:T(8,128)S(1)}, f32[1,128,128]{2,1,0:T(8,128)S(1)}, u32[]{:S(2)}, u32[]{:S(2)}) collective-permute-start(f32[1,128,128]{2,1,0:T(8,128)S(1)} %bitcast.36), channel_id=1, source_target_pairs={{0,0},{1,68},{2,136},{3,204},{4,64},{5,4},{6,128},{7,8},{8,192},{9... | collective-permute-start | bytes 196616 | tf_op jit(solution)/shard_map/ppermute | solution.py:143
  121.0 8.6 %collective-permute-done = f32[1,128,128]{2,1,0:T(8,128)S(1)} collective-permute-done((f32[1,128,128]{2,1,0:T(8,128)S(1)}, f32[1,128,128]{2,1,0:T(8,128)S(1)}, u32[]{:S(2)}, u32[]{:S(2)}) %collective-permute-start) | collective-permute-done | bytes 65568 | tf_op jit(solution)/shard_map/ppermute | solution.py:143
  129.6 0.6 copy.45
  (37 shorter events, 1.0 us)
Async XLA Ops:
  0.0 1.1 copy-start
  6.7 7.4 %copy-start.3 = (s32[64]{0:T(128)S(1)}, s32[64]{0:T(128)}, u32[]{:S(2)}) copy-start(s32[64]{0:T(128)} %star_ref.1) | copy-start | bytes 772
  6.7 7.4 %copy-start.5 = (s32[64]{0:T(128)S(1)}, s32[64]{0:T(128)}, u32[]{:S(2)}) copy-start(s32[64]{0:T(128)} %param.12) | copy-start | bytes 772
  6.7 8.1 %copy-start.4 = (f32[8,256]{1,0:T(8,128)S(1)}, f32[8,256]{1,0:T(8,128)}, u32[]{:S(2)}) copy-start(f32[8,256]{1,0:T(8,128)} %param.10) | copy-start | bytes 24580
  6.7 8.8 %copy-start.1 = (f32[8,8]{1,0:T(8,128)S(1)}, f32[8,8]{1,0:T(8,128)}, u32[]{:S(2)}) copy-start(f32[8,8]{1,0:T(8,128)} %param.9) | copy-start | bytes 772
  6.7 10.7 %copy-start.6 = (s32[64]{0:T(128)S(1)}, s32[64]{0:T(128)}, u32[]{:S(2)}) copy-start(s32[64]{0:T(128)} %param.14) | copy-start | bytes 772
  6.8 11.5 %copy-start.2 = (s32[48,2048]{1,0:T(8,128)S(1)}, s32[48,2048]{1,0:T(8,128)}, u32[]{:S(2)}) copy-start(s32[48,2048]{1,0:T(8,128)} %param.13) | copy-start | bytes 1179652
  6.8 34.7 %all-to-all-start = ((bf16[8,8,2,8,2,512]{5,3,4,2,1,0:T(8,128)(2,1)}), bf16[8,8,2,8,2,512]{5,3,4,2,1,0:T(8,128)(2,1)S(1)}, u32[]{:S(2)}, u32[]{:S(2)}) async-start(bf16[8,8,2,8,2,512]{5,3,4,2,1,0:T(8,128)(2,1)} %copy.34), calls=%async_computation | async-start | bytes 4194304 | tf_op jit(solution)/shard_map/all_to_all | solution.py:113
  116.5 13.1 %collective-permute-start = (f32[1,128,128]{2,1,0:T(8,128)S(1)}, f32[1,128,128]{2,1,0:T(8,128)S(1)}, u32[]{:S(2)}, u32[]{:S(2)}) collective-permute-start(f32[1,128,128]{2,1,0:T(8,128)S(1)} %bitcast.36), channel_id=1, source_target_pairs={{0,0},{1,68},{2,136},{3,204},{4,64},{5,4},{6,128},{7,8},{8,192},{9... | collective-permute-start | bytes 196616 | tf_op jit(solution)/shard_map/ppermute | solution.py:143

commit v3 on v2

--- a/solution.py
+++ b/solution.py
@@ -26,7 +26,7 @@
 freq_step = 2.0
 
 
-def chi_kernel(star_ref, loc_ref, perm_ref, w_ref, out_ref):
+def chi_kernel(star_ref, loc_ref, perm_ref, perm_t_ref, w_ref, out_ref):
     step = pl.program_id(0)
 
     @pl.when(step == 0)
@@ -34,32 +34,48 @@
         out_ref[...] = jnp.zeros_like(out_ref)
 
     lane = lax.broadcasted_iota(jnp.int32, (GB, GB), 1)
+    sub = lax.broadcasted_iota(jnp.int32, (GB, GB), 0)
     nt = (((1,), (1,)), ((), ()))
+    subs = BW // GB
+    lhs_parts = []
+    rhs_parts = [[] for _ in range(NF)]
     for t in range(KB):
         x = loc_ref[star_ref[step * KB + t]]
-        slots = perm_ref[t]
-        parts = []
-        for q in range(2 * BW // GB):
-            onehot = jnp.where(slots[:, q : q + 1] == lane, 1.0, 0.0).astype(jnp.bfloat16)
-            parts.append(
+        slots_col = perm_t_ref[t]
+        row_parts = []
+        for q in range(subs):
+            onehot = jnp.where(slots_col[:, q : q + 1] == lane, 1.0, 0.0).astype(jnp.bfloat16)
+            row_parts.append(
                 lax.dot_general(
                     onehot, x[:, q * GB : (q + 1) * GB], nt,
                     preferred_element_type=jnp.float32,
                 )
             )
-        rot_t = jnp.concatenate(parts, axis=0)
-        row_t = rot_t[:BW].astype(jnp.bfloat16)
-        col_t = rot_t[BW:]
-        lhs = jnp.concatenate([row_t, row_t], axis=1)
+        row_t = jnp.concatenate(row_parts, axis=0).astype(jnp.bfloat16)
+        slots_row = perm_ref[t]
+        col_parts = []
+        for q in range(subs, 2 * subs):
+            onehot_t = jnp.where(slots_row[q : q + 1, :] == sub, 1.0, 0.0).astype(jnp.bfloat16)
+            col_parts.append(
+                jnp.dot(
+                    x[:, q * GB : (q + 1) * GB], onehot_t,
+                    preferred_element_type=jnp.float32,
+                )
+            )
+        col = jnp.concatenate(col_parts, axis=1)
+        lhs_parts += [row_t, row_t]
         for f in range(NF):
-            product = col_t * w_ref[t, f : f + 1, :]
+            product = col * w_ref[t][:, f : f + 1]
             scaled_hi = product.astype(jnp.bfloat16)
             scaled_lo = (product - scaled_hi.astype(jnp.float32)).astype(jnp.bfloat16)
-            rhs = jnp.concatenate([scaled_hi, scaled_lo], axis=1)
-            out_ref[f] += lax.dot_general(lhs, rhs, nt, preferred_element_type=jnp.float32)
+            rhs_parts[f] += [scaled_hi, scaled_lo]
+    lhs = jnp.concatenate(lhs_parts, axis=1)
+    for f in range(NF):
+        rhs = jnp.concatenate(rhs_parts[f], axis=0)
+        out_ref[f] += jnp.dot(lhs, rhs, preferred_element_type=jnp.float32)
 
 
-def chi_block(star_map, loc, perm_t, weight_t):
+def chi_block(star_map, loc, perm, perm_t, weight_c):
     rows = loc.shape[1]
     return pl.pallas_call(
         chi_kernel,
@@ -69,13 +85,14 @@
             grid=(KF // KB,),
             in_specs=[
                 pl.BlockSpec((KI, rows, 2 * BW), lambda st, sm: (0, 0, 0)),
+                pl.BlockSpec((KB, 2 * BW // GB, GB), lambda st, sm: (st, 0, 0)),
                 pl.BlockSpec((KB, GB, 2 * BW // GB), lambda st, sm: (st, 0, 0)),
-                pl.BlockSpec((KB, NF, rows), lambda st, sm: (st, 0, 0)),
+                pl.BlockSpec((KB, rows, NF), lambda st, sm: (st, 0, 0)),
             ],
             out_specs=pl.BlockSpec((NF, BW, BW), lambda st, sm: (0, 0, 0)),
         ),
         compiler_params=pltpu.CompilerParams(dimension_semantics=("arbitrary",)),
-    )(star_map, loc, perm_t, weight_t)
+    )(star_map, loc, perm, perm_t, weight_c)
 
 
 def slab_perm(ka_count, band_count, ga_count):
@@ -124,7 +141,7 @@
     omega_sq = (omega * omega)[:, None, None, None]
     diff = val_local[:, None, :] - cond_local[:, :, None]
     weight = 4.0 / KF * diff[None] / (diff[None] * diff[None] + omega_sq) * mask
-    weight_t = jnp.transpose(weight.reshape(NF, KF, c_loc * NV), (1, 0, 2))
+    weight_c = jnp.transpose(weight.reshape(NF, KF, c_loc * NV), (1, 2, 0))
 
     my_blocks = blocks[band_index, ga_index]
     perm_blocks = perm_lists.reshape(perm_lists.shape[0], NB, BW)
@@ -134,7 +151,7 @@
         my_blocks.repeat(subs) * BW + (jnp.arange(2 * subs) % subs) * GB
     )[None, :, None]
     perm_t = jnp.transpose(local, (0, 2, 1))
-    partial_value = chi_block(star_map, loc, perm_t, weight_t)
+    partial_value = chi_block(star_map, loc, local, perm_t, weight_c)
 
     pieces = partial_value.reshape(NF, subs, GB, subs, GB).transpose(1, 3, 0, 2, 4)
     pieces = pieces.reshape(subs * subs, NF, GB, GB)

time: 132 us -> 124 us (0.939)
  waiting for transfers between devices: 21.1 us -> 9.92 us
  Pallas kernels: 34.8 us -> 25.9 us
  local copies, waits for them, and re-layouts: 17.7 us -> 25.2 us
  other arithmetic: 7.75 us -> 14.9 us
  starting transfers between devices: 11.8 us -> 10.1 us
    all_to_all x1, waiting for transfers between devices: 12.5 us -> 0.01 us  [on_device(): recv = lax.all_to_all(send, 'band', 0, 0, tiled=False)]
    pallas_call x1, Pallas kernels: 34.8 us -> 25.9 us  [chi_block(): pl.pallas_call(chi_kernel, out_shape=jax.ShapeDtypeStruct((NF, BW, BW), j...]
    sub x0 -> x1, other arithmetic: none -> 4.87 us  [on_device(): my_perm.reshape(KF, 2 * subs, GB)]
    mul x1, local copies, waits for them, and re-layouts: 0.7 us -> 4.52 us  [on_device(): weight = 4.0 / KF * diff[None] / (diff[None] * diff[None] + omega_sq) * mask]
    sub x0 -> x1, local copies, waits for them, and re-layouts: none -> 3.5 us  [on_device(): my_perm.reshape(KF, 2 * subs, GB)]
    ppermute x1, starting transfers between devices: 4.48 us -> 2.87 us  [on_device(): lax.ppermute(slab, ('ka', 'band', 'ga'), slab_perm(ka_count, band_count,...]
  transfers between devices with their start and end apart: 2 -> 2, of which waited for: 2 -> 1; matrix products, arithmetic and copies ran while one was open for 11% -> 24% of each run, Pallas kernels for 0% -> 0%
where the time goes in v3:
time: 124 us; the launch traced here: 123 us
  blocking collectives  37 us (30%)
  Pallas kernels  25.9 us (21%)
  local copies, waits for them, and re-layouts  25.2 us (20%)
  other arithmetic  14.9 us (12%)
  starting transfers between devices  10.1 us (8%)
  waiting for transfers between devices  9.92 us (8%)
    all_to_all x1, blocking collectives, on_device(): got = lax.all_to_all(pieces, 'ka', 0, 0, tiled=False)  37 us
    pallas_call x1, Pallas kernels, chi_block(): pl.pallas_call(chi_kernel, out_shape=jax.ShapeDtypeStruct((NF, BW, BW), j...  25.9 us
    ppermute x1, waiting for transfers between devices, on_device(): lax.ppermute(slab, ('ka', 'band', 'ga'), slab_perm(ka_count, band_count,...  9.91 us
    all_to_all x1, starting transfers between devices, on_device(): recv = lax.all_to_all(send, 'band', 0, 0, tiled=False)  7.18 us
    transpose x1, other arithmetic, on_device(): perm_t = jnp.transpose(local, (0, 2, 1))  4.89 us
    sub x1, other arithmetic, on_device(): my_perm.reshape(KF, 2 * subs, GB)  4.87 us
    mul x1, local copies, waits for them, and re-layouts, on_device(): weight = 4.0 / KF * diff[None] / (diff[None] * diff[None] + omega_sq) * mask  4.52 us
    gather x2, local copies, waits for them, and re-layouts, on_device(): send = jnp.take(blocked, blocks[:, ga_index].reshape(-1), axis=3)  3.84 us
  transfers between devices with their start and end apart: 2, of which 1 were waited for; matrix products, arithmetic and copies ran while one was open for 24% of the time, Pallas kernels for 0%

profile of v3, /device:TPU:22, one launch (start us, length us, event | category | flops | bytes accessed | tf_op | source)
XLA Modules:
  0.0 123.1 jit_solution(7263190120335278026)
XLA Ops:
  0.0 0.8 constant_dynamic-slice_fusion.2
  0.9 0.2 copy-done
  1.1 2.0 %gather_fusion = bf16[16,8,2,8,512]{4,3,2,1,0:T(8,128)(2,1)} fusion(bf16[8,2,8,4,512]{4,2,3,1,0:T(8,128)(2,1)S(1)} %bitcast.29, s32[1024]{0:T(1024)S(1)} %pad_clamp_fusion.3), kind=kCustom, calls=%fused_computation | custom fusion | bytes 4194368 | tf_op jit(solution)/shard_map/jit(_take)/gather | solution.py:127
  3.1 1.8 %copy.36 = bf16[8,2,8,16,512]{4,2,3,1,0:T(8,128)(2,1)S(1)} copy(bf16[8,2,8,16,512]{4,2,1,0,3:T(8,128)(2,1)} %bitcast.32) | data formatting | bytes 4194304 | tf_op jit(solution)/shard_map/jit(_take)/gather | solution.py:127
  5.1 0.3 select_bitcast_fusion
  5.4 1.6 %copy.37 = bf16[8,8,2,8,2,512]{5,3,4,2,1,0:T(8,128)(2,1)} copy(bf16[8,8,2,8,2,512]{5,3,4,0,2,1:T(8,128)(2,1)S(1)} %select_bitcast_fusion) | data formatting | bytes 4194304 | tf_op jit(solution)/shard_map/transpose | solution.py:129
  7.0 7.2 %all-to-all-start = ((bf16[8,8,2,8,2,512]{5,3,4,2,1,0:T(8,128)(2,1)}), bf16[8,8,2,8,2,512]{5,3,4,2,1,0:T(8,128)(2,1)S(1)}, u32[]{:S(2)}, u32[]{:S(2)}) async-start(bf16[8,8,2,8,2,512]{5,3,4,2,1,0:T(8,128)(2,1)} %copy.37), calls=%async_computation | async-start | bytes 4194304 | tf_op jit(solution)/shard_map/all_to_all | solution.py:130
  14.2 0.5 compare_select_fusion.1
  14.7 0.5 compare_and_fusion
  15.2 0.7 fusion.6
  15.9 1.2 %bitcast_multiply_fusion = s32[2]{0:T(128)} fusion(s32[8,2,2]{2,1,0:T(2,128)} %constant.114.clone, s32[]{:T(128)S(6)} %select_n.99, s32[]{:T(128)S(6)} %select_n.95), kind=kLoop, calls=%fused_computation.38 | loop fusion | flops 2 | bytes 24 | tf_op jit(solution)/shard_map/mul | solution.py:151
  17.1 0.7 compare_and_fusion.2
  17.9 0.3 reshape.240
  18.1 0.9 gather_fusion.1
  19.0 0.8 broadcast_select_fusion
  20.0 0.6 gather_fusion.2
  20.6 0.2 copy.40
  20.8 0.2 gather.28
  21.0 2.6 %copy.41 = s32[64,8,128]{1,2,0:T(8,128)} copy(s32[64,8,128]{2,1,0:T(8,128)S(1)} %gather.28) | data formatting | bytes 524288 | tf_op jit(solution)/shard_map/jit(_take)/gather | solution.py:148
  24.0 4.9 %select_subtract_fusion = s32[64,8,128]{1,2,0:T(8,128)} fusion(s32[64,8,128]{1,2,0:T(8,128)} %copy.41, s32[8]{0:T(128)S(1)} %fusion.4, pred[8]{0:T(512)(128)(4,1)S(1)} %broadcast_in_dim.73), kind=kLoop, calls=%fused_computation.5 | loop fusion | flops 131072 | bytes 524328 | tf_op jit(solution)/shard_map/sub | solution.py:150
  28.8 3.5 %copy.44.perm_ref = s32[64,8,128]{2,1,0:T(8,128)} copy(s32[64,8,128]{1,2,0:T(8,128)} %select_subtract_fusion) | data formatting | bytes 524288 | tf_op jit(solution)/shard_map/sub | solution.py:150
  32.4 0.6 gather_fusion.4
  33.2 0.6 gather_fusion.3
  34.0 4.5 %copy.45.w_ref = f32[64,128,1]{2,1,0:T(8,128)} copy(f32[64,128,1]{0,1,2:T(8,128)S(1)} %fusion.2) | data formatting | bytes 65536 | tf_op jit(solution)/shard_map/mul | solution.py:143
  38.6 4.9 %fusion.8.perm_t_ref = s32[64,128,8]{2,1,0:T(8,128)} fusion(s32[8]{0:T(128)S(1)} %fusion.4, s32[64,8,128]{1,2,0:T(8,128)} %copy.41, pred[8]{0:T(512)(128)(4,1)S(1)} %broadcast_in_dim.73), kind=kLoop, calls=%fused_computation.41 | loop fusion | flops 131072 | bytes 524328 | tf_op jit(solution)/shard_map/transpose | solution.py:153
  43.5 1.6 %copy.38 = bf16[8,8,2,8,2,512]{5,3,4,2,1,0:T(8,128)(2,1)} copy(bf16[8,8,2,8,2,512]{5,3,4,2,0,1:T(8,128)(2,1)S(1)} %bitcast.31) | data formatting | bytes 4194304 | tf_op jit(solution)/shard_map/transpose | solution.py:132
  45.0 25.9 %shard_map.82 = f32[1,512,512]{2,1,0:T(8,128)} custom-call(s32[64]{0:T(128)} %star_ref.1, bf16[8,128,1024]{2,1,0:T(8,128)(2,1)} %bitcast.33, s32[64,8,128]{2,1,0:T(8,128)} %copy.44.perm_ref, s32[64,128,8]{2,1,0:T(8,128)} %fusion.8.perm_t_ref, f32[64,128,1]{2,1,0:T(8,128)} %copy.45.w_ref), custom_call_target="tpu_custom_call" | custom-call | tf_op jit(solution)/shard_map/pallas_call | solution.py:80
  70.9 1.6 %reshape.241 = f32[1,4,128,4,128]{4,3,2,1,0:T(4,128)S(1)} reshape(f32[1,512,512]{2,1,0:T(8,128)} %shard_map.82) | data formatting | bytes 2097152 | tf_op jit(solution)/shard_map/reshape | solution.py:156
  72.6 37.0 %all_to_all.10 = f32[16,1,128,128]{3,2,1,0:T(8,128)S(1)} all-to-all(f32[16,1,128,128]{3,2,1,0:T(8,128)S(1)} %bitcast.34), channel_id=1, replica_groups=mesh['ka'=16,'band'=8,'ga'=2] {'ka'}, dimensions={0} | all-to-all | bytes 2097152 | tf_op jit(solution)/shard_map/all_to_all | solution.py:158
  109.7 2.9 %collective-permute-start = (f32[1,128,128]{2,1,0:T(8,128)S(1)}, f32[1,128,128]{2,1,0:T(8,128)S(1)}, u32[]{:S(2)}, u32[]{:S(2)}) collective-permute-start(f32[1,128,128]{2,1,0:T(8,128)S(1)} %bitcast.36), channel_id=1, source_target_pairs={{0,0},{1,68},{2,136},{3,204},{4,64},{5,4},{6,128},{7,8},{8,192},{9... | collective-permute-start | bytes 196616 | tf_op jit(solution)/shard_map/ppermute | solution.py:160
  112.6 9.9 %collective-permute-done = f32[1,128,128]{2,1,0:T(8,128)S(1)} collective-permute-done((f32[1,128,128]{2,1,0:T(8,128)S(1)}, f32[1,128,128]{2,1,0:T(8,128)S(1)}, u32[]{:S(2)}, u32[]{:S(2)}) %collective-permute-start) | collective-permute-done | bytes 65568 | tf_op jit(solution)/shard_map/ppermute | solution.py:160
  122.5 0.6 copy.49
  (43 shorter events, 1.5 us)
Async XLA Ops:
  0.0 1.1 copy-start
  5.4 8.8 %copy-start.3 = (s32[64]{0:T(128)S(1)}, s32[64]{0:T(128)}, u32[]{:S(2)}) copy-start(s32[64]{0:T(128)} %star_ref.1) | copy-start | bytes 772
  5.4 8.8 %copy-start.6 = (s32[64]{0:T(128)S(1)}, s32[64]{0:T(128)}, u32[]{:S(2)}) copy-start(s32[64]{0:T(128)} %param.12) | copy-start | bytes 772
  5.4 12.5 %copy-start.2 = (s32[48,2048]{1,0:T(8,128)S(1)}, s32[48,2048]{1,0:T(8,128)}, u32[]{:S(2)}) copy-start(s32[48,2048]{1,0:T(8,128)} %param.13) | copy-start | bytes 1179652
  7.0 36.5 %all-to-all-start = ((bf16[8,8,2,8,2,512]{5,3,4,2,1,0:T(8,128)(2,1)}), bf16[8,8,2,8,2,512]{5,3,4,2,1,0:T(8,128)(2,1)S(1)}, u32[]{:S(2)}, u32[]{:S(2)}) async-start(bf16[8,8,2,8,2,512]{5,3,4,2,1,0:T(8,128)(2,1)} %copy.37), calls=%async_computation | async-start | bytes 4194304 | tf_op jit(solution)/shard_map/all_to_all | solution.py:130
  19.0 4.6 %copy-start.8 = (s32[2]{0:T(128)S(1)}, s32[2]{0:T(128)}, u32[]{:S(2)}) copy-start(s32[2]{0:T(128)} %bitcast_multiply_fusion) | copy-start | bytes 28
  28.8 3.5 %copy-start.5 = (s32[64]{0:T(128)S(1)}, s32[64]{0:T(128)}, u32[]{:S(2)}) copy-start(s32[64]{0:T(128)} %get-tuple-element.7) | copy-start | bytes 772
  28.8 3.5 %copy-start.4 = (f32[8,256]{1,0:T(8,128)S(1)}, f32[8,256]{1,0:T(8,128)}, u32[]{:S(2)}) copy-start(f32[8,256]{1,0:T(8,128)} %param.10) | copy-start | bytes 24580
  28.8 4.3 %copy-start.1 = (f32[8,8]{1,0:T(8,128)S(1)}, f32[8,8]{1,0:T(8,128)}, u32[]{:S(2)}) copy-start(f32[8,8]{1,0:T(8,128)} %param.9) | copy-start | bytes 772
  28.8 5.1 %copy-start.7 = (s32[64]{0:T(128)S(1)}, s32[64]{0:T(128)}, u32[]{:S(2)}) copy-start(s32[64]{0:T(128)} %param.14) | copy-start | bytes 772
  109.7 12.8 %collective-permute-start = (f32[1,128,128]{2,1,0:T(8,128)S(1)}, f32[1,128,128]{2,1,0:T(8,128)S(1)}, u32[]{:S(2)}, u32[]{:S(2)}) collective-permute-start(f32[1,128,128]{2,1,0:T(8,128)S(1)} %bitcast.36), channel_id=1, source_target_pairs={{0,0},{1,68},{2,136},{3,204},{4,64},{5,4},{6,128},{7,8},{8,192},{9... | collective-permute-start | bytes 196616 | tf_op jit(solution)/shard_map/ppermute | solution.py:160

commit v4 on v3

--- a/solution.py
+++ b/solution.py
@@ -1,3 +1,5 @@
+import functools
+
 import jax
 import jax.numpy as jnp
 from jax import lax
@@ -26,14 +28,15 @@
 freq_step = 2.0
 
 
-def chi_kernel(star_ref, loc_ref, perm_ref, perm_t_ref, w_ref, out_ref):
+def chi_kernel(half, star_ref, loc_ref, perm_ref, perm_t_ref, w_ref, out_ref):
     step = pl.program_id(0)
+    rows_half = GB // 2
 
     @pl.when(step == 0)
     def _():
         out_ref[...] = jnp.zeros_like(out_ref)
 
-    lane = lax.broadcasted_iota(jnp.int32, (GB, GB), 1)
+    lane = lax.broadcasted_iota(jnp.int32, (rows_half, GB), 1)
     sub = lax.broadcasted_iota(jnp.int32, (GB, GB), 0)
     nt = (((1,), (1,)), ((), ()))
     subs = BW // GB
@@ -41,7 +44,7 @@
     rhs_parts = [[] for _ in range(NF)]
     for t in range(KB):
         x = loc_ref[star_ref[step * KB + t]]
-        slots_col = perm_t_ref[t]
+        slots_col = perm_t_ref[t, half * rows_half : (half + 1) * rows_half, :]
         row_parts = []
         for q in range(subs):
             onehot = jnp.where(slots_col[:, q : q + 1] == lane, 1.0, 0.0).astype(jnp.bfloat16)
@@ -75,11 +78,11 @@
         out_ref[f] += jnp.dot(lhs, rhs, preferred_element_type=jnp.float32)
 
 
-def chi_block(star_map, loc, perm, perm_t, weight_c):
+def chi_block(half, star_map, loc, perm, perm_t, weight_c):
     rows = loc.shape[1]
     return pl.pallas_call(
-        chi_kernel,
-        out_shape=jax.ShapeDtypeStruct((NF, BW, BW), jnp.float32),
+        functools.partial(chi_kernel, half),
+        out_shape=jax.ShapeDtypeStruct((NF, BW // 2, BW), jnp.float32),
         grid_spec=pltpu.PrefetchScalarGridSpec(
             num_scalar_prefetch=1,
             grid=(KF // KB,),
@@ -89,7 +92,7 @@
                 pl.BlockSpec((KB, GB, 2 * BW // GB), lambda st, sm: (st, 0, 0)),
                 pl.BlockSpec((KB, rows, NF), lambda st, sm: (st, 0, 0)),
             ],
-            out_specs=pl.BlockSpec((NF, BW, BW), lambda st, sm: (0, 0, 0)),
+            out_specs=pl.BlockSpec((NF, BW // 2, BW), lambda st, sm: (0, 0, 0)),
         ),
         compiler_params=pltpu.CompilerParams(dimension_semantics=("arbitrary",)),
     )(star_map, loc, perm, perm_t, weight_c)
@@ -151,12 +154,14 @@
         my_blocks.repeat(subs) * BW + (jnp.arange(2 * subs) % subs) * GB
     )[None, :, None]
     perm_t = jnp.transpose(local, (0, 2, 1))
-    partial_value = chi_block(star_map, loc, local, perm_t, weight_c)
-
-    pieces = partial_value.reshape(NF, subs, GB, subs, GB).transpose(1, 3, 0, 2, 4)
-    pieces = pieces.reshape(subs * subs, NF, GB, GB)
-    got = lax.all_to_all(pieces, "ka", 0, 0, tiled=False)
-    slab = got.sum(axis=0)
+    halves = []
+    for half in range(2):
+        part = chi_block(half, star_map, loc, local, perm_t, weight_c)
+        pieces = part.reshape(NF, subs, GB // 2, subs, GB).transpose(1, 3, 0, 2, 4)
+        pieces = pieces.reshape(subs * subs, NF, GB // 2, GB)
+        got = lax.all_to_all(pieces, "ka", 0, 0, tiled=False)
+        halves.append(got.sum(axis=0))
+    slab = jnp.concatenate(halves, axis=1)
     return lax.ppermute(
         slab, ("ka", "band", "ga"), slab_perm(ka_count, band_count, ga_count)
     )

time: 124 us -> 137 us (1.10)
  blocking collectives: 37 us -> 0 us
  starting transfers between devices: 10.1 us -> 27.4 us
  waiting for transfers between devices: 9.92 us -> 26.1 us
  Pallas kernels: 25.9 us -> 39.5 us
  local copies, waits for them, and re-layouts: 25.2 us -> 28.3 us
    all_to_all x1 -> x0, blocking collectives: 37 us -> none  [on_device(): got = lax.all_to_all(pieces, 'ka', 0, 0, tiled=False)]
    all_to_all x0 -> x2, starting transfers between devices: none -> 17.4 us  [on_device(): got = lax.all_to_all(pieces, 'ka', 0, 0, tiled=False)]
    all_to_all x0 -> x2, waiting for transfers between devices: none -> 16.1 us  [on_device(): got = lax.all_to_all(pieces, 'ka', 0, 0, tiled=False)]
    pallas_call x1 -> x2, Pallas kernels: 25.9 us -> 39.5 us  [chi_block(): pl.pallas_call(functools.partial(chi_kernel, half), out_shape=jax.ShapeDt...]
    reshape x2 -> x4, local copies, waits for them, and re-layouts: 1.68 us -> 4.15 us  [on_device(): pieces = part.reshape(NF, subs, GB // 2, subs, GB).transpose(1, 3, 0, 2, 4)]
  transfers between devices with their start and end apart: 2 -> 4, of which waited for: 1 -> 2; matrix products, arithmetic and copies ran while one was open for 24% -> 23% of each run, Pallas kernels for 0% -> 15%
where the time goes in v4:
time: 137 us; the launch traced here: 136 us
  Pallas kernels  39.5 us (29%)
  local copies, waits for them, and re-layouts  28.3 us (21%)
  starting transfers between devices  27.4 us (20%)
  waiting for transfers between devices  26.1 us (19%)
  other arithmetic  14.3 us (10%)
    pallas_call x2, Pallas kernels, chi_block(): pl.pallas_call(functools.partial(chi_kernel, half), out_shape=jax.ShapeDt...  39.5 us
    all_to_all x2, starting transfers between devices, on_device(): got = lax.all_to_all(pieces, 'ka', 0, 0, tiled=False)  17.4 us
    all_to_all x2, waiting for transfers between devices, on_device(): got = lax.all_to_all(pieces, 'ka', 0, 0, tiled=False)  16.1 us
    ppermute x1, waiting for transfers between devices, on_device(): lax.ppermute(slab, ('ka', 'band', 'ga'), slab_perm(ka_count, band_count,...  9.98 us
    all_to_all x1, starting transfers between devices, on_device(): recv = lax.all_to_all(send, 'band', 0, 0, tiled=False)  7.18 us
    transpose x1, other arithmetic, on_device(): perm_t = jnp.transpose(local, (0, 2, 1))  4.89 us
    sub x1, other arithmetic, on_device(): my_perm.reshape(KF, 2 * subs, GB)  4.87 us
    mul x1, local copies, waits for them, and re-layouts, on_device(): weight = 4.0 / KF * diff[None] / (diff[None] * diff[None] + omega_sq) * mask  4.58 us
  transfers between devices with their start and end apart: 4, of which 2 were waited for; matrix products, arithmetic and copies ran while one was open for 23% of the time, Pallas kernels for 15%

profile of v4, /device:TPU:22, one launch (start us, length us, event | category | flops | bytes accessed | tf_op | source)
XLA Modules:
  0.0 135.8 jit_solution(12665742653583363222)
XLA Ops:
  0.0 0.8 constant_dynamic-slice_fusion.2
  1.1 2.0 %gather_fusion = bf16[16,8,2,8,512]{4,3,2,1,0:T(8,128)(2,1)} fusion(bf16[8,2,8,4,512]{4,2,3,1,0:T(8,128)(2,1)S(1)} %bitcast.35, s32[1024]{0:T(1024)S(1)} %pad_clamp_fusion.3), kind=kCustom, calls=%fused_computation | custom fusion | bytes 4194368 | tf_op jit(solution)/shard_map/jit(_take)/gather | solution.py:130
  3.1 1.8 %copy.61 = bf16[8,2,8,16,512]{4,2,3,1,0:T(8,128)(2,1)S(1)} copy(bf16[8,2,8,16,512]{4,2,1,0,3:T(8,128)(2,1)} %bitcast.40) | data formatting | bytes 4194304 | tf_op jit(solution)/shard_map/jit(_take)/gather | solution.py:130
  5.4 1.6 %copy.62 = bf16[8,8,2,8,2,512]{5,3,4,2,1,0:T(8,128)(2,1)} copy(bf16[8,8,2,8,2,512]{5,3,4,0,2,1:T(8,128)(2,1)S(1)} %select_bitcast_fusion) | data formatting | bytes 4194304 | tf_op jit(solution)/shard_map/transpose | solution.py:132
  7.0 7.2 %all-to-all-start = ((bf16[8,8,2,8,2,512]{5,3,4,2,1,0:T(8,128)(2,1)}), bf16[8,8,2,8,2,512]{5,3,4,2,1,0:T(8,128)(2,1)S(1)}, u32[]{:S(2)}, u32[]{:S(2)}) async-start(bf16[8,8,2,8,2,512]{5,3,4,2,1,0:T(8,128)(2,1)} %copy.62), calls=%async_computation | async-start | bytes 4194304 | tf_op jit(solution)/shard_map/all_to_all | solution.py:133
  14.1 0.5 compare_select_fusion.1
  14.7 0.7 fusion.6
  15.4 1.2 bitcast_multiply_fusion
  16.6 1.3 compare_and_fusion.2
  18.1 0.9 gather_fusion.1
  19.4 0.6 gather_fusion.2
  20.4 2.6 %copy.66 = s32[64,8,128]{1,2,0:T(8,128)} copy(s32[64,8,128]{2,1,0:T(8,128)S(1)} %gather.28) | data formatting | bytes 524288 | tf_op jit(solution)/shard_map/jit(_take)/gather | solution.py:151
  23.0 0.7 broadcast_in_dim.79
  24.0 4.9 %select_subtract_fusion = s32[64,8,128]{1,2,0:T(8,128)} fusion(s32[64,8,128]{1,2,0:T(8,128)} %copy.66, s32[8]{0:T(128)S(1)} %fusion.4, pred[8]{0:T(512)(128)(4,1)S(1)} %broadcast_in_dim.73), kind=kLoop, calls=%fused_computation.5 | loop fusion | flops 131072 | bytes 524328 | tf_op jit(solution)/shard_map/sub | solution.py:153
  28.8 3.5 %copy.70.perm_ref = s32[64,8,128]{2,1,0:T(8,128)} copy(s32[64,8,128]{1,2,0:T(8,128)} %select_subtract_fusion) | data formatting | bytes 524288 | tf_op jit(solution)/shard_map/sub | solution.py:153
  32.5 0.6 gather_fusion.4
  33.2 0.6 gather_fusion.3
  34.1 4.6 %copy.71.w_ref = f32[64,128,1]{2,1,0:T(8,128)} copy(f32[64,128,1]{0,1,2:T(8,128)S(1)} %fusion.2) | data formatting | bytes 65536 | tf_op jit(solution)/shard_map/mul | solution.py:146
  38.6 4.9 %fusion.8.perm_t_ref = s32[64,128,8]{2,1,0:T(8,128)} fusion(s32[8]{0:T(128)S(1)} %fusion.4, s32[64,8,128]{1,2,0:T(8,128)} %copy.66, pred[8]{0:T(512)(128)(4,1)S(1)} %broadcast_in_dim.73), kind=kLoop, calls=%fused_computation.42 | loop fusion | flops 131072 | bytes 524328 | tf_op jit(solution)/shard_map/transpose | solution.py:156
  43.5 1.5 %copy.63 = bf16[8,8,2,8,2,512]{5,3,4,2,1,0:T(8,128)(2,1)} copy(bf16[8,8,2,8,2,512]{5,3,4,2,0,1:T(8,128)(2,1)S(1)} %bitcast.39) | data formatting | bytes 4194304 | tf_op jit(solution)/shard_map/transpose | solution.py:135
  45.1 19.8 %shard_map.82 = f32[1,256,512]{2,1,0:T(8,128)} custom-call(s32[64]{0:T(128)} %star_ref.3, bf16[8,128,1024]{2,1,0:T(8,128)(2,1)} %bitcast.36, s32[64,8,128]{2,1,0:T(8,128)} %copy.70.perm_ref, s32[64,128,8]{2,1,0:T(8,128)} %fusion.8.perm_t_ref, f32[64,128,1]{2,1,0:T(8,128)} %copy.71.w_ref), custom_call_target="tpu_custom_call" | custom-call | tf_op jit(solution)/shard_map/pallas_call | solution.py:83
  64.8 1.2 reshape.248
  66.1 0.9 copy.72
  66.9 9.3 %all-to-all-start.1 = ((f32[16,1,64,128]{3,2,1,0:T(8,128)}), f32[16,1,64,128]{3,2,1,0:T(8,128)S(1)}, u32[]{:S(2)}, u32[]{:S(2)}) async-start(f32[16,1,64,128]{3,2,1,0:T(8,128)} %bitcast.16), calls=%async_computation.1 | async-start | bytes 1048576 | tf_op jit(solution)/shard_map/all_to_all | solution.py:162
  76.2 19.8 %shard_map.83 = f32[1,256,512]{2,1,0:T(8,128)} custom-call(s32[64]{0:T(128)} %star_ref.3, bf16[8,128,1024]{2,1,0:T(8,128)(2,1)} %bitcast.37, s32[64,8,128]{2,1,0:T(8,128)} %copy.70.perm_ref, s32[64,128,8]{2,1,0:T(8,128)} %fusion.8.perm_t_ref, f32[64,128,1]{2,1,0:T(8,128)} %copy.71.w_ref), custom_call_target="tpu_custom_call" | custom-call | tf_op jit(solution)/shard_map/pallas_call | solution.py:83
  96.0 1.2 reshape.250
  97.2 0.9 copy.76
  98.1 8.1 %all-to-all-start.2 = ((f32[16,1,64,128]{3,2,1,0:T(8,128)}), f32[16,1,64,128]{3,2,1,0:T(8,128)S(1)}, u32[]{:S(2)}, u32[]{:S(2)}) async-start(f32[16,1,64,128]{3,2,1,0:T(8,128)} %bitcast.20), calls=%async_computation.2 | async-start | bytes 1048576 | tf_op jit(solution)/shard_map/all_to_all | solution.py:162
  106.2 16.1 %all-to-all-done.2 = f32[16,1,64,128]{3,2,1,0:T(8,128)S(1)} async-done(((f32[16,1,64,128]{3,2,1,0:T(8,128)}), f32[16,1,64,128]{3,2,1,0:T(8,128)S(1)}, u32[]{:S(2)}, u32[]{:S(2)}) %all-to-all-start.2) | async-done | bytes 524320 | tf_op jit(solution)/shard_map/all_to_all | solution.py:162
  122.4 2.8 %collective-permute-start = (f32[1,128,128]{2,1,0:T(8,128)S(1)}, f32[1,128,128]{2,1,0:T(8,128)S(1)}, u32[]{:S(2)}, u32[]{:S(2)}) collective-permute-start(f32[1,128,128]{2,1,0:T(8,128)S(1)} %pad_maximum_fusion), channel_id=1, source_target_pairs={{0,0},{1,68},{2,136},{3,204},{4,64},{5,4},{6,128},{7,8},{8,192},{9... | collective-permute-start | bytes 196616 | tf_op jit(solution)/shard_map/ppermute | solution.py:165
  125.2 10.0 %collective-permute-done = f32[1,128,128]{2,1,0:T(8,128)S(1)} collective-permute-done((f32[1,128,128]{2,1,0:T(8,128)S(1)}, f32[1,128,128]{2,1,0:T(8,128)S(1)}, u32[]{:S(2)}, u32[]{:S(2)}) %collective-permute-start) | collective-permute-done | bytes 65568 | tf_op jit(solution)/shard_map/ppermute | solution.py:165
  135.2 0.6 copy.79
  (51 shorter events, 2.6 us)
Async XLA Ops:
  0.0 1.1 copy-start
  5.4 8.8 %copy-start.3 = (s32[64]{0:T(128)S(1)}, s32[64]{0:T(128)}, u32[]{:S(2)}) copy-start(s32[64]{0:T(128)} %star_ref.3) | copy-start | bytes 772
  5.4 8.8 %copy-start.6 = (s32[64]{0:T(128)S(1)}, s32[64]{0:T(128)}, u32[]{:S(2)}) copy-start(s32[64]{0:T(128)} %param.12) | copy-start | bytes 772
  5.4 12.5 %copy-start.2 = (s32[48,2048]{1,0:T(8,128)S(1)}, s32[48,2048]{1,0:T(8,128)}, u32[]{:S(2)}) copy-start(s32[48,2048]{1,0:T(8,128)} %param.13) | copy-start | bytes 1179652
  7.0 36.6 %all-to-all-start = ((bf16[8,8,2,8,2,512]{5,3,4,2,1,0:T(8,128)(2,1)}), bf16[8,8,2,8,2,512]{5,3,4,2,1,0:T(8,128)(2,1)S(1)}, u32[]{:S(2)}, u32[]{:S(2)}) async-start(bf16[8,8,2,8,2,512]{5,3,4,2,1,0:T(8,128)(2,1)} %copy.62), calls=%async_computation | async-start | bytes 4194304 | tf_op jit(solution)/shard_map/all_to_all | solution.py:133
  19.0 4.8 %copy-start.8 = (pred[2]{0:T(512)(128)(4,1)S(1)}, pred[2]{0:T(512)(128)(4,1)}, u32[]{:S(2)}) copy-start(pred[2]{0:T(512)(128)(4,1)} %compare_and_fusion.2) | copy-start | bytes 10
  28.8 3.5 %copy-start.5 = (s32[64]{0:T(128)S(1)}, s32[64]{0:T(128)}, u32[]{:S(2)}) copy-start(s32[64]{0:T(128)} %get-tuple-element.7) | copy-start | bytes 772
  28.8 3.5 %copy-start.4 = (f32[8,256]{1,0:T(8,128)S(1)}, f32[8,256]{1,0:T(8,128)}, u32[]{:S(2)}) copy-start(f32[8,256]{1,0:T(8,128)} %param.10) | copy-start | bytes 24580
  28.8 4.4 %copy-start.1 = (f32[8,8]{1,0:T(8,128)S(1)}, f32[8,8]{1,0:T(8,128)}, u32[]{:S(2)}) copy-start(f32[8,8]{1,0:T(8,128)} %param.9) | copy-start | bytes 772
  28.8 5.1 %copy-start.7 = (s32[64]{0:T(128)S(1)}, s32[64]{0:T(128)}, u32[]{:S(2)}) copy-start(s32[64]{0:T(128)} %param.14) | copy-start | bytes 772
  66.9 31.1 %all-to-all-start.1 = ((f32[16,1,64,128]{3,2,1,0:T(8,128)}), f32[16,1,64,128]{3,2,1,0:T(8,128)S(1)}, u32[]{:S(2)}, u32[]{:S(2)}) async-start(f32[16,1,64,128]{3,2,1,0:T(8,128)} %bitcast.16), calls=%async_computation.1 | async-start | bytes 1048576 | tf_op jit(solution)/shard_map/all_to_all | solution.py:162
  98.1 24.3 %all-to-all-start.2 = ((f32[16,1,64,128]{3,2,1,0:T(8,128)}), f32[16,1,64,128]{3,2,1,0:T(8,128)S(1)}, u32[]{:S(2)}, u32[]{:S(2)}) async-start(f32[16,1,64,128]{3,2,1,0:T(8,128)} %bitcast.20), calls=%async_computation.2 | async-start | bytes 1048576 | tf_op jit(solution)/shard_map/all_to_all | solution.py:162
  122.4 12.8 %collective-permute-start = (f32[1,128,128]{2,1,0:T(8,128)S(1)}, f32[1,128,128]{2,1,0:T(8,128)S(1)}, u32[]{:S(2)}, u32[]{:S(2)}) collective-permute-start(f32[1,128,128]{2,1,0:T(8,128)S(1)} %pad_maximum_fusion), channel_id=1, source_target_pairs={{0,0},{1,68},{2,136},{3,204},{4,64},{5,4},{6,128},{7,8},{8,192},{9... | collective-permute-start | bytes 196616 | tf_op jit(solution)/shard_map/ppermute | solution.py:165

commit v5 on v3

--- a/solution.py
+++ b/solution.py
@@ -26,39 +26,33 @@
 freq_step = 2.0
 
 
-def chi_kernel(star_ref, loc_ref, perm_ref, perm_t_ref, w_ref, out_ref):
+def chi_kernel(star_ref, loc_ref, onehot_ref, w_ref, out_ref):
     step = pl.program_id(0)
 
     @pl.when(step == 0)
     def _():
         out_ref[...] = jnp.zeros_like(out_ref)
 
-    lane = lax.broadcasted_iota(jnp.int32, (GB, GB), 1)
-    sub = lax.broadcasted_iota(jnp.int32, (GB, GB), 0)
     nt = (((1,), (1,)), ((), ()))
     subs = BW // GB
     lhs_parts = []
     rhs_parts = [[] for _ in range(NF)]
     for t in range(KB):
         x = loc_ref[star_ref[step * KB + t]]
-        slots_col = perm_t_ref[t]
         row_parts = []
         for q in range(subs):
-            onehot = jnp.where(slots_col[:, q : q + 1] == lane, 1.0, 0.0).astype(jnp.bfloat16)
             row_parts.append(
                 lax.dot_general(
-                    onehot, x[:, q * GB : (q + 1) * GB], nt,
+                    onehot_ref[t, q], x[:, q * GB : (q + 1) * GB], nt,
                     preferred_element_type=jnp.float32,
                 )
             )
         row_t = jnp.concatenate(row_parts, axis=0).astype(jnp.bfloat16)
-        slots_row = perm_ref[t]
         col_parts = []
         for q in range(subs, 2 * subs):
-            onehot_t = jnp.where(slots_row[q : q + 1, :] == sub, 1.0, 0.0).astype(jnp.bfloat16)
             col_parts.append(
                 jnp.dot(
-                    x[:, q * GB : (q + 1) * GB], onehot_t,
+                    x[:, q * GB : (q + 1) * GB], onehot_ref[t, q],
                     preferred_element_type=jnp.float32,
                 )
             )
@@ -75,7 +69,7 @@
         out_ref[f] += jnp.dot(lhs, rhs, preferred_element_type=jnp.float32)
 
 
-def chi_block(star_map, loc, perm, perm_t, weight_c):
+def chi_block(star_map, loc, onehot, weight_c):
     rows = loc.shape[1]
     return pl.pallas_call(
         chi_kernel,
@@ -85,14 +79,13 @@
             grid=(KF // KB,),
             in_specs=[
                 pl.BlockSpec((KI, rows, 2 * BW), lambda st, sm: (0, 0, 0)),
-                pl.BlockSpec((KB, 2 * BW // GB, GB), lambda st, sm: (st, 0, 0)),
-                pl.BlockSpec((KB, GB, 2 * BW // GB), lambda st, sm: (st, 0, 0)),
+                pl.BlockSpec((KB, 2 * BW // GB, GB, GB), lambda st, sm: (st, 0, 0, 0)),
                 pl.BlockSpec((KB, rows, NF), lambda st, sm: (st, 0, 0)),
             ],
             out_specs=pl.BlockSpec((NF, BW, BW), lambda st, sm: (0, 0, 0)),
         ),
         compiler_params=pltpu.CompilerParams(dimension_semantics=("arbitrary",)),
-    )(star_map, loc, perm, perm_t, weight_c)
+    )(star_map, loc, onehot, weight_c)
 
 
 def slab_perm(ka_count, band_count, ga_count):
@@ -150,8 +143,11 @@
     local = my_perm.reshape(KF, 2 * subs, GB) - (
         my_blocks.repeat(subs) * BW + (jnp.arange(2 * subs) % subs) * GB
     )[None, :, None]
-    perm_t = jnp.transpose(local, (0, 2, 1))
-    partial_value = chi_block(star_map, loc, local, perm_t, weight_c)
+    slot = jnp.arange(GB)
+    row_side = local[:, :subs, :, None] == slot[None, None, None, :]
+    col_side = local[:, subs:, None, :] == slot[None, None, :, None]
+    onehot = jnp.concatenate([row_side, col_side], axis=1).astype(jnp.bfloat16)
+    partial_value = chi_block(star_map, loc, onehot, weight_c)
 
     pieces = partial_value.reshape(NF, subs, GB, subs, GB).transpose(1, 3, 0, 2, 4)
     pieces = pieces.reshape(subs * subs, NF, GB, GB)

time: 124 us -> 124 us (level)
  other arithmetic: 14.9 us -> 21.3 us
  local copies, waits for them, and re-layouts: 25.2 us -> 20.5 us
  Pallas kernels: 25.9 us -> 24.5 us
    eq x0 -> x2, other arithmetic: none -> 9.11 us  [the longest x1 6.42 us: on_device(): row_side = local[:, :subs, :, None] == slot[None, None, None, :]]
    convert_element_type x0 -> x1, other arithmetic: none -> 6.43 us  [on_device(): onehot = jnp.concatenate([row_side, col_side], axis=1).astype(jnp.bfloat16)]
    transpose x1 -> x0, other arithmetic: 4.89 us -> none  [on_device(): perm_t = jnp.transpose(local, (0, 2, 1))]
    sub x1, other arithmetic: 4.87 us -> 0.09 us  [on_device(): my_perm.reshape(KF, 2 * subs, GB)]
    sub x1 -> x0, local copies, waits for them, and re-layouts: 3.5 us -> none  [on_device(): my_perm.reshape(KF, 2 * subs, GB)]
    gather x4 -> x3, local copies, waits for them, and re-layouts: 3.61 us -> 0.98 us  [on_device(): jnp.take(jnp.take(perm_blocks, op_of_k, axis=0), my_blocks, axis=1)]
    pallas_call x1, Pallas kernels: 25.9 us -> 24.5 us  [chi_block(): pl.pallas_call(chi_kernel, out_shape=jax.ShapeDtypeStruct((NF, BW, BW), j...]
  transfers between devices with their start and end apart: 2 -> 2, of which waited for: 1 -> 1; matrix products, arithmetic and copies ran while one was open for 24% -> 25% of each run, Pallas kernels for 0% -> 0%
where the time goes in v5:
time: 124 us; the launch traced here: 123 us
  blocking collectives  37 us (30%)
  Pallas kernels  24.5 us (20%)
  other arithmetic  21.3 us (17%)
  local copies, waits for them, and re-layouts  20.5 us (17%)
  starting transfers between devices  10 us (8%)
  waiting for transfers between devices  9.92 us (8%)
    all_to_all x1, blocking collectives, on_device(): got = lax.all_to_all(pieces, 'ka', 0, 0, tiled=False)  37 us
    pallas_call x1, Pallas kernels, chi_block(): pl.pallas_call(chi_kernel, out_shape=jax.ShapeDtypeStruct((NF, BW, BW), j...  24.5 us
    ppermute x1, waiting for transfers between devices, on_device(): lax.ppermute(slab, ('ka', 'band', 'ga'), slab_perm(ka_count, band_count,...  9.92 us
    all_to_all x1, starting transfers between devices, on_device(): recv = lax.all_to_all(send, 'band', 0, 0, tiled=False)  7.18 us
    convert_element_type x1, other arithmetic, on_device(): onehot = jnp.concatenate([row_side, col_side], axis=1).astype(jnp.bfloat16)  6.43 us
    eq x1, other arithmetic, on_device(): row_side = local[:, :subs, :, None] == slot[None, None, None, :]  6.42 us
    mul x1, local copies, waits for them, and re-layouts, on_device(): weight = 4.0 / KF * diff[None] / (diff[None] * diff[None] + omega_sq) * mask  4.57 us
    gather x2, local copies, waits for them, and re-layouts, on_device(): send = jnp.take(blocked, blocks[:, ga_index].reshape(-1), axis=3)  3.84 us
  transfers between devices with their start and end apart: 2, of which 1 were waited for; matrix products, arithmetic and copies ran while one was open for 25% of the time, Pallas kernels for 0%

profile of v5, /device:TPU:22, one launch (start us, length us, event | category | flops | bytes accessed | tf_op | source)
XLA Modules:
  0.0 123.5 jit_solution(10244080841680821211)
XLA Ops:
  0.0 0.8 constant_dynamic-slice_fusion.2
  1.1 2.0 %gather_fusion = bf16[16,8,2,8,512]{4,3,2,1,0:T(8,128)(2,1)} fusion(bf16[8,2,8,4,512]{4,2,3,1,0:T(8,128)(2,1)S(1)} %bitcast.27, s32[1024]{0:T(1024)S(1)} %pad_clamp_fusion.3), kind=kCustom, calls=%fused_computation | custom fusion | bytes 4194368 | tf_op jit(solution)/shard_map/jit(_take)/gather | solution.py:120
  3.1 1.8 %copy.30 = bf16[8,2,8,16,512]{4,2,3,1,0:T(8,128)(2,1)S(1)} copy(bf16[8,2,8,16,512]{4,2,1,0,3:T(8,128)(2,1)} %bitcast.30) | data formatting | bytes 4194304 | tf_op jit(solution)/shard_map/jit(_take)/gather | solution.py:120
  5.1 0.3 select_bitcast_fusion
  5.4 1.5 %copy.31 = bf16[8,8,2,8,2,512]{5,3,4,2,1,0:T(8,128)(2,1)} copy(bf16[8,8,2,8,2,512]{5,3,4,0,2,1:T(8,128)(2,1)S(1)} %select_bitcast_fusion) | data formatting | bytes 4194304 | tf_op jit(solution)/shard_map/transpose | solution.py:122
  6.9 7.2 %all-to-all-start = ((bf16[8,8,2,8,2,512]{5,3,4,2,1,0:T(8,128)(2,1)}), bf16[8,8,2,8,2,512]{5,3,4,2,1,0:T(8,128)(2,1)S(1)}, u32[]{:S(2)}, u32[]{:S(2)}) async-start(bf16[8,8,2,8,2,512]{5,3,4,2,1,0:T(8,128)(2,1)} %copy.31), calls=%async_computation | async-start | bytes 4194304 | tf_op jit(solution)/shard_map/all_to_all | solution.py:123
  14.1 0.5 compare_select_fusion.1
  14.6 0.5 compare_and_fusion
  15.2 0.7 fusion.6
  15.9 1.3 %bitcast_multiply_fusion = s32[2]{0:T(128)} fusion(s32[8,2,2]{2,1,0:T(2,128)} %constant.114.clone, s32[]{:T(128)S(6)} %select_n.99, s32[]{:T(128)S(6)} %select_n.95), kind=kLoop, calls=%fused_computation.41 | loop fusion | flops 2 | bytes 24 | tf_op jit(solution)/shard_map/mul | solution.py:144
  17.1 1.2 compare_and_fusion.2
  18.4 0.3 reshape.242
  18.6 0.9 gather_fusion.1
  19.5 0.8 broadcast_select_fusion
  20.5 0.6 gather_fusion.2
  21.1 0.2 copy.34
  21.3 0.2 gather.28
  21.5 0.7 broadcast_in_dim.83
  22.4 0.7 broadcast_in_dim.76
  23.3 6.4 %iota_compare_fusion.1 = pred[64,4,128,128]{3,2,1,0:T(8,128)(4,1)} fusion(s32[64,4,128]{2,1,0:T(4,128)S(1)} %get-tuple-element.5), kind=kLoop, calls=%fused_computation.7 | loop fusion | flops 4194304 | bytes 4325376 | tf_op jit(solution)/shard_map/eq | solution.py:147
  29.8 0.6 gather_fusion.4
  30.6 0.6 gather_fusion.3
  31.4 4.6 %copy.37.w_ref = f32[64,128,1]{2,1,0:T(8,128)} copy(f32[64,128,1]{0,1,2:T(8,128)S(1)} %fusion.2) | data formatting | bytes 65536 | tf_op jit(solution)/shard_map/mul | solution.py:136
  36.0 2.7 %iota_compare_fusion = pred[64,4,128,128]{3,2,1,0:T(8,128)(4,1)S(1)} fusion(s32[64,4,128]{2,1,0:T(4,128)S(1)} %get-tuple-element.6), kind=kLoop, calls=%fused_computation.6 | loop fusion | flops 4194304 | bytes 4325376 | tf_op jit(solution)/shard_map/eq | solution.py:148
  38.7 6.4 %add_convert_fusion.onehot_ref = bf16[64,8,128,128]{3,2,1,0:T(8,128)(2,1)} fusion(pred[64,4,128,128]{3,2,1,0:T(8,128)(4,1)S(1)} %iota_compare_fusion, pred[64,4,128,128]{3,2,1,0:T(8,128)(4,1)S(1)} %copy-done.2), kind=kLoop, calls=%fused_computation.5 | loop fusion | flops 16777216 | bytes 25165824 | tf_op jit(solution)/shard_map/convert_element_type | solution.py:149
  45.1 1.6 %copy.32 = bf16[8,8,2,8,2,512]{5,3,4,2,1,0:T(8,128)(2,1)} copy(bf16[8,8,2,8,2,512]{5,3,4,2,0,1:T(8,128)(2,1)S(1)} %bitcast.29) | data formatting | bytes 4194304 | tf_op jit(solution)/shard_map/transpose | solution.py:125
  46.8 24.5 %shard_map.82 = f32[1,512,512]{2,1,0:T(8,128)} custom-call(s32[64]{0:T(128)} %star_ref.1, bf16[8,128,1024]{2,1,0:T(8,128)(2,1)} %bitcast.31, bf16[64,8,128,128]{3,2,1,0:T(8,128)(2,1)} %add_convert_fusion.onehot_ref, f32[64,128,1]{2,1,0:T(8,128)} %copy.37.w_ref), custom_call_target="tpu_custom_call" | custom-call | tf_op jit(solution)/shard_map/pallas_call | solution.py:74
  71.3 1.6 %reshape.243 = f32[1,4,128,4,128]{4,3,2,1,0:T(4,128)S(1)} reshape(f32[1,512,512]{2,1,0:T(8,128)} %shard_map.82) | data formatting | bytes 2097152 | tf_op jit(solution)/shard_map/reshape | solution.py:152
  73.0 37.0 %all_to_all.10 = f32[16,1,128,128]{3,2,1,0:T(8,128)S(1)} all-to-all(f32[16,1,128,128]{3,2,1,0:T(8,128)S(1)} %bitcast.32), channel_id=1, replica_groups=mesh['ka'=16,'band'=8,'ga'=2] {'ka'}, dimensions={0} | all-to-all | bytes 2097152 | tf_op jit(solution)/shard_map/all_to_all | solution.py:154
  110.1 2.9 %collective-permute-start = (f32[1,128,128]{2,1,0:T(8,128)S(1)}, f32[1,128,128]{2,1,0:T(8,128)S(1)}, u32[]{:S(2)}, u32[]{:S(2)}) collective-permute-start(f32[1,128,128]{2,1,0:T(8,128)S(1)} %bitcast.34), channel_id=1, source_target_pairs={{0,0},{1,68},{2,136},{3,204},{4,64},{5,4},{6,128},{7,8},{8,192},{9... | collective-permute-start | bytes 196616 | tf_op jit(solution)/shard_map/ppermute | solution.py:156
  112.9 9.9 %collective-permute-done = f32[1,128,128]{2,1,0:T(8,128)S(1)} collective-permute-done((f32[1,128,128]{2,1,0:T(8,128)S(1)}, f32[1,128,128]{2,1,0:T(8,128)S(1)}, u32[]{:S(2)}, u32[]{:S(2)}) %collective-permute-start) | collective-permute-done | bytes 65568 | tf_op jit(solution)/shard_map/ppermute | solution.py:156
  122.9 0.6 copy.41
  (44 shorter events, 1.7 us)
Async XLA Ops:
  0.0 1.1 copy-start
  5.4 8.8 %copy-start.4 = (s32[64]{0:T(128)S(1)}, s32[64]{0:T(128)}, u32[]{:S(2)}) copy-start(s32[64]{0:T(128)} %star_ref.1) | copy-start | bytes 772
  5.4 8.7 %copy-start.7 = (s32[64]{0:T(128)S(1)}, s32[64]{0:T(128)}, u32[]{:S(2)}) copy-start(s32[64]{0:T(128)} %param.12) | copy-start | bytes 772
  5.4 13.0 %copy-start.3 = (s32[48,2048]{1,0:T(8,128)S(1)}, s32[48,2048]{1,0:T(8,128)}, u32[]{:S(2)}) copy-start(s32[48,2048]{1,0:T(8,128)} %param.13) | copy-start | bytes 1179652
  6.9 38.2 %all-to-all-start = ((bf16[8,8,2,8,2,512]{5,3,4,2,1,0:T(8,128)(2,1)}), bf16[8,8,2,8,2,512]{5,3,4,2,1,0:T(8,128)(2,1)S(1)}, u32[]{:S(2)}, u32[]{:S(2)}) async-start(bf16[8,8,2,8,2,512]{5,3,4,2,1,0:T(8,128)(2,1)} %copy.31), calls=%async_computation | async-start | bytes 4194304 | tf_op jit(solution)/shard_map/all_to_all | solution.py:123
  20.3 9.4 %copy-start.6 = (s32[64]{0:T(128)S(1)}, s32[64]{0:T(128)}, u32[]{:S(2)}) copy-start(s32[64]{0:T(128)} %get-tuple-element.9) | copy-start | bytes 772
  20.3 9.4 %copy-start.5 = (f32[8,256]{1,0:T(8,128)S(1)}, f32[8,256]{1,0:T(8,128)}, u32[]{:S(2)}) copy-start(f32[8,256]{1,0:T(8,128)} %param.10) | copy-start | bytes 24580
  20.3 10.2 %copy-start.1 = (f32[8,8]{1,0:T(8,128)S(1)}, f32[8,8]{1,0:T(8,128)}, u32[]{:S(2)}) copy-start(f32[8,8]{1,0:T(8,128)} %param.9) | copy-start | bytes 772
  20.4 11.0 %copy-start.8 = (s32[64]{0:T(128)S(1)}, s32[64]{0:T(128)}, u32[]{:S(2)}) copy-start(s32[64]{0:T(128)} %param.14) | copy-start | bytes 772
  36.0 2.7 %copy-start.2 = (pred[64,4,128,128]{3,2,1,0:T(8,128)(4,1)S(1)}, pred[64,4,128,128]{3,2,1,0:T(8,128)(4,1)}, u32[]{:S(2)}) copy-start(pred[64,4,128,128]{3,2,1,0:T(8,128)(4,1)} %iota_compare_fusion.1) | copy-start | bytes 12582916
  110.1 12.8 %collective-permute-start = (f32[1,128,128]{2,1,0:T(8,128)S(1)}, f32[1,128,128]{2,1,0:T(8,128)S(1)}, u32[]{:S(2)}, u32[]{:S(2)}) collective-permute-start(f32[1,128,128]{2,1,0:T(8,128)S(1)} %bitcast.34), channel_id=1, source_target_pairs={{0,0},{1,68},{2,136},{3,204},{4,64},{5,4},{6,128},{7,8},{8,192},{9... | collective-permute-start | bytes 196616 | tf_op jit(solution)/shard_map/ppermute | solution.py:156

commit v6 on v5

--- a/solution.py
+++ b/solution.py
@@ -4,6 +4,7 @@
 from jax.experimental import pallas as pl
 from jax.experimental.pallas import tpu as pltpu
 from jax.sharding import PartitionSpec as P
+
 
 NG = 2048
 GB = 128
@@ -20,18 +21,22 @@
     tuple((PAIR[j][LOCAL[j][g][0]], PAIR[j][LOCAL[j][g][1]]) for g in range(2))
     for j in range(len(PAIR))
 )
-KB = 4
+KB = 8
 
 
 freq_step = 2.0
 
 
-def chi_kernel(star_ref, loc_ref, onehot_ref, w_ref, out_ref):
+def chi_kernel(star_ref, loc_ref, onehot_ref, w_ref, *refs):
     step = pl.program_id(0)
+    out_ref = refs[-1]
 
     @pl.when(step == 0)
     def _():
-        out_ref[...] = jnp.zeros_like(out_ref)
+        if len(refs) == 2:
+            out_ref[...] = refs[0][...]
+        else:
+            out_ref[...] = jnp.zeros_like(out_ref)
 
     nt = (((1,), (1,)), ((), ()))
     subs = BW // GB
@@ -69,8 +74,10 @@
         out_ref[f] += jnp.dot(lhs, rhs, preferred_element_type=jnp.float32)
 
 
-def chi_block(star_map, loc, onehot, weight_c):
+def chi_block(star_map, loc, onehot, weight_c, start=None):
     rows = loc.shape[1]
+    extra = [] if start is None else [start]
+    extra_specs = [pl.BlockSpec((NF, BW, BW), lambda st, sm: (0, 0, 0))] * len(extra)
     return pl.pallas_call(
         chi_kernel,
         out_shape=jax.ShapeDtypeStruct((NF, BW, BW), jnp.float32),
@@ -81,11 +88,12 @@
                 pl.BlockSpec((KI, rows, 2 * BW), lambda st, sm: (0, 0, 0)),
                 pl.BlockSpec((KB, 2 * BW // GB, GB, GB), lambda st, sm: (st, 0, 0, 0)),
                 pl.BlockSpec((KB, rows, NF), lambda st, sm: (st, 0, 0)),
-            ],
+            ]
+            + extra_specs,
             out_specs=pl.BlockSpec((NF, BW, BW), lambda st, sm: (0, 0, 0)),
         ),
         compiler_params=pltpu.CompilerParams(dimension_semantics=("arbitrary",)),
-    )(star_map, loc, onehot, weight_c)
+    )(star_map, loc, onehot, weight_c, *extra)
 
 
 def slab_perm(ka_count, band_count, ga_count):
@@ -120,9 +128,14 @@
     send = jnp.take(blocked, blocks[:, ga_index].reshape(-1), axis=3)
     send = send.reshape(KI, cond_piece, NV, band_count, 2, BW)
     send = jnp.moveaxis(send, 3, 0)
-    recv = lax.all_to_all(send, "band", 0, 0, tiled=False)
     c_loc = band_count * cond_piece
-    loc = jnp.moveaxis(recv, 0, 1).reshape(KI, c_loc * NV, 2 * BW)
+    v_half = NV // 2
+    locs = []
+    for h in range(2):
+        recv = lax.all_to_all(
+            send[:, :, :, h * v_half : (h + 1) * v_half], "band", 0, 0, tiled=False
+        )
+        locs.append(jnp.moveaxis(recv, 0, 1).reshape(KI, c_loc * v_half, 2 * BW))
 
     c_base = ka_index * c_loc
     cond_grp = lax.dynamic_slice_in_dim(conduction_energy, c_base, c_loc, axis=1)
@@ -134,7 +147,7 @@
     omega_sq = (omega * omega)[:, None, None, None]
     diff = val_local[:, None, :] - cond_local[:, :, None]
     weight = 4.0 / KF * diff[None] / (diff[None] * diff[None] + omega_sq) * mask
-    weight_c = jnp.transpose(weight.reshape(NF, KF, c_loc * NV), (1, 2, 0))
+    weight_c = jnp.transpose(weight, (1, 2, 3, 0))
 
     my_blocks = blocks[band_index, ga_index]
     perm_blocks = perm_lists.reshape(perm_lists.shape[0], NB, BW)
@@ -147,7 +160,10 @@
     row_side = local[:, :subs, :, None] == slot[None, None, None, :]
     col_side = local[:, subs:, None, :] == slot[None, None, :, None]
     onehot = jnp.concatenate([row_side, col_side], axis=1).astype(jnp.bfloat16)
-    partial_value = chi_block(star_map, loc, onehot, weight_c)
+    partial_value = None
+    for h in range(2):
+        weight_h = weight_c[:, :, h * v_half : (h + 1) * v_half].reshape(KF, c_loc * v_half, NF)
+        partial_value = chi_block(star_map, locs[h], onehot, weight_h, partial_value)
 
     pieces = partial_value.reshape(NF, subs, GB, subs, GB).transpose(1, 3, 0, 2, 4)
     pieces = pieces.reshape(subs * subs, NF, GB, GB)

time: 124 us -> 154 us (1.24)
  local copies, waits for them, and re-layouts: 20.5 us -> 30.2 us
  Pallas kernels: 24.5 us -> 31.7 us
  starting transfers between devices: 10 us -> 16.9 us
  other arithmetic: 21.3 us -> 26.7 us
    reshape x0 -> x4, local copies, waits for them, and re-layouts: none -> 9.97 us  [the longest x2 5.84 us: on_device(): weight_c[:, :, h * v_half:(h + 1) * v_half].reshape(KF, c_loc * v_half, NF)]
    all_to_all x1 -> x2, starting transfers between devices: 7.18 us -> 14.4 us  [on_device(): lax.all_to_all(send[:, :, :, h * v_half:(h + 1) * v_half], 'band', 0, 0,...]
    pallas_call x1 -> x2, Pallas kernels: 24.5 us -> 31.7 us  [chi_block(): pl.pallas_call(chi_kernel, out_shape=jax.ShapeDtypeStruct((NF, BW, BW), j...]
    mul x1 -> x0, local copies, waits for them, and re-layouts: 4.57 us -> none  [on_device(): weight = 4.0 / KF * diff[None] / (diff[None] * diff[None] + omega_sq) * mask]
    slice x0 -> x4, local copies, waits for them, and re-layouts: none -> 4.15 us  [the longest x3 4.14 us: on_device(): send[:, :, :, h * v_half:(h + 1) * v_half]]
    convert_element_type x1, other arithmetic: 6.43 us -> 9.93 us  [on_device(): onehot = jnp.concatenate([row_side, col_side], axis=1).astype(jnp.bfloat16)]
    eq x1, other arithmetic: 2.69 us -> 4.67 us  [on_device(): col_side = local[:, subs:, None, :] == slot[None, None, :, None]]
  transfers between devices with their start and end apart: 2 -> 3, of which waited for: 1 -> 1; matrix products, arithmetic and copies ran while one was open for 25% -> 29% of each run, Pallas kernels for 0% -> 0%
where the time goes in v6:
time: 154 us; the launch traced here: 153 us
  blocking collectives  36.9 us (24%)
  Pallas kernels  31.7 us (21%)
  local copies, waits for them, and re-layouts  30.2 us (20%)
  other arithmetic  26.7 us (17%)
  starting transfers between devices  16.9 us (11%)
  waiting for transfers between devices  10.3 us (7%)
    all_to_all x1, blocking collectives, on_device(): got = lax.all_to_all(pieces, 'ka', 0, 0, tiled=False)  36.9 us
    pallas_call x2, Pallas kernels, chi_block(): pl.pallas_call(chi_kernel, out_shape=jax.ShapeDtypeStruct((NF, BW, BW), j...  31.7 us
    all_to_all x2, starting transfers between devices, on_device(): lax.all_to_all(send[:, :, :, h * v_half:(h + 1) * v_half], 'band', 0, 0,...  14.4 us
    ppermute x1, waiting for transfers between devices, on_device(): lax.ppermute(slab, ('ka', 'band', 'ga'), slab_perm(ka_count, band_count,...  10.3 us
    convert_element_type x1, other arithmetic, on_device(): onehot = jnp.concatenate([row_side, col_side], axis=1).astype(jnp.bfloat16)  9.93 us
    eq x1, other arithmetic, on_device(): row_side = local[:, :subs, :, None] == slot[None, None, None, :]  6.41 us
    reshape x2, local copies, waits for them, and re-layouts, on_device(): weight_c[:, :, h * v_half:(h + 1) * v_half].reshape(KF, c_loc * v_half, NF)  5.84 us
    eq x1, other arithmetic, on_device(): col_side = local[:, subs:, None, :] == slot[None, None, :, None]  4.67 us
  transfers between devices with their start and end apart: 3, of which 1 were waited for; matrix products, arithmetic and copies ran while one was open for 29% of the time, Pallas kernels for 0%

profile of v6, /device:TPU:22, one launch (start us, length us, event | category | flops | bytes accessed | tf_op | source)
XLA Modules:
  0.0 152.8 jit_solution(10557668129702140917)
XLA Ops:
  0.0 0.8 constant_dynamic-slice_fusion.2
  1.1 2.0 %gather_fusion = bf16[16,8,2,8,512]{4,3,2,1,0:T(8,128)(2,1)} fusion(bf16[8,2,8,4,512]{4,2,3,1,0:T(8,128)(2,1)S(1)} %bitcast.27, s32[1024]{0:T(1024)S(1)} %pad_clamp_fusion.3), kind=kCustom, calls=%fused_computation | custom fusion | bytes 4194368 | tf_op jit(solution)/shard_map/jit(_take)/gather | solution.py:128
  3.1 1.8 %copy.34 = bf16[8,2,8,16,512]{4,2,3,1,0:T(8,128)(2,1)S(1)} copy(bf16[8,2,8,16,512]{4,2,1,0,3:T(8,128)(2,1)} %bitcast.29) | data formatting | bytes 4194304 | tf_op jit(solution)/shard_map/jit(_take)/gather | solution.py:128
  5.4 0.8 fusion.7
  6.2 1.7 %copy.41 = bf16[8,8,2,4,2,512]{5,3,4,2,1,0:T(4,128)(2,1)} copy(bf16[8,8,2,4,2,512]{5,3,4,0,2,1:T(4,128)(2,1)S(1)} %get-tuple-element.5) | data formatting | bytes 2097152 | tf_op jit(solution)/shard_map/slice | solution.py:136
  7.8 7.2 %all-to-all-start.1 = ((bf16[8,8,2,4,2,512]{5,3,4,2,1,0:T(4,128)(2,1)}), bf16[8,8,2,4,2,512]{5,3,4,2,1,0:T(4,128)(2,1)S(1)}, u32[]{:S(2)}, u32[]{:S(2)}) async-start(bf16[8,8,2,4,2,512]{5,3,4,2,1,0:T(4,128)(2,1)} %copy.41), calls=%async_computation.1 | async-start | bytes 2097152 | tf_op jit(solution)/shard_map/all_to_all | solution.py:135
  16.1 0.7 fusion.5
  16.7 1.2 bitcast_multiply_fusion
  18.0 1.3 compare_and_fusion.2
  19.5 0.9 gather_fusion.1
  20.4 0.8 broadcast_select_fusion
  22.4 0.7 broadcast_in_dim.83
  23.2 0.7 broadcast_in_dim.76
  24.2 6.4 %iota_compare_fusion.1 = pred[64,4,128,128]{3,2,1,0:T(8,128)(4,1)} fusion(s32[64,4,128]{2,1,0:T(4,128)S(1)} %get-tuple-element.7), kind=kLoop, calls=%fused_computation.7 | loop fusion | flops 4194304 | bytes 4325376 | tf_op jit(solution)/shard_map/eq | solution.py:160
  31.5 0.6 gather_fusion.3
  32.2 1.7 %copy.35 = bf16[8,8,2,4,2,512]{5,3,4,2,1,0:T(4,128)(2,1)} copy(bf16[8,8,2,4,2,512]{5,3,4,0,2,1:T(4,128)(2,1)S(1)} %get-tuple-element.6) | data formatting | bytes 2097152 | tf_op jit(solution)/shard_map/slice | solution.py:136
  34.0 4.7 %iota_compare_fusion = pred[64,4,128,128]{3,2,1,0:T(8,128)(4,1)} fusion(s32[64,4,128]{2,1,0:T(4,128)S(1)} %get-tuple-element.8), kind=kLoop, calls=%fused_computation.6 | loop fusion | flops 4194304 | bytes 4325376 | tf_op jit(solution)/shard_map/eq | solution.py:161
  38.7 7.2 %all-to-all-start = ((bf16[8,8,2,4,2,512]{5,3,4,2,1,0:T(4,128)(2,1)}), bf16[8,8,2,4,2,512]{5,3,4,2,1,0:T(4,128)(2,1)S(1)}, u32[]{:S(2)}, u32[]{:S(2)}) async-start(bf16[8,8,2,4,2,512]{5,3,4,2,1,0:T(4,128)(2,1)} %copy.35), calls=%async_computation | async-start | bytes 2097152 | tf_op jit(solution)/shard_map/all_to_all | solution.py:135
  45.9 2.9 %copy.43.w_ref = f32[64,64,1]{2,1,0:T(8,128)} copy(f32[64,64,1]{0,1,2:T(8,128)S(1)} %bitcast.35) | data formatting | bytes 32768 | tf_op jit(solution)/shard_map/reshape | solution.py:165
  48.8 2.9 %copy.44.w_ref = f32[64,64,1]{2,1,0:T(8,128)} copy(f32[64,64,1]{0,1,2:T(8,128)S(1)} %bitcast.34) | data formatting | bytes 32768 | tf_op jit(solution)/shard_map/reshape | solution.py:165
  51.7 9.9 %add_convert_fusion.onehot_ref = bf16[64,8,128,128]{3,2,1,0:T(8,128)(2,1)} fusion(pred[64,4,128,128]{3,2,1,0:T(8,128)(4,1)} %iota_compare_fusion, pred[64,4,128,128]{3,2,1,0:T(8,128)(4,1)} %iota_compare_fusion.1), kind=kLoop, calls=%fused_computation.5 | loop fusion | flops 16777216 | bytes 25165824 | tf_op jit(solution)/shard_map/convert_element_type | solution.py:162
  61.7 2.1 %copy.42 = bf16[8,8,2,4,2,512]{5,4,3,2,1,0:T(2,128)(2,1)} copy(bf16[8,8,2,4,2,512]{5,3,4,2,0,1:T(4,128)(2,1)S(1)} %bitcast.30) | data formatting | bytes 2097152 | tf_op jit(solution)/shard_map/transpose | solution.py:138
  63.8 2.6 %reshape.220.loc_ref = bf16[8,64,1024]{2,1,0:T(8,128)(2,1)} reshape(bf16[8,8,2,4,2,512]{5,4,3,2,1,0:T(2,128)(2,1)} %copy.42) | data formatting | bytes 2097152 | tf_op jit(solution)/shard_map/reshape | solution.py:138
  66.4 1.2 copy.36
  67.6 1.5 %reshape.217.loc_ref = bf16[8,64,1024]{2,1,0:T(8,128)(2,1)} reshape(bf16[8,8,2,4,2,512]{5,4,3,2,1,0:T(2,128)(2,1)S(1)} %copy.36) | data formatting | bytes 2097152 | tf_op jit(solution)/shard_map/reshape | solution.py:138
  69.1 15.7 %shard_map.82.refs_0_ = f32[1,512,512]{2,1,0:T(8,128)} custom-call(s32[64]{0:T(128)} %star_ref.3, bf16[8,64,1024]{2,1,0:T(8,128)(2,1)} %reshape.220.loc_ref, bf16[64,8,128,128]{3,2,1,0:T(8,128)(2,1)} %add_convert_fusion.onehot_ref, f32[64,64,1]{2,1,0:T(8,128)} %copy.43.w_ref), custom_call_target="tpu_custom_call" | custom-call | tf_op jit(solution)/shard_map/pallas_call | solution.py:81
  84.8 16.0 %shard_map.83 = f32[1,512,512]{2,1,0:T(8,128)} custom-call(s32[64]{0:T(128)} %star_ref.3, bf16[8,64,1024]{2,1,0:T(8,128)(2,1)} %reshape.217.loc_ref, bf16[64,8,128,128]{3,2,1,0:T(8,128)(2,1)} %add_convert_fusion.onehot_ref, f32[64,64,1]{2,1,0:T(8,128)} %copy.44.w_ref, f32[1,512,512]{2,1,0:T(8,128)} %shard_map.82.refs_0_), custom_call_target="tpu_custom_call" | custom-call | tf_op jit(solution)/shard_map/pallas_call | solution.py:81
  100.8 1.6 %reshape.222 = f32[1,4,128,4,128]{4,3,2,1,0:T(4,128)S(1)} reshape(f32[1,512,512]{2,1,0:T(8,128)} %shard_map.83) | data formatting | bytes 2097152 | tf_op jit(solution)/shard_map/reshape | solution.py:168
  102.5 36.9 %all_to_all.15 = f32[16,1,128,128]{3,2,1,0:T(8,128)S(1)} all-to-all(f32[16,1,128,128]{3,2,1,0:T(8,128)S(1)} %bitcast.32), channel_id=1, replica_groups=mesh['ka'=16,'band'=8,'ga'=2] {'ka'}, dimensions={0} | all-to-all | bytes 2097152 | tf_op jit(solution)/shard_map/all_to_all | solution.py:170
  139.4 2.5 %collective-permute-start = (f32[1,128,128]{2,1,0:T(8,128)S(1)}, f32[1,128,128]{2,1,0:T(8,128)S(1)}, u32[]{:S(2)}, u32[]{:S(2)}) collective-permute-start(f32[1,128,128]{2,1,0:T(8,128)S(1)} %bitcast.36), channel_id=1, source_target_pairs={{0,0},{1,68},{2,136},{3,204},{4,64},{5,4},{6,128},{7,8},{8,192},{9... | collective-permute-start | bytes 196616 | tf_op jit(solution)/shard_map/ppermute | solution.py:172
  141.8 10.3 %collective-permute-done = f32[1,128,128]{2,1,0:T(8,128)S(1)} collective-permute-done((f32[1,128,128]{2,1,0:T(8,128)S(1)}, f32[1,128,128]{2,1,0:T(8,128)S(1)}, u32[]{:S(2)}, u32[]{:S(2)}) %collective-permute-start) | collective-permute-done | bytes 65568 | tf_op jit(solution)/shard_map/ppermute | solution.py:172
  152.2 0.6 copy.48
  (52 shorter events, 4.8 us)
Async XLA Ops:
  0.0 1.1 copy-start
  5.3 9.7 %copy-start.3 = (s32[64]{0:T(128)S(1)}, s32[64]{0:T(128)}, u32[]{:S(2)}) copy-start(s32[64]{0:T(128)} %star_ref.3) | copy-start | bytes 772
  5.4 9.7 %copy-start.6 = (s32[64]{0:T(128)S(1)}, s32[64]{0:T(128)}, u32[]{:S(2)}) copy-start(s32[64]{0:T(128)} %param.12) | copy-start | bytes 772
  5.4 13.9 %copy-start.2 = (s32[48,2048]{1,0:T(8,128)S(1)}, s32[48,2048]{1,0:T(8,128)}, u32[]{:S(2)}) copy-start(s32[48,2048]{1,0:T(8,128)} %param.13) | copy-start | bytes 1179652
  7.8 30.8 %all-to-all-start.1 = ((bf16[8,8,2,4,2,512]{5,3,4,2,1,0:T(4,128)(2,1)}), bf16[8,8,2,4,2,512]{5,3,4,2,1,0:T(4,128)(2,1)S(1)}, u32[]{:S(2)}, u32[]{:S(2)}) async-start(bf16[8,8,2,4,2,512]{5,3,4,2,1,0:T(4,128)(2,1)} %copy.41), calls=%async_computation.1 | async-start | bytes 2097152 | tf_op jit(solution)/shard_map/all_to_all | solution.py:135
  21.2 9.4 %copy-start.5 = (s32[64]{0:T(128)S(1)}, s32[64]{0:T(128)}, u32[]{:S(2)}) copy-start(s32[64]{0:T(128)} %get-tuple-element.13) | copy-start | bytes 772
  21.2 9.4 %copy-start.4 = (f32[8,256]{1,0:T(8,128)S(1)}, f32[8,256]{1,0:T(8,128)}, u32[]{:S(2)}) copy-start(f32[8,256]{1,0:T(8,128)} %param.10) | copy-start | bytes 24580
  21.2 10.2 %copy-start.1 = (f32[8,8]{1,0:T(8,128)S(1)}, f32[8,8]{1,0:T(8,128)}, u32[]{:S(2)}) copy-start(f32[8,8]{1,0:T(8,128)} %param.9) | copy-start | bytes 772
  22.4 11.5 %copy-start.7 = (s32[64]{0:T(128)S(1)}, s32[64]{0:T(128)}, u32[]{:S(2)}) copy-start(s32[64]{0:T(128)} %param.14) | copy-start | bytes 772
  38.7 27.7 %all-to-all-start = ((bf16[8,8,2,4,2,512]{5,3,4,2,1,0:T(4,128)(2,1)}), bf16[8,8,2,4,2,512]{5,3,4,2,1,0:T(4,128)(2,1)S(1)}, u32[]{:S(2)}, u32[]{:S(2)}) async-start(bf16[8,8,2,4,2,512]{5,3,4,2,1,0:T(4,128)(2,1)} %copy.35), calls=%async_computation | async-start | bytes 2097152 | tf_op jit(solution)/shard_map/all_to_all | solution.py:135
  139.4 12.8 %collective-permute-start = (f32[1,128,128]{2,1,0:T(8,128)S(1)}, f32[1,128,128]{2,1,0:T(8,128)S(1)}, u32[]{:S(2)}, u32[]{:S(2)}) collective-permute-start(f32[1,128,128]{2,1,0:T(8,128)S(1)} %bitcast.36), channel_id=1, source_target_pairs={{0,0},{1,68},{2,136},{3,204},{4,64},{5,4},{6,128},{7,8},{8,192},{9... | collective-permute-start | bytes 196616 | tf_op jit(solution)/shard_map/ppermute | solution.py:172

commit v7 on v5

--- a/solution.py
+++ b/solution.py
@@ -20,25 +20,26 @@
     tuple((PAIR[j][LOCAL[j][g][0]], PAIR[j][LOCAL[j][g][1]]) for g in range(2))
     for j in range(len(PAIR))
 )
-KB = 4
+KB = 8
 
 
 freq_step = 2.0
 
 
-def chi_kernel(star_ref, loc_ref, onehot_ref, w_ref, out_ref):
+def chi_kernel(star_ref, loc_ref, onehot_ref, w_ref, out_ref, acc_ref):
     step = pl.program_id(0)
 
     @pl.when(step == 0)
     def _():
-        out_ref[...] = jnp.zeros_like(out_ref)
+        acc_ref[...] = jnp.zeros_like(acc_ref)
 
     nt = (((1,), (1,)), ((), ()))
     subs = BW // GB
     lhs_parts = []
     rhs_parts = [[] for _ in range(NF)]
     for t in range(KB):
-        x = loc_ref[star_ref[step * KB + t]]
+        x = loc_ref[:, star_ref[step * KB + t]]
+        x = x.reshape(x.shape[0] * x.shape[1], x.shape[2])
         row_parts = []
         for q in range(subs):
             row_parts.append(
@@ -66,23 +67,34 @@
     lhs = jnp.concatenate(lhs_parts, axis=1)
     for f in range(NF):
         rhs = jnp.concatenate(rhs_parts[f], axis=0)
-        out_ref[f] += jnp.dot(lhs, rhs, preferred_element_type=jnp.float32)
+        acc_ref[f] += jnp.dot(lhs, rhs, preferred_element_type=jnp.float32)
+
+    @pl.when(step == pl.num_programs(0) - 1)
+    def _():
+        for f in range(NF):
+            for rho in range(subs):
+                for gamma in range(subs):
+                    out_ref[rho * subs + gamma, f] = acc_ref[
+                        f, rho * GB : (rho + 1) * GB, gamma * GB : (gamma + 1) * GB
+                    ]
 
 
 def chi_block(star_map, loc, onehot, weight_c):
-    rows = loc.shape[1]
+    rows = loc.shape[0] * loc.shape[2]
+    pieces = (BW // GB) ** 2
     return pl.pallas_call(
         chi_kernel,
-        out_shape=jax.ShapeDtypeStruct((NF, BW, BW), jnp.float32),
+        out_shape=jax.ShapeDtypeStruct((pieces, NF, GB, GB), jnp.float32),
         grid_spec=pltpu.PrefetchScalarGridSpec(
             num_scalar_prefetch=1,
             grid=(KF // KB,),
             in_specs=[
-                pl.BlockSpec((KI, rows, 2 * BW), lambda st, sm: (0, 0, 0)),
+                pl.BlockSpec(loc.shape, lambda st, sm: (0, 0, 0, 0)),
                 pl.BlockSpec((KB, 2 * BW // GB, GB, GB), lambda st, sm: (st, 0, 0, 0)),
                 pl.BlockSpec((KB, rows, NF), lambda st, sm: (st, 0, 0)),
             ],
-            out_specs=pl.BlockSpec((NF, BW, BW), lambda st, sm: (0, 0, 0)),
+            out_specs=pl.BlockSpec((pieces, NF, GB, GB), lambda st, sm: (0, 0, 0, 0)),
+            scratch_shapes=[pltpu.VMEM((NF, BW, BW), jnp.float32)],
         ),
         compiler_params=pltpu.CompilerParams(dimension_semantics=("arbitrary",)),
     )(star_map, loc, onehot, weight_c)
@@ -122,7 +134,7 @@
     send = jnp.moveaxis(send, 3, 0)
     recv = lax.all_to_all(send, "band", 0, 0, tiled=False)
     c_loc = band_count * cond_piece
-    loc = jnp.moveaxis(recv, 0, 1).reshape(KI, c_loc * NV, 2 * BW)
+    loc = recv.reshape(band_count, KI, cond_piece * NV, 2 * BW)
 
     c_base = ka_index * c_loc
     cond_grp = lax.dynamic_slice_in_dim(conduction_energy, c_base, c_loc, axis=1)
@@ -147,10 +159,8 @@
     row_side = local[:, :subs, :, None] == slot[None, None, None, :]
     col_side = local[:, subs:, None, :] == slot[None, None, :, None]
     onehot = jnp.concatenate([row_side, col_side], axis=1).astype(jnp.bfloat16)
-    partial_value = chi_block(star_map, loc, onehot, weight_c)
+    pieces = chi_block(star_map, loc, onehot, weight_c)
 
-    pieces = partial_value.reshape(NF, subs, GB, subs, GB).transpose(1, 3, 0, 2, 4)
-    pieces = pieces.reshape(subs * subs, NF, GB, GB)
     got = lax.all_to_all(pieces, "ka", 0, 0, tiled=False)
     slab = got.sum(axis=0)
     return lax.ppermute(

time: 124 us -> 121 us (0.976)
  local copies, waits for them, and re-layouts: 20.5 us -> 18.4 us
  Pallas kernels: 24.5 us -> 23.2 us
    reshape x2 -> x0, local copies, waits for them, and re-layouts: 1.68 us -> none  [on_device(): partial_value.reshape(NF, subs, GB, subs, GB).transpose(1, 3, 0, 2, 4)]
    transpose x1 -> x0, local copies, waits for them, and re-layouts: 1.64 us -> none  [on_device(): loc = jnp.moveaxis(recv, 0, 1).reshape(KI, c_loc * NV, 2 * BW)]
    unnamed x19 -> x21, local copies, waits for them, and re-layouts: 0.86 us -> 2.19 us
    pallas_call x1, Pallas kernels: 24.5 us -> 23.2 us  [chi_block(): pl.pallas_call(chi_kernel, out_shape=jax.ShapeDtypeStruct((pieces, NF, GB...]
  transfers between devices with their start and end apart: 2 -> 2, of which waited for: 1 -> 1; matrix products, arithmetic and copies ran while one was open for 25% -> 26% of each run, Pallas kernels for 0% -> 0%
where the time goes in v7:
time: 121 us; the launch traced here: 120 us
  blocking collectives  37.2 us (31%)
  Pallas kernels  23.2 us (19%)
  other arithmetic  21.3 us (18%)
  local copies, waits for them, and re-layouts  18.4 us (15%)
  starting transfers between devices  10 us (8%)
  waiting for transfers between devices  9.92 us (8%)
    all_to_all x1, blocking collectives, on_device(): got = lax.all_to_all(pieces, 'ka', 0, 0, tiled=False)  37.2 us
    pallas_call x1, Pallas kernels, chi_block(): pl.pallas_call(chi_kernel, out_shape=jax.ShapeDtypeStruct((pieces, NF, GB...  23.2 us
    ppermute x1, waiting for transfers between devices, on_device(): lax.ppermute(slab, ('ka', 'band', 'ga'), slab_perm(ka_count, band_count,...  9.92 us
    all_to_all x1, starting transfers between devices, on_device(): recv = lax.all_to_all(send, 'band', 0, 0, tiled=False)  7.18 us
    convert_element_type x1, other arithmetic, on_device(): onehot = jnp.concatenate([row_side, col_side], axis=1).astype(jnp.bfloat16)  6.44 us
    eq x1, other arithmetic, on_device(): row_side = local[:, :subs, :, None] == slot[None, None, None, :]  6.42 us
    mul x1, local copies, waits for them, and re-layouts, on_device(): weight = 4.0 / KF * diff[None] / (diff[None] * diff[None] + omega_sq) * mask  4.52 us
    gather x2, local copies, waits for them, and re-layouts, on_device(): send = jnp.take(blocked, blocks[:, ga_index].reshape(-1), axis=3)  3.83 us
  transfers between devices with their start and end apart: 2, of which 1 were waited for; matrix products, arithmetic and copies ran while one was open for 26% of the time, Pallas kernels for 0%

profile of v7, /device:TPU:22, one launch (start us, length us, event | category | flops | bytes accessed | tf_op | source)
XLA Modules:
  0.0 120.3 jit_solution(5752579400879823522)
XLA Ops:
  0.0 0.8 constant_dynamic-slice_fusion.2
  0.9 0.2 copy-done
  1.1 2.0 %gather_fusion = bf16[16,8,2,8,512]{4,3,2,1,0:T(8,128)(2,1)} fusion(bf16[8,2,8,4,512]{4,2,3,1,0:T(8,128)(2,1)S(1)} %bitcast.21, s32[1024]{0:T(1024)S(1)} %pad_clamp_fusion.3), kind=kCustom, calls=%fused_computation | custom fusion | bytes 4194368 | tf_op jit(solution)/shard_map/jit(_take)/gather | solution.py:132
  3.1 1.8 %copy.28 = bf16[8,2,8,16,512]{4,2,3,1,0:T(8,128)(2,1)S(1)} copy(bf16[8,2,8,16,512]{4,2,1,0,3:T(8,128)(2,1)} %bitcast.23) | data formatting | bytes 4194304 | tf_op jit(solution)/shard_map/jit(_take)/gather | solution.py:132
  5.1 0.3 select_bitcast_fusion
  5.4 1.5 %copy.29 = bf16[8,8,2,8,2,512]{5,3,4,2,1,0:T(8,128)(2,1)} copy(bf16[8,8,2,8,2,512]{5,3,4,0,2,1:T(8,128)(2,1)S(1)} %select_bitcast_fusion) | data formatting | bytes 4194304 | tf_op jit(solution)/shard_map/transpose | solution.py:134
  6.9 7.2 %all-to-all-start = ((bf16[8,8,2,8,2,512]{5,3,4,2,1,0:T(8,128)(2,1)}), bf16[8,8,2,8,2,512]{5,3,4,2,1,0:T(8,128)(2,1)S(1)}, u32[]{:S(2)}, u32[]{:S(2)}) async-start(bf16[8,8,2,8,2,512]{5,3,4,2,1,0:T(8,128)(2,1)} %copy.29), calls=%async_computation | async-start | bytes 4194304 | tf_op jit(solution)/shard_map/all_to_all | solution.py:135
  14.1 0.5 compare_select_fusion.1
  14.6 0.6 compare_and_fusion
  15.2 0.7 fusion.6
  15.9 1.2 %bitcast_multiply_fusion = s32[2]{0:T(128)} fusion(s32[8,2,2]{2,1,0:T(2,128)} %constant.114.clone, s32[]{:T(128)S(6)} %select_n.99, s32[]{:T(128)S(6)} %select_n.95), kind=kLoop, calls=%fused_computation.41 | loop fusion | flops 2 | bytes 24 | tf_op jit(solution)/shard_map/mul | solution.py:156
  17.1 1.2 compare_and_fusion.2
  18.3 0.3 reshape.236
  18.6 0.9 gather_fusion.1
  19.5 0.8 broadcast_select_fusion
  20.6 0.6 gather_fusion.2
  21.1 0.2 copy.31
  21.3 0.2 gather.28
  21.6 0.7 broadcast_in_dim.83
  22.3 0.7 broadcast_in_dim.76
  23.3 6.4 %iota_compare_fusion.1 = pred[64,4,128,128]{3,2,1,0:T(8,128)(4,1)} fusion(s32[64,4,128]{2,1,0:T(4,128)S(1)} %get-tuple-element.5), kind=kLoop, calls=%fused_computation.7 | loop fusion | flops 4194304 | bytes 4325376 | tf_op jit(solution)/shard_map/eq | solution.py:159
  29.8 0.6 gather_fusion.4
  30.5 0.6 gather_fusion.3
  31.4 4.5 %copy.34.w_ref = f32[64,128,1]{2,1,0:T(8,128)} copy(f32[64,128,1]{0,1,2:T(8,128)S(1)} %fusion.2) | data formatting | bytes 65536 | tf_op jit(solution)/shard_map/mul | solution.py:148
  35.9 2.7 %iota_compare_fusion = pred[64,4,128,128]{3,2,1,0:T(8,128)(4,1)S(1)} fusion(s32[64,4,128]{2,1,0:T(4,128)S(1)} %get-tuple-element.6), kind=kLoop, calls=%fused_computation.6 | loop fusion | flops 4194304 | bytes 4325376 | tf_op jit(solution)/shard_map/eq | solution.py:160
  38.6 6.4 %add_convert_fusion.onehot_ref = bf16[64,8,128,128]{3,2,1,0:T(8,128)(2,1)} fusion(pred[64,4,128,128]{3,2,1,0:T(8,128)(4,1)S(1)} %iota_compare_fusion, pred[64,4,128,128]{3,2,1,0:T(8,128)(4,1)S(1)} %copy-done.2), kind=kLoop, calls=%fused_computation.5 | loop fusion | flops 16777216 | bytes 25165824 | tf_op jit(solution)/shard_map/convert_element_type | solution.py:161
  45.0 1.3 %copy-done.3 = bf16[8,8,2,8,2,512]{5,3,4,2,1,0:T(8,128)(2,1)} copy-done((bf16[8,8,2,8,2,512]{5,3,4,2,1,0:T(8,128)(2,1)}, bf16[8,8,2,8,2,512]{5,3,4,2,1,0:T(8,128)(2,1)S(1)}, u32[]{:S(2)}) %copy-start.3) | copy-done | bytes 2097176
  46.4 23.2 %shard_map.82 = f32[16,1,128,128]{3,2,1,0:T(8,128)} custom-call(s32[64]{0:T(128)} %star_ref.1, bf16[8,8,16,1024]{3,2,1,0:T(8,128)(2,1)} %bitcast.24, bf16[64,8,128,128]{3,2,1,0:T(8,128)(2,1)} %add_convert_fusion.onehot_ref, f32[64,128,1]{2,1,0:T(8,128)} %copy.34.w_ref), custom_call_target="tpu_custom_call" | custom-call | tf_op jit(solution)/shard_map/pallas_call | solution.py:85
  69.6 37.2 %all_to_all.10 = f32[16,1,128,128]{3,2,1,0:T(8,128)S(1)} all-to-all(f32[16,1,128,128]{3,2,1,0:T(8,128)} %shard_map.82), channel_id=1, replica_groups=mesh['ka'=16,'band'=8,'ga'=2] {'ka'}, dimensions={0} | all-to-all | bytes 2097152 | tf_op jit(solution)/shard_map/all_to_all | solution.py:164
  106.9 2.9 %collective-permute-start = (f32[1,128,128]{2,1,0:T(8,128)S(1)}, f32[1,128,128]{2,1,0:T(8,128)S(1)}, u32[]{:S(2)}, u32[]{:S(2)}) collective-permute-start(f32[1,128,128]{2,1,0:T(8,128)S(1)} %bitcast.26), channel_id=1, source_target_pairs={{0,0},{1,68},{2,136},{3,204},{4,64},{5,4},{6,128},{7,8},{8,192},{9... | collective-permute-start | bytes 196616 | tf_op jit(solution)/shard_map/ppermute | solution.py:166
  109.7 9.9 %collective-permute-done = f32[1,128,128]{2,1,0:T(8,128)S(1)} collective-permute-done((f32[1,128,128]{2,1,0:T(8,128)S(1)}, f32[1,128,128]{2,1,0:T(8,128)S(1)}, u32[]{:S(2)}, u32[]{:S(2)}) %collective-permute-start) | collective-permute-done | bytes 65568 | tf_op jit(solution)/shard_map/ppermute | solution.py:166
  119.7 0.6 copy.36
  (43 shorter events, 1.4 us)
Async XLA Ops:
  0.0 1.1 copy-start
  5.4 8.7 %copy-start.5 = (s32[64]{0:T(128)S(1)}, s32[64]{0:T(128)}, u32[]{:S(2)}) copy-start(s32[64]{0:T(128)} %star_ref.1) | copy-start | bytes 772
  5.4 8.7 %copy-start.8 = (s32[64]{0:T(128)S(1)}, s32[64]{0:T(128)}, u32[]{:S(2)}) copy-start(s32[64]{0:T(128)} %param.12) | copy-start | bytes 772
  5.4 13.0 %copy-start.4 = (s32[48,2048]{1,0:T(8,128)S(1)}, s32[48,2048]{1,0:T(8,128)}, u32[]{:S(2)}) copy-start(s32[48,2048]{1,0:T(8,128)} %param.13) | copy-start | bytes 1179652
  6.9 38.1 %all-to-all-start = ((bf16[8,8,2,8,2,512]{5,3,4,2,1,0:T(8,128)(2,1)}), bf16[8,8,2,8,2,512]{5,3,4,2,1,0:T(8,128)(2,1)S(1)}, u32[]{:S(2)}, u32[]{:S(2)}) async-start(bf16[8,8,2,8,2,512]{5,3,4,2,1,0:T(8,128)(2,1)} %copy.29), calls=%async_computation | async-start | bytes 4194304 | tf_op jit(solution)/shard_map/all_to_all | solution.py:135
  20.3 9.3 %copy-start.7 = (s32[64]{0:T(128)S(1)}, s32[64]{0:T(128)}, u32[]{:S(2)}) copy-start(s32[64]{0:T(128)} %get-tuple-element.9) | copy-start | bytes 772
  20.3 9.3 %copy-start.6 = (f32[8,256]{1,0:T(8,128)S(1)}, f32[8,256]{1,0:T(8,128)}, u32[]{:S(2)}) copy-start(f32[8,256]{1,0:T(8,128)} %param.10) | copy-start | bytes 24580
  20.4 10.2 %copy-start.1 = (f32[8,8]{1,0:T(8,128)S(1)}, f32[8,8]{1,0:T(8,128)}, u32[]{:S(2)}) copy-start(f32[8,8]{1,0:T(8,128)} %param.9) | copy-start | bytes 772
  20.4 10.9 %copy-start.9 = (s32[64]{0:T(128)S(1)}, s32[64]{0:T(128)}, u32[]{:S(2)}) copy-start(s32[64]{0:T(128)} %param.14) | copy-start | bytes 772
  35.9 2.7 %copy-start.2 = (pred[64,4,128,128]{3,2,1,0:T(8,128)(4,1)S(1)}, pred[64,4,128,128]{3,2,1,0:T(8,128)(4,1)}, u32[]{:S(2)}) copy-start(pred[64,4,128,128]{3,2,1,0:T(8,128)(4,1)} %iota_compare_fusion.1) | copy-start | bytes 12582916
  45.0 1.3 %copy-start.3 = (bf16[8,8,2,8,2,512]{5,3,4,2,1,0:T(8,128)(2,1)}, bf16[8,8,2,8,2,512]{5,3,4,2,1,0:T(8,128)(2,1)S(1)}, u32[]{:S(2)}) copy-start(bf16[8,8,2,8,2,512]{5,3,4,2,1,0:T(8,128)(2,1)S(1)} %all-to-all-done) | copy-start | bytes 6291460
  106.9 12.8 %collective-permute-start = (f32[1,128,128]{2,1,0:T(8,128)S(1)}, f32[1,128,128]{2,1,0:T(8,128)S(1)}, u32[]{:S(2)}, u32[]{:S(2)}) collective-permute-start(f32[1,128,128]{2,1,0:T(8,128)S(1)} %bitcast.26), channel_id=1, source_target_pairs={{0,0},{1,68},{2,136},{3,204},{4,64},{5,4},{6,128},{7,8},{8,192},{9... | collective-permute-start | bytes 196616 | tf_op jit(solution)/shard_map/ppermute | solution.py:166

commit v8 on v7

--- a/solution.py
+++ b/solution.py
@@ -26,7 +26,7 @@
 freq_step = 2.0
 
 
-def chi_kernel(star_ref, loc_ref, onehot_ref, w_ref, out_ref, acc_ref):
+def chi_kernel(star_ref, sel_ref, loc_ref, onehot_ref, w_ref, out_ref, acc_ref):
     step = pl.program_id(0)
 
     @pl.when(step == 0)
@@ -40,11 +40,13 @@
     for t in range(KB):
         x = loc_ref[:, star_ref[step * KB + t]]
         x = x.reshape(x.shape[0] * x.shape[1], x.shape[2])
+        x_row = jnp.where(sel_ref[0] == 0, x[:, :BW], x[:, BW:])
+        x_col = jnp.where(sel_ref[1] == 0, x[:, :BW], x[:, BW:])
         row_parts = []
         for q in range(subs):
             row_parts.append(
                 lax.dot_general(
-                    onehot_ref[t, q], x[:, q * GB : (q + 1) * GB], nt,
+                    onehot_ref[t, q], x_row[:, q * GB : (q + 1) * GB], nt,
                     preferred_element_type=jnp.float32,
                 )
             )
@@ -53,7 +55,7 @@
         for q in range(subs, 2 * subs):
             col_parts.append(
                 jnp.dot(
-                    x[:, q * GB : (q + 1) * GB], onehot_ref[t, q],
+                    x_col[:, (q - subs) * GB : (q - subs + 1) * GB], onehot_ref[t, q],
                     preferred_element_type=jnp.float32,
                 )
             )
@@ -79,25 +81,25 @@
                     ]
 
 
-def chi_block(star_map, loc, onehot, weight_c):
+def chi_block(star_map, sel, loc, onehot, weight_c):
     rows = loc.shape[0] * loc.shape[2]
     pieces = (BW // GB) ** 2
     return pl.pallas_call(
         chi_kernel,
         out_shape=jax.ShapeDtypeStruct((pieces, NF, GB, GB), jnp.float32),
         grid_spec=pltpu.PrefetchScalarGridSpec(
-            num_scalar_prefetch=1,
+            num_scalar_prefetch=2,
             grid=(KF // KB,),
             in_specs=[
-                pl.BlockSpec(loc.shape, lambda st, sm: (0, 0, 0, 0)),
-                pl.BlockSpec((KB, 2 * BW // GB, GB, GB), lambda st, sm: (st, 0, 0, 0)),
-                pl.BlockSpec((KB, rows, NF), lambda st, sm: (st, 0, 0)),
+                pl.BlockSpec(loc.shape, lambda st, sm, se: (0, 0, 0, 0)),
+                pl.BlockSpec((KB, 2 * BW // GB, GB, GB), lambda st, sm, se: (st, 0, 0, 0)),
+                pl.BlockSpec((KB, rows, NF), lambda st, sm, se: (st, 0, 0)),
             ],
-            out_specs=pl.BlockSpec((pieces, NF, GB, GB), lambda st, sm: (0, 0, 0, 0)),
+            out_specs=pl.BlockSpec((pieces, NF, GB, GB), lambda st, sm, se: (0, 0, 0, 0)),
             scratch_shapes=[pltpu.VMEM((NF, BW, BW), jnp.float32)],
         ),
         compiler_params=pltpu.CompilerParams(dimension_semantics=("arbitrary",)),
-    )(star_map, loc, onehot, weight_c)
+    )(star_map, sel, loc, onehot, weight_c)
 
 
 def slab_perm(ka_count, band_count, ga_count):
@@ -129,9 +131,9 @@
     blocks = jnp.asarray(BLOCKS, jnp.int32)
 
     blocked = pair_density.reshape(KI, cond_piece, NV, NB, BW)
-    send = jnp.take(blocked, blocks[:, ga_index].reshape(-1), axis=3)
-    send = send.reshape(KI, cond_piece, NV, band_count, 2, BW)
-    send = jnp.moveaxis(send, 3, 0)
+    send = jnp.stack(
+        [jnp.stack([blocked[:, :, :, a], blocked[:, :, :, b]], axis=3) for a, b in PAIR]
+    )
     recv = lax.all_to_all(send, "band", 0, 0, tiled=False)
     c_loc = band_count * cond_piece
     loc = recv.reshape(band_count, KI, cond_piece * NV, 2 * BW)
@@ -159,7 +161,8 @@
     row_side = local[:, :subs, :, None] == slot[None, None, None, :]
     col_side = local[:, subs:, None, :] == slot[None, None, :, None]
     onehot = jnp.concatenate([row_side, col_side], axis=1).astype(jnp.bfloat16)
-    pieces = chi_block(star_map, loc, onehot, weight_c)
+    sel = jnp.asarray(LOCAL, jnp.int32)[band_index, ga_index]
+    pieces = chi_block(star_map, sel, loc, onehot, weight_c)
 
     got = lax.all_to_all(pieces, "ka", 0, 0, tiled=False)
     slab = got.sum(axis=0)

time: 121 us -> 121 us (level)
    unnamed x21 -> x23, local copies, waits for them, and re-layouts: 2.19 us -> 6.89 us
    gather x2 -> x0, local copies, waits for them, and re-layouts: 3.83 us -> none  [on_device(): send = jnp.take(blocked, blocks[:, ga_index].reshape(-1), axis=3)]
    unnamed x0 -> x3, other arithmetic: none -> 2.2 us
    transpose x1 -> x0, local copies, waits for them, and re-layouts: 1.53 us -> none  [on_device(): send = jnp.moveaxis(send, 3, 0)]
  transfers between devices with their start and end apart: 2 -> 2, of which waited for: 1 -> 1; matrix products, arithmetic and copies ran while one was open for 26% -> 23% of each run, Pallas kernels for 0% -> 0%
where the time goes in v8:
time: 121 us; the launch traced here: 120 us
  blocking collectives  37.2 us (31%)
  Pallas kernels  23.6 us (20%)
  other arithmetic  20.4 us (17%)
  local copies, waits for them, and re-layouts  18.5 us (15%)
  starting transfers between devices  10.9 us (9%)
  waiting for transfers between devices  9.2 us (8%)
    all_to_all x1, blocking collectives, on_device(): got = lax.all_to_all(pieces, 'ka', 0, 0, tiled=False)  37.2 us
    pallas_call x1, Pallas kernels, chi_block(): pl.pallas_call(chi_kernel, out_shape=jax.ShapeDtypeStruct((pieces, NF, GB...  23.6 us
    ppermute x1, waiting for transfers between devices, on_device(): lax.ppermute(slab, ('ka', 'band', 'ga'), slab_perm(ka_count, band_count,...  9.2 us
    all_to_all x1, starting transfers between devices, on_device(): recv = lax.all_to_all(send, 'band', 0, 0, tiled=False)  7.31 us
    unnamed x23, local copies, waits for them, and re-layouts  6.89 us
    convert_element_type x1, other arithmetic, on_device(): onehot = jnp.concatenate([row_side, col_side], axis=1).astype(jnp.bfloat16)  6.43 us
    eq x1, other arithmetic, on_device(): row_side = local[:, :subs, :, None] == slot[None, None, None, :]  6.41 us
    mul x1, local copies, waits for them, and re-layouts, on_device(): weight = 4.0 / KF * diff[None] / (diff[None] * diff[None] + omega_sq) * mask  4.53 us
  transfers between devices with their start and end apart: 2, of which 1 were waited for; matrix products, arithmetic and copies ran while one was open for 23% of the time, Pallas kernels for 0%

profile of v8, /device:TPU:22, one launch (start us, length us, event | category | flops | bytes accessed | tf_op | source)
XLA Modules:
  0.0 120.0 jit_solution(5349763742733469234)
XLA Ops:
  0.0 1.7 %fusion.7 = bf16[8,8,2,8,2,512]{5,3,4,2,1,0:T(8,128)(2,1)} fusion(bf16[8,2,8,4,512]{4,2,3,1,0:T(8,128)(2,1)} %bitcast.44), kind=kLoop, calls=%fused_computation.22 | loop fusion | bytes 524288
  1.7 1.1 fusion.18
  2.9 1.7 %fusion.9 = bf16[8,8,2,8,2,512]{5,3,4,2,1,0:T(8,128)(2,1)} fusion(bf16[8,8,2,8,2,512]{5,3,4,2,1,0:T(8,128)(2,1)} %fusion.7, bf16[8,2,8,4,512]{4,2,3,1,0:T(8,128)(2,1)} %bitcast.46), kind=kLoop, calls=%fused_computation.24 | loop fusion | bytes 524288
  4.6 0.7 fusion.8
  5.3 0.7 fusion.3
  6.0 0.7 fusion.5
  6.8 0.7 fusion.6
  7.5 0.7 fusion.1
  8.2 0.7 fusion.10
  9.0 7.3 %all-to-all-start = ((bf16[8,8,2,8,2,512]{5,3,4,2,1,0:T(8,128)(2,1)}), bf16[8,8,2,8,2,512]{5,3,4,2,1,0:T(8,128)(2,1)S(1)}, u32[]{:S(2)}, u32[]{:S(2)}) async-start(bf16[8,8,2,8,2,512]{5,3,4,2,1,0:T(8,128)(2,1)} %fusion.10), calls=%async_computation | async-start | bytes 4194304 | tf_op jit(solution)/shard_map/all_to_all | solution.py:137
  16.3 0.7 fusion.17
  17.0 0.7 bitcast_multiply_fusion
  17.7 0.7 compare_and_fusion.2
  18.4 0.3 reshape.198
  18.7 0.9 gather_fusion
  19.6 0.2 broadcast_select_fusion
  19.9 0.6 gather_fusion.1
  20.5 0.2 copy.14
  20.7 0.2 gather.20
  21.4 6.4 %iota_compare_fusion.1 = pred[64,4,128,128]{3,2,1,0:T(8,128)(4,1)} fusion(s32[64,4,128]{2,1,0:T(4,128)S(1)} %get-tuple-element.9), kind=kLoop, calls=%fused_computation.6 | loop fusion | flops 4194304 | bytes 4325376 | tf_op jit(solution)/shard_map/eq | solution.py:161
  27.8 1.2 fusion.14.sel_ref
  29.1 0.6 gather_fusion.3
  29.9 0.6 gather_fusion.2
  30.7 4.5 %copy.17.w_ref = f32[64,128,1]{2,1,0:T(8,128)} copy(f32[64,128,1]{0,1,2:T(8,128)S(1)} %fusion.13) | data formatting | bytes 65536 | tf_op jit(solution)/shard_map/mul | solution.py:150
  35.3 2.7 %iota_compare_fusion = pred[64,4,128,128]{3,2,1,0:T(8,128)(4,1)S(1)} fusion(s32[64,4,128]{2,1,0:T(4,128)S(1)} %get-tuple-element.10), kind=kLoop, calls=%fused_computation.5 | loop fusion | flops 4194304 | bytes 4325376 | tf_op jit(solution)/shard_map/eq | solution.py:162
  38.0 6.4 %add_convert_fusion.onehot_ref = bf16[64,8,128,128]{3,2,1,0:T(8,128)(2,1)} fusion(pred[64,4,128,128]{3,2,1,0:T(8,128)(4,1)S(1)} %iota_compare_fusion, pred[64,4,128,128]{3,2,1,0:T(8,128)(4,1)S(1)} %copy-done.2), kind=kLoop, calls=%fused_computation.4 | loop fusion | flops 16777216 | bytes 25165824 | tf_op jit(solution)/shard_map/convert_element_type | solution.py:163
  44.4 1.3 %copy-done.3 = bf16[8,8,2,8,2,512]{5,3,4,2,1,0:T(8,128)(2,1)} copy-done((bf16[8,8,2,8,2,512]{5,3,4,2,1,0:T(8,128)(2,1)}, bf16[8,8,2,8,2,512]{5,3,4,2,1,0:T(8,128)(2,1)S(1)}, u32[]{:S(2)}) %copy-start.3) | copy-done | bytes 2097176
  45.7 23.6 %shard_map.91 = f32[16,1,128,128]{3,2,1,0:T(8,128)} custom-call(s32[64]{0:T(128)} %star_ref.1, s32[2]{0:T(128)} %fusion.14.sel_ref, bf16[8,8,16,1024]{3,2,1,0:T(8,128)(2,1)} %bitcast.43, bf16[64,8,128,128]{3,2,1,0:T(8,128)(2,1)} %add_convert_fusion.onehot_ref, f32[64,128,1]{2,1,0:T(8,128)} %copy.17.w_ref), custom_call_target="tpu_custom_call" | custom-call | tf_op jit(solution)/shard_map/pallas_call | solution.py:87
  69.3 37.2 %all_to_all.10 = f32[16,1,128,128]{3,2,1,0:T(8,128)S(1)} all-to-all(f32[16,1,128,128]{3,2,1,0:T(8,128)} %shard_map.91), channel_id=1, replica_groups=mesh['ka'=16,'band'=8,'ga'=2] {'ka'}, dimensions={0} | all-to-all | bytes 2097152 | tf_op jit(solution)/shard_map/all_to_all | solution.py:167
  106.6 3.6 %collective-permute-start = (f32[1,128,128]{2,1,0:T(8,128)S(1)}, f32[1,128,128]{2,1,0:T(8,128)S(1)}, u32[]{:S(2)}, u32[]{:S(2)}) collective-permute-start(f32[1,128,128]{2,1,0:T(8,128)S(1)} %bitcast.51), channel_id=1, source_target_pairs={{0,0},{1,68},{2,136},{3,204},{4,64},{5,4},{6,128},{7,8},{8,192},{9... | collective-permute-start | bytes 196616 | tf_op jit(solution)/shard_map/ppermute | solution.py:169
  110.2 9.2 %collective-permute-done = f32[1,128,128]{2,1,0:T(8,128)S(1)} collective-permute-done((f32[1,128,128]{2,1,0:T(8,128)S(1)}, f32[1,128,128]{2,1,0:T(8,128)S(1)}, u32[]{:S(2)}, u32[]{:S(2)}) %collective-permute-start) | collective-permute-done | bytes 65568 | tf_op jit(solution)/shard_map/ppermute | solution.py:169
  119.4 0.6 copy.26
  (40 shorter events, 1.2 us)
Async XLA Ops:
  0.0 29.0 %copy-start = (f32[8,256]{1,0:T(8,128)S(1)}, f32[8,256]{1,0:T(8,128)}, u32[]{:S(2)}) copy-start(f32[8,256]{1,0:T(8,128)} %param.11) | copy-start | bytes 24580
  0.0 4.6 %copy-start.4 = (bf16[8,2,8,2048]{3,2,1,0:T(8,128)(2,1)S(1)}, bf16[8,2,8,2048]{3,2,1,0:T(8,128)(2,1)}, u32[]{:S(2)}) copy-start(bf16[8,2,8,2048]{3,2,1,0:T(8,128)(2,1)} %param.9) | copy-start | bytes 1572868
  9.0 7.3 %copy-start.6 = (s32[64]{0:T(128)S(1)}, s32[64]{0:T(128)}, u32[]{:S(2)}) copy-start(s32[64]{0:T(128)} %star_ref.1) | copy-start | bytes 772
  9.0 7.3 %copy-start.7 = (s32[64]{0:T(128)S(1)}, s32[64]{0:T(128)}, u32[]{:S(2)}) copy-start(s32[64]{0:T(128)} %param.13) | copy-start | bytes 772
  9.0 9.5 %copy-start.5 = (s32[48,2048]{1,0:T(8,128)S(1)}, s32[48,2048]{1,0:T(8,128)}, u32[]{:S(2)}) copy-start(s32[48,2048]{1,0:T(8,128)} %param.14) | copy-start | bytes 1179652
  9.0 35.4 %all-to-all-start = ((bf16[8,8,2,8,2,512]{5,3,4,2,1,0:T(8,128)(2,1)}), bf16[8,8,2,8,2,512]{5,3,4,2,1,0:T(8,128)(2,1)S(1)}, u32[]{:S(2)}, u32[]{:S(2)}) async-start(bf16[8,8,2,8,2,512]{5,3,4,2,1,0:T(8,128)(2,1)} %fusion.10), calls=%async_computation | async-start | bytes 4194304 | tf_op jit(solution)/shard_map/all_to_all | solution.py:137
  21.4 8.5 %copy-start.1 = (f32[8,8]{1,0:T(8,128)S(1)}, f32[8,8]{1,0:T(8,128)}, u32[]{:S(2)}) copy-start(f32[8,8]{1,0:T(8,128)} %param.10) | copy-start | bytes 772
  21.4 9.2 %copy-start.8 = (s32[64]{0:T(128)S(1)}, s32[64]{0:T(128)}, u32[]{:S(2)}) copy-start(s32[64]{0:T(128)} %param.15) | copy-start | bytes 772
  35.3 2.7 %copy-start.2 = (pred[64,4,128,128]{3,2,1,0:T(8,128)(4,1)S(1)}, pred[64,4,128,128]{3,2,1,0:T(8,128)(4,1)}, u32[]{:S(2)}) copy-start(pred[64,4,128,128]{3,2,1,0:T(8,128)(4,1)} %iota_compare_fusion.1) | copy-start | bytes 12582916
  44.4 1.3 %copy-start.3 = (bf16[8,8,2,8,2,512]{5,3,4,2,1,0:T(8,128)(2,1)}, bf16[8,8,2,8,2,512]{5,3,4,2,1,0:T(8,128)(2,1)S(1)}, u32[]{:S(2)}) copy-start(bf16[8,8,2,8,2,512]{5,3,4,2,1,0:T(8,128)(2,1)S(1)} %all-to-all-done) | copy-start | bytes 6291460
  106.6 12.8 %collective-permute-start = (f32[1,128,128]{2,1,0:T(8,128)S(1)}, f32[1,128,128]{2,1,0:T(8,128)S(1)}, u32[]{:S(2)}, u32[]{:S(2)}) collective-permute-start(f32[1,128,128]{2,1,0:T(8,128)S(1)} %bitcast.51), channel_id=1, source_target_pairs={{0,0},{1,68},{2,136},{3,204},{4,64},{5,4},{6,128},{7,8},{8,192},{9... | collective-permute-start | bytes 196616 | tf_op jit(solution)/shard_map/ppermute | solution.py:169

commit v9 on v8

--- a/solution.py
+++ b/solution.py
@@ -4,6 +4,7 @@
 from jax.experimental import pallas as pl
 from jax.experimental.pallas import tpu as pltpu
 from jax.sharding import PartitionSpec as P
+
 
 NG = 2048
 GB = 128
@@ -38,10 +39,11 @@
     lhs_parts = []
     rhs_parts = [[] for _ in range(NF)]
     for t in range(KB):
-        x = loc_ref[:, star_ref[step * KB + t]]
-        x = x.reshape(x.shape[0] * x.shape[1], x.shape[2])
-        x_row = jnp.where(sel_ref[0] == 0, x[:, :BW], x[:, BW:])
-        x_col = jnp.where(sel_ref[1] == 0, x[:, :BW], x[:, BW:])
+        s = star_ref[step * KB + t]
+        x_row = loc_ref[:, sel_ref[0], s]
+        x_row = x_row.reshape(x_row.shape[0] * x_row.shape[1], BW)
+        x_col = loc_ref[:, sel_ref[1], s]
+        x_col = x_col.reshape(x_col.shape[0] * x_col.shape[1], BW)
         row_parts = []
         for q in range(subs):
             row_parts.append(
@@ -82,7 +84,7 @@
 
 
 def chi_block(star_map, sel, loc, onehot, weight_c):
-    rows = loc.shape[0] * loc.shape[2]
+    rows = loc.shape[0] * loc.shape[3]
     pieces = (BW // GB) ** 2
     return pl.pallas_call(
         chi_kernel,
@@ -91,7 +93,7 @@
             num_scalar_prefetch=2,
             grid=(KF // KB,),
             in_specs=[
-                pl.BlockSpec(loc.shape, lambda st, sm, se: (0, 0, 0, 0)),
+                pl.BlockSpec(loc.shape, lambda st, sm, se: (0, 0, 0, 0, 0)),
                 pl.BlockSpec((KB, 2 * BW // GB, GB, GB), lambda st, sm, se: (st, 0, 0, 0)),
                 pl.BlockSpec((KB, rows, NF), lambda st, sm, se: (st, 0, 0)),
             ],
@@ -130,13 +132,12 @@
     cond_piece = pair_density.shape[1]
     blocks = jnp.asarray(BLOCKS, jnp.int32)
 
-    blocked = pair_density.reshape(KI, cond_piece, NV, NB, BW)
-    send = jnp.stack(
-        [jnp.stack([blocked[:, :, :, a], blocked[:, :, :, b]], axis=3) for a, b in PAIR]
-    )
+    blocked = jnp.moveaxis(pair_density.reshape(KI, cond_piece, NV, NB, BW), 3, 0)
+    send = jnp.take(blocked, jnp.asarray(PAIR, jnp.int32).reshape(-1), axis=0)
+    send = send.reshape(band_count, 2, KI, cond_piece, NV, BW)
     recv = lax.all_to_all(send, "band", 0, 0, tiled=False)
     c_loc = band_count * cond_piece
-    loc = recv.reshape(band_count, KI, cond_piece * NV, 2 * BW)
+    loc = recv.reshape(band_count, 2, KI, cond_piece * NV, BW)
 
     c_base = ka_index * c_loc
     cond_grp = lax.dynamic_slice_in_dim(conduction_energy, c_base, c_loc, axis=1)

time: 121 us -> 119 us (0.983)
  local copies, waits for them, and re-layouts: 18.5 us -> 15.5 us
  other arithmetic: 20.4 us -> 22.2 us
    unnamed x23, local copies, waits for them, and re-layouts: 6.89 us -> 2.35 us
    unnamed x3 -> x0, other arithmetic: 2.2 us -> none
    gather x0 -> x1, local copies, waits for them, and re-layouts: none -> 2.03 us  [on_device(): send = jnp.take(blocked, jnp.asarray(PAIR, jnp.int32).reshape(-1), axis=0)]
  transfers between devices with their start and end apart: 2 -> 2, of which waited for: 1 -> 1; matrix products, arithmetic and copies ran while one was open for 23% -> 28% of each run, Pallas kernels for 0% -> 0%
where the time goes in v9:
time: 119 us; the launch traced here: 118 us
  blocking collectives  37.2 us (31%)
  Pallas kernels  23.3 us (20%)
  other arithmetic  22.2 us (19%)
  local copies, waits for them, and re-layouts  15.5 us (13%)
  starting transfers between devices  10.1 us (8%)
  waiting for transfers between devices  9.92 us (8%)
    all_to_all x1, blocking collectives, on_device(): got = lax.all_to_all(pieces, 'ka', 0, 0, tiled=False)  37.2 us
    pallas_call x1, Pallas kernels, chi_block(): pl.pallas_call(chi_kernel, out_shape=jax.ShapeDtypeStruct((pieces, NF, GB...  23.3 us
    ppermute x1, waiting for transfers between devices, on_device(): lax.ppermute(slab, ('ka', 'band', 'ga'), slab_perm(ka_count, band_count,...  9.91 us
    all_to_all x1, starting transfers between devices, on_device(): recv = lax.all_to_all(send, 'band', 0, 0, tiled=False)  7.18 us
    convert_element_type x1, other arithmetic, on_device(): onehot = jnp.concatenate([row_side, col_side], axis=1).astype(jnp.bfloat16)  6.44 us
    eq x1, other arithmetic, on_device(): row_side = local[:, :subs, :, None] == slot[None, None, None, :]  6.42 us
    mul x1, local copies, waits for them, and re-layouts, on_device(): weight = 4.0 / KF * diff[None] / (diff[None] * diff[None] + omega_sq) * mask  4.56 us
    ppermute x1, starting transfers between devices, on_device(): lax.ppermute(slab, ('ka', 'band', 'ga'), slab_perm(ka_count, band_count,...  2.87 us
  transfers between devices with their start and end apart: 2, of which 1 were waited for; matrix products, arithmetic and copies ran while one was open for 28% of the time, Pallas kernels for 0%

profile of v9, /device:TPU:22, one launch (start us, length us, event | category | flops | bytes accessed | tf_op | source)
XLA Modules:
  0.0 118.3 jit_solution(11092547793823260793)
XLA Ops:
  0.0 0.7 pad_clamp_fusion.3
  0.7 0.3 copy-done
  1.1 2.0 %gather_fusion = bf16[16,8,2,8,512]{4,3,2,1,0:T(8,128)(2,1)} fusion(bf16[4,8,2,8,512]{4,3,0,2,1:T(8,128)(2,1)S(1)} %bitcast.18, s32[1024]{0:T(1024)S(1)} %pad_clamp_fusion.3), kind=kCustom, calls=%fused_computation | custom fusion | bytes 4194368 | tf_op jit(solution)/shard_map/jit(_take)/gather | solution.py:136
  3.1 7.2 %all-to-all-start = ((bf16[8,2,8,2,8,512]{5,4,3,2,1,0:T(8,128)(2,1)}), bf16[8,2,8,2,8,512]{5,4,3,2,1,0:T(8,128)(2,1)S(1)}, u32[]{:S(2)}, u32[]{:S(2)}) async-start(bf16[8,2,8,2,8,512]{5,4,3,2,1,0:T(8,128)(2,1)} %bitcast.20), calls=%async_computation | async-start | bytes 4194304 | tf_op jit(solution)/shard_map/all_to_all | solution.py:138
  10.3 0.5 compare_select_fusion
  10.8 0.5 compare_and_fusion
  11.3 0.7 fusion.6
  12.0 1.2 %bitcast_multiply_fusion = s32[2]{0:T(128)} fusion(s32[8,2,2]{2,1,0:T(2,128)} %constant.118.clone, s32[]{:T(128)S(6)} %select_n.96, s32[]{:T(128)S(6)} %select_n.97), kind=kLoop, calls=%fused_computation.37 | loop fusion | flops 2 | bytes 24 | tf_op jit(solution)/shard_map/mul | solution.py:159
  13.2 1.3 %compare_and_fusion.2 = pred[2]{0:T(512)(128)(4,1)} fusion(s32[8,2,2]{2,1,0:T(2,128)} %constant.118.clone, s32[]{:T(128)S(6)} %select_n.96, s32[]{:T(128)S(6)} %select_n.97), kind=kLoop, calls=%fused_computation.29 | loop fusion | flops 12 | bytes 18 | tf_op jit(solution)/shard_map/jit(_take)/and | solution.py:156
  14.5 0.5 iota_add_fusion
  15.0 0.3 reshape.239
  15.3 0.9 gather_fusion.1
  16.1 0.8 broadcast_select_fusion
  17.0 0.2 copy.14
  17.2 0.6 gather_fusion.2
  17.8 0.2 copy.15
  18.0 0.2 gather.28
  18.2 0.7 broadcast_in_dim.83
  19.0 0.7 broadcast_in_dim.76
  20.0 6.4 %iota_compare_fusion.1 = pred[64,4,128,128]{3,2,1,0:T(8,128)(4,1)} fusion(s32[64,4,128]{2,1,0:T(4,128)S(1)} %get-tuple-element.5), kind=kLoop, calls=%fused_computation.7 | loop fusion | flops 4194304 | bytes 4325376 | tf_op jit(solution)/shard_map/eq | solution.py:162
  26.4 1.2 %fusion.3.sel_ref = s32[2]{0:T(128)} fusion(s32[8,2,2]{2,1,0:T(2,128)} %constant.120.clone, s32[]{:T(128)S(6)} %select_n.96, s32[]{:T(128)S(6)} %select_n.97), kind=kLoop, calls=%fused_computation.33 | loop fusion | bytes 24 | tf_op jit(solution)/shard_map/squeeze | solution.py:165
  27.7 0.6 gather_fusion.4
  28.4 0.6 gather_fusion.3
  29.3 4.6 %copy.18.w_ref = f32[64,128,1]{2,1,0:T(8,128)} copy(f32[64,128,1]{0,1,2:T(8,128)S(1)} %fusion.2) | data formatting | bytes 65536 | tf_op jit(solution)/shard_map/mul | solution.py:151
  33.9 2.7 %iota_compare_fusion = pred[64,4,128,128]{3,2,1,0:T(8,128)(4,1)S(1)} fusion(s32[64,4,128]{2,1,0:T(4,128)S(1)} %get-tuple-element.6), kind=kLoop, calls=%fused_computation.6 | loop fusion | flops 4194304 | bytes 4325376 | tf_op jit(solution)/shard_map/eq | solution.py:163
  36.6 6.4 %add_convert_fusion.onehot_ref = bf16[64,8,128,128]{3,2,1,0:T(8,128)(2,1)} fusion(pred[64,4,128,128]{3,2,1,0:T(8,128)(4,1)S(1)} %iota_compare_fusion, pred[64,4,128,128]{3,2,1,0:T(8,128)(4,1)S(1)} %copy-done.2), kind=kLoop, calls=%fused_computation.5 | loop fusion | flops 16777216 | bytes 25165824 | tf_op jit(solution)/shard_map/convert_element_type | solution.py:164
  43.0 1.3 %copy-done.3 = bf16[8,2,8,2,8,512]{5,4,3,2,1,0:T(8,128)(2,1)} copy-done((bf16[8,2,8,2,8,512]{5,4,3,2,1,0:T(8,128)(2,1)}, bf16[8,2,8,2,8,512]{5,4,3,2,1,0:T(8,128)(2,1)S(1)}, u32[]{:S(2)}) %copy-start.3) | copy-done | bytes 2097176
  44.4 23.3 %shard_map.100 = f32[16,1,128,128]{3,2,1,0:T(8,128)} custom-call(s32[64]{0:T(128)} %star_ref.1, s32[2]{0:T(128)} %fusion.3.sel_ref, bf16[8,2,8,16,512]{4,3,2,1,0:T(8,128)(2,1)} %bitcast.19, bf16[64,8,128,128]{3,2,1,0:T(8,128)(2,1)} %add_convert_fusion.onehot_ref, f32[64,128,1]{2,1,0:T(8,128)} %copy.18.w_ref), custom_call_target="tpu_custom_call" | custom-call | tf_op jit(solution)/shard_map/pallas_call | solution.py:89
  67.6 37.2 %all_to_all.10 = f32[16,1,128,128]{3,2,1,0:T(8,128)S(1)} all-to-all(f32[16,1,128,128]{3,2,1,0:T(8,128)} %shard_map.100), channel_id=1, replica_groups=mesh['ka'=16,'band'=8,'ga'=2] {'ka'}, dimensions={0} | all-to-all | bytes 2097152 | tf_op jit(solution)/shard_map/all_to_all | solution.py:168
  104.9 2.9 %collective-permute-start = (f32[1,128,128]{2,1,0:T(8,128)S(1)}, f32[1,128,128]{2,1,0:T(8,128)S(1)}, u32[]{:S(2)}, u32[]{:S(2)}) collective-permute-start(f32[1,128,128]{2,1,0:T(8,128)S(1)} %bitcast.22), channel_id=1, source_target_pairs={{0,0},{1,68},{2,136},{3,204},{4,64},{5,4},{6,128},{7,8},{8,192},{9... | collective-permute-start | bytes 196616 | tf_op jit(solution)/shard_map/ppermute | solution.py:170
  107.8 9.9 %collective-permute-done = f32[1,128,128]{2,1,0:T(8,128)S(1)} collective-permute-done((f32[1,128,128]{2,1,0:T(8,128)S(1)}, f32[1,128,128]{2,1,0:T(8,128)S(1)}, u32[]{:S(2)}, u32[]{:S(2)}) %collective-permute-start) | collective-permute-done | bytes 65568 | tf_op jit(solution)/shard_map/ppermute | solution.py:170
  117.7 0.6 copy.20
  (37 shorter events, 0.9 us)
Async XLA Ops:
  0.0 1.1 copy-start
  1.1 9.2 %copy-start.5 = (s32[64]{0:T(128)S(1)}, s32[64]{0:T(128)}, u32[]{:S(2)}) copy-start(s32[64]{0:T(128)} %star_ref.1) | copy-start | bytes 772
  1.1 9.2 %copy-start.8 = (s32[64]{0:T(128)S(1)}, s32[64]{0:T(128)}, u32[]{:S(2)}) copy-start(s32[64]{0:T(128)} %param.14) | copy-start | bytes 772
  1.1 13.9 %copy-start.4 = (s32[48,2048]{1,0:T(8,128)S(1)}, s32[48,2048]{1,0:T(8,128)}, u32[]{:S(2)}) copy-start(s32[48,2048]{1,0:T(8,128)} %param.15) | copy-start | bytes 1179652
  3.1 39.9 %all-to-all-start = ((bf16[8,2,8,2,8,512]{5,4,3,2,1,0:T(8,128)(2,1)}), bf16[8,2,8,2,8,512]{5,4,3,2,1,0:T(8,128)(2,1)S(1)}, u32[]{:S(2)}, u32[]{:S(2)}) async-start(bf16[8,2,8,2,8,512]{5,4,3,2,1,0:T(8,128)(2,1)} %bitcast.20), calls=%async_computation | async-start | bytes 4194304 | tf_op jit(solution)/shard_map/all_to_all | solution.py:138
  17.0 10.6 %copy-start.7 = (s32[64]{0:T(128)S(1)}, s32[64]{0:T(128)}, u32[]{:S(2)}) copy-start(s32[64]{0:T(128)} %get-tuple-element.7) | copy-start | bytes 772
  17.0 10.6 %copy-start.6 = (f32[8,256]{1,0:T(8,128)S(1)}, f32[8,256]{1,0:T(8,128)}, u32[]{:S(2)}) copy-start(f32[8,256]{1,0:T(8,128)} %param.12) | copy-start | bytes 24580
  17.0 11.4 %copy-start.1 = (f32[8,8]{1,0:T(8,128)S(1)}, f32[8,8]{1,0:T(8,128)}, u32[]{:S(2)}) copy-start(f32[8,8]{1,0:T(8,128)} %param.11) | copy-start | bytes 772
  17.0 12.2 %copy-start.9 = (s32[64]{0:T(128)S(1)}, s32[64]{0:T(128)}, u32[]{:S(2)}) copy-start(s32[64]{0:T(128)} %param.16) | copy-start | bytes 772
  17.0 12.2 %copy-start.10 = (s32[16]{0:T(128)S(1)}, s32[16]{0:T(128)}, u32[]{:S(2)}) copy-start(s32[16]{0:T(128)} %iota_add_fusion) | copy-start | bytes 196
  33.9 2.7 %copy-start.2 = (pred[64,4,128,128]{3,2,1,0:T(8,128)(4,1)S(1)}, pred[64,4,128,128]{3,2,1,0:T(8,128)(4,1)}, u32[]{:S(2)}) copy-start(pred[64,4,128,128]{3,2,1,0:T(8,128)(4,1)} %iota_compare_fusion.1) | copy-start | bytes 12582916
  43.0 1.3 %copy-start.3 = (bf16[8,2,8,2,8,512]{5,4,3,2,1,0:T(8,128)(2,1)}, bf16[8,2,8,2,8,512]{5,4,3,2,1,0:T(8,128)(2,1)S(1)}, u32[]{:S(2)}) copy-start(bf16[8,2,8,2,8,512]{5,4,3,2,1,0:T(8,128)(2,1)S(1)} %all-to-all-done) | copy-start | bytes 6291460
  104.9 12.8 %collective-permute-start = (f32[1,128,128]{2,1,0:T(8,128)S(1)}, f32[1,128,128]{2,1,0:T(8,128)S(1)}, u32[]{:S(2)}, u32[]{:S(2)}) collective-permute-start(f32[1,128,128]{2,1,0:T(8,128)S(1)} %bitcast.22), channel_id=1, source_target_pairs={{0,0},{1,68},{2,136},{3,204},{4,64},{5,4},{6,128},{7,8},{8,192},{9... | collective-permute-start | bytes 196616 | tf_op jit(solution)/shard_map/ppermute | solution.py:170

commit v10 on v9

--- a/solution.py
+++ b/solution.py
@@ -159,9 +159,12 @@
         my_blocks.repeat(subs) * BW + (jnp.arange(2 * subs) % subs) * GB
     )[None, :, None]
     slot = jnp.arange(GB)
-    row_side = local[:, :subs, :, None] == slot[None, None, None, :]
-    col_side = local[:, subs:, None, :] == slot[None, None, :, None]
-    onehot = jnp.concatenate([row_side, col_side], axis=1).astype(jnp.bfloat16)
+    row_side = local[:, :, :, None] == slot[None, None, None, :]
+    col_side = local[:, :, None, :] == slot[None, None, :, None]
+    is_row = (jnp.arange(2 * subs) < subs)[None, :, None, None]
+    onehot = jnp.where(
+        jnp.where(is_row, row_side, col_side), jnp.bfloat16(1), jnp.bfloat16(0)
+    )
     sel = jnp.asarray(LOCAL, jnp.int32)[band_index, ga_index]
     pieces = chi_block(star_map, sel, loc, onehot, weight_c)
 

time: 119 us -> 117 us (0.983)
    select_n x0 -> x1, other arithmetic: none -> 13.6 us  [on_device(): jnp.where(jnp.where(is_row, row_side, col_side), jnp.bfloat16(1), jnp.bfl...]
    eq x2 -> x0, other arithmetic: 9.11 us -> none  [the longest x1 6.42 us: on_device(): row_side = local[:, :subs, :, None] == slot[None, None, None, :]]
    convert_element_type x1 -> x0, other arithmetic: 6.44 us -> none  [on_device(): onehot = jnp.concatenate([row_side, col_side], axis=1).astype(jnp.bfloat16)]
  transfers between devices with their start and end apart: 2 -> 2, of which waited for: 1 -> 1; matrix products, arithmetic and copies ran while one was open for 28% -> 27% of each run, Pallas kernels for 0% -> 0%
where the time goes in v10:
time: 117 us
  blocking collectives  37.2 us (32%)
  Pallas kernels  23.4 us (20%)
  other arithmetic  21.6 us (18%)
  local copies, waits for them, and re-layouts  14.7 us (13%)
  starting transfers between devices  10.1 us (9%)
  waiting for transfers between devices  9.92 us (8%)
    all_to_all x1, blocking collectives, on_device(): got = lax.all_to_all(pieces, 'ka', 0, 0, tiled=False)  37.2 us
    pallas_call x1, Pallas kernels, chi_block(): pl.pallas_call(chi_kernel, out_shape=jax.ShapeDtypeStruct((pieces, NF, GB...  23.4 us
    select_n x1, other arithmetic, on_device(): jnp.where(jnp.where(is_row, row_side, col_side), jnp.bfloat16(1), jnp.bfl...  13.6 us
    ppermute x1, waiting for transfers between devices, on_device(): lax.ppermute(slab, ('ka', 'band', 'ga'), slab_perm(ka_count, band_count,...  9.91 us
    all_to_all x1, starting transfers between devices, on_device(): recv = lax.all_to_all(send, 'band', 0, 0, tiled=False)  7.18 us
    mul x1, local copies, waits for them, and re-layouts, on_device(): weight = 4.0 / KF * diff[None] / (diff[None] * diff[None] + omega_sq) * mask  4.52 us
    ppermute x1, starting transfers between devices, on_device(): lax.ppermute(slab, ('ka', 'band', 'ga'), slab_perm(ka_count, band_count,...  2.87 us
  transfers between devices with their start and end apart: 2, of which 1 were waited for; matrix products, arithmetic and copies ran while one was open for 27% of the time, Pallas kernels for 0%

profile of v10, /device:TPU:22, one launch (start us, length us, event | category | flops | bytes accessed | tf_op | source)
XLA Modules:
  0.0 117.0 jit_solution(12427054364854853749)
XLA Ops:
  0.0 0.7 pad_clamp_fusion.3
  0.8 0.3 copy-done
  1.1 2.0 %gather_fusion = bf16[16,8,2,8,512]{4,3,2,1,0:T(8,128)(2,1)} fusion(bf16[4,8,2,8,512]{4,3,0,2,1:T(8,128)(2,1)S(1)} %bitcast.18, s32[1024]{0:T(1024)S(1)} %pad_clamp_fusion.3), kind=kCustom, calls=%fused_computation | custom fusion | bytes 4194368 | tf_op jit(solution)/shard_map/jit(_take)/gather | solution.py:136
  3.1 7.2 %all-to-all-start = ((bf16[8,2,8,2,8,512]{5,4,3,2,1,0:T(8,128)(2,1)}), bf16[8,2,8,2,8,512]{5,4,3,2,1,0:T(8,128)(2,1)S(1)}, u32[]{:S(2)}, u32[]{:S(2)}) async-start(bf16[8,2,8,2,8,512]{5,4,3,2,1,0:T(8,128)(2,1)} %bitcast.20), calls=%async_computation | async-start | bytes 4194304 | tf_op jit(solution)/shard_map/all_to_all | solution.py:138
  10.2 0.5 iota_add_fusion
  10.8 0.7 fusion.8
  11.5 0.7 compare_and_fusion.2
  12.2 0.7 bitcast_multiply_fusion
  12.8 0.6 iota_compare_fusion.2
  13.4 0.5 compare_and_fusion
  13.9 1.2 %fusion.5.sel_ref = s32[2]{0:T(128)} fusion(s32[8,2,2]{2,1,0:T(2,128)} %constant.125.clone, s32[]{:T(128)S(6)} %select_n.112, s32[]{:T(128)S(6)} %select_n.113), kind=kLoop, calls=%fused_computation.34 | loop fusion | bytes 24 | tf_op jit(solution)/shard_map/squeeze | solution.py:168
  15.2 0.6 broadcast_in_dim.95
  16.0 0.6 fusion.7
  16.6 0.6 pad_clamp_fusion.2
  17.2 0.6 gather_fusion.4
  18.0 0.6 gather_fusion.3
  18.7 0.3 reshape.253
  19.0 1.0 gather_fusion.1
  20.0 0.8 broadcast_select_fusion
  20.9 0.6 gather_fusion.2
  21.5 0.2 copy.15
  21.7 0.2 gather.28
  22.0 0.7 compare_convert_fusion
  22.7 4.5 %copy.18.w_ref = f32[64,128,1]{2,1,0:T(8,128)} copy(f32[64,128,1]{0,1,2:T(8,128)S(1)} %fusion.4) | data formatting | bytes 65536 | tf_op jit(solution)/shard_map/mul | solution.py:151
  27.2 0.7 select_subtract_fusion
  28.0 13.6 %fusion.1.onehot_ref = bf16[64,8,128,128]{3,2,1,0:T(8,128)(2,1)} fusion(s32[64,8,128]{2,1,0:T(8,128)S(1)} %select_subtract_fusion, pred[8]{0:T(512)(128)(4,1)} %iota_compare_fusion.2), kind=kLoop, calls=%fused_computation.8 | loop fusion | flops 33554432 | bytes 17039368 | tf_op jit(solution)/shard_map/jit(_where)/select_n | solution.py:165
  41.6 1.3 %copy-done.2 = bf16[8,2,8,2,8,512]{5,4,3,2,1,0:T(8,128)(2,1)} copy-done((bf16[8,2,8,2,8,512]{5,4,3,2,1,0:T(8,128)(2,1)}, bf16[8,2,8,2,8,512]{5,4,3,2,1,0:T(8,128)(2,1)S(1)}, u32[]{:S(2)}) %copy-start.2) | copy-done | bytes 2097176
  42.9 23.4 %shard_map.100 = f32[16,1,128,128]{3,2,1,0:T(8,128)} custom-call(s32[64]{0:T(128)} %star_ref.1, s32[2]{0:T(128)} %fusion.5.sel_ref, bf16[8,2,8,16,512]{4,3,2,1,0:T(8,128)(2,1)} %bitcast.19, bf16[64,8,128,128]{3,2,1,0:T(8,128)(2,1)} %fusion.1.onehot_ref, f32[64,128,1]{2,1,0:T(8,128)} %copy.18.w_ref), custom_call_target="tpu_custom_call" | custom-call | tf_op jit(solution)/shard_map/pallas_call | solution.py:89
  66.3 37.2 %all_to_all.10 = f32[16,1,128,128]{3,2,1,0:T(8,128)S(1)} all-to-all(f32[16,1,128,128]{3,2,1,0:T(8,128)} %shard_map.100), channel_id=1, replica_groups=mesh['ka'=16,'band'=8,'ga'=2] {'ka'}, dimensions={0} | all-to-all | bytes 2097152 | tf_op jit(solution)/shard_map/all_to_all | solution.py:171
  103.6 2.9 %collective-permute-start = (f32[1,128,128]{2,1,0:T(8,128)S(1)}, f32[1,128,128]{2,1,0:T(8,128)S(1)}, u32[]{:S(2)}, u32[]{:S(2)}) collective-permute-start(f32[1,128,128]{2,1,0:T(8,128)S(1)} %bitcast.22), channel_id=1, source_target_pairs={{0,0},{1,68},{2,136},{3,204},{4,64},{5,4},{6,128},{7,8},{8,192},{9... | collective-permute-start | bytes 196616 | tf_op jit(solution)/shard_map/ppermute | solution.py:173
  106.4 9.9 %collective-permute-done = f32[1,128,128]{2,1,0:T(8,128)S(1)} collective-permute-done((f32[1,128,128]{2,1,0:T(8,128)S(1)}, f32[1,128,128]{2,1,0:T(8,128)S(1)}, u32[]{:S(2)}, u32[]{:S(2)}) %collective-permute-start) | collective-permute-done | bytes 65568 | tf_op jit(solution)/shard_map/ppermute | solution.py:173
  116.4 0.6 copy.20
  (27 shorter events, 0.9 us)
Async XLA Ops:
  0.0 1.1 copy-start
  0.0 13.4 %copy-start.4 = (s32[64]{0:T(128)S(1)}, s32[64]{0:T(128)}, u32[]{:S(2)}) copy-start(s32[64]{0:T(128)} %star_ref.1) | copy-start | bytes 772
  0.0 13.4 %copy-start.6 = (s32[64]{0:T(128)S(1)}, s32[64]{0:T(128)}, u32[]{:S(2)}) copy-start(s32[64]{0:T(128)} %param.14) | copy-start | bytes 772
  0.0 17.2 %copy-start.5 = (f32[8,256]{1,0:T(8,128)S(1)}, f32[8,256]{1,0:T(8,128)}, u32[]{:S(2)}) copy-start(f32[8,256]{1,0:T(8,128)} %param.12) | copy-start | bytes 24580
  0.0 18.0 %copy-start.1 = (f32[8,8]{1,0:T(8,128)S(1)}, f32[8,8]{1,0:T(8,128)}, u32[]{:S(2)}) copy-start(f32[8,8]{1,0:T(8,128)} %param.11) | copy-start | bytes 772
  0.0 18.7 %copy-start.3 = (s32[48,2048]{1,0:T(8,128)S(1)}, s32[48,2048]{1,0:T(8,128)}, u32[]{:S(2)}) copy-start(s32[48,2048]{1,0:T(8,128)} %param.15) | copy-start | bytes 1179652
  3.1 38.5 %all-to-all-start = ((bf16[8,2,8,2,8,512]{5,4,3,2,1,0:T(8,128)(2,1)}), bf16[8,2,8,2,8,512]{5,4,3,2,1,0:T(8,128)(2,1)S(1)}, u32[]{:S(2)}, u32[]{:S(2)}) async-start(bf16[8,2,8,2,8,512]{5,4,3,2,1,0:T(8,128)(2,1)} %bitcast.20), calls=%async_computation | async-start | bytes 4194304 | tf_op jit(solution)/shard_map/all_to_all | solution.py:138
  41.6 1.3 %copy-start.2 = (bf16[8,2,8,2,8,512]{5,4,3,2,1,0:T(8,128)(2,1)}, bf16[8,2,8,2,8,512]{5,4,3,2,1,0:T(8,128)(2,1)S(1)}, u32[]{:S(2)}) copy-start(bf16[8,2,8,2,8,512]{5,4,3,2,1,0:T(8,128)(2,1)S(1)} %all-to-all-done) | copy-start | bytes 6291460
  103.6 12.8 %collective-permute-start = (f32[1,128,128]{2,1,0:T(8,128)S(1)}, f32[1,128,128]{2,1,0:T(8,128)S(1)}, u32[]{:S(2)}, u32[]{:S(2)}) collective-permute-start(f32[1,128,128]{2,1,0:T(8,128)S(1)} %bitcast.22), channel_id=1, source_target_pairs={{0,0},{1,68},{2,136},{3,204},{4,64},{5,4},{6,128},{7,8},{8,192},{9... | collective-permute-start | bytes 196616 | tf_op jit(solution)/shard_map/ppermute | solution.py:173

commit v11 on v10

--- a/solution.py
+++ b/solution.py
@@ -21,13 +21,13 @@
     tuple((PAIR[j][LOCAL[j][g][0]], PAIR[j][LOCAL[j][g][1]]) for g in range(2))
     for j in range(len(PAIR))
 )
-KB = 8
+KB = 16
 
 
 freq_step = 2.0
 
 
-def chi_kernel(star_ref, sel_ref, loc_ref, onehot_ref, w_ref, out_ref, acc_ref):
+def chi_kernel(star_ref, sel_ref, loc_ref, onehot_ref, w_ref, out_ref, acc_ref, row_ref, hi_ref, lo_ref):
     step = pl.program_id(0)
 
     @pl.when(step == 0)
@@ -36,42 +36,39 @@
 
     nt = (((1,), (1,)), ((), ()))
     subs = BW // GB
-    lhs_parts = []
-    rhs_parts = [[] for _ in range(NF)]
-    for t in range(KB):
-        s = star_ref[step * KB + t]
-        x_row = loc_ref[:, sel_ref[0], s]
-        x_row = x_row.reshape(x_row.shape[0] * x_row.shape[1], BW)
-        x_col = loc_ref[:, sel_ref[1], s]
-        x_col = x_col.reshape(x_col.shape[0] * x_col.shape[1], BW)
-        row_parts = []
-        for q in range(subs):
-            row_parts.append(
-                lax.dot_general(
-                    onehot_ref[t, q], x_row[:, q * GB : (q + 1) * GB], nt,
-                    preferred_element_type=jnp.float32,
+    for f in range(NF):
+        for t in range(KB):
+            s = star_ref[step * KB + t]
+            x_row = loc_ref[:, sel_ref[0], s]
+            x_row = x_row.reshape(x_row.shape[0] * x_row.shape[1], BW)
+            x_col = loc_ref[:, sel_ref[1], s]
+            x_col = x_col.reshape(x_col.shape[0] * x_col.shape[1], BW)
+            rows = x_row.shape[0]
+            if f == 0:
+                for q in range(subs):
+                    row_ref[q * GB : (q + 1) * GB, t * rows : (t + 1) * rows] = lax.dot_general(
+                        onehot_ref[t, q], x_row[:, q * GB : (q + 1) * GB], nt,
+                        preferred_element_type=jnp.float32,
+                    ).astype(jnp.bfloat16)
+            col_parts = []
+            for q in range(subs, 2 * subs):
+                col_parts.append(
+                    jnp.dot(
+                        x_col[:, (q - subs) * GB : (q - subs + 1) * GB], onehot_ref[t, q],
+                        preferred_element_type=jnp.float32,
+                    )
                 )
-            )
-        row_t = jnp.concatenate(row_parts, axis=0).astype(jnp.bfloat16)
-        col_parts = []
-        for q in range(subs, 2 * subs):
-            col_parts.append(
-                jnp.dot(
-                    x_col[:, (q - subs) * GB : (q - subs + 1) * GB], onehot_ref[t, q],
-                    preferred_element_type=jnp.float32,
-                )
-            )
-        col = jnp.concatenate(col_parts, axis=1)
-        lhs_parts += [row_t, row_t]
-        for f in range(NF):
+            col = jnp.concatenate(col_parts, axis=1)
             product = col * w_ref[t][:, f : f + 1]
             scaled_hi = product.astype(jnp.bfloat16)
-            scaled_lo = (product - scaled_hi.astype(jnp.float32)).astype(jnp.bfloat16)
-            rhs_parts[f] += [scaled_hi, scaled_lo]
-    lhs = jnp.concatenate(lhs_parts, axis=1)
-    for f in range(NF):
-        rhs = jnp.concatenate(rhs_parts[f], axis=0)
-        acc_ref[f] += jnp.dot(lhs, rhs, preferred_element_type=jnp.float32)
+            hi_ref[t * rows : (t + 1) * rows, :] = scaled_hi
+            lo_ref[t * rows : (t + 1) * rows, :] = (
+                product - scaled_hi.astype(jnp.float32)
+            ).astype(jnp.bfloat16)
+        lhs = row_ref[...]
+        acc_ref[f] += jnp.dot(lhs, hi_ref[...], preferred_element_type=jnp.float32) + jnp.dot(
+            lhs, lo_ref[...], preferred_element_type=jnp.float32
+        )
 
     @pl.when(step == pl.num_programs(0) - 1)
     def _():
@@ -95,10 +92,15 @@
             in_specs=[
                 pl.BlockSpec(loc.shape, lambda st, sm, se: (0, 0, 0, 0, 0)),
                 pl.BlockSpec((KB, 2 * BW // GB, GB, GB), lambda st, sm, se: (st, 0, 0, 0)),
-                pl.BlockSpec((KB, rows, NF), lambda st, sm, se: (st, 0, 0)),
+                pl.BlockSpec((KB, rows, GB), lambda st, sm, se: (st, 0, 0)),
             ],
             out_specs=pl.BlockSpec((pieces, NF, GB, GB), lambda st, sm, se: (0, 0, 0, 0)),
-            scratch_shapes=[pltpu.VMEM((NF, BW, BW), jnp.float32)],
+            scratch_shapes=[
+                pltpu.VMEM((NF, BW, BW), jnp.float32),
+                pltpu.VMEM((BW, KB * rows), jnp.bfloat16),
+                pltpu.VMEM((KB * rows, BW), jnp.bfloat16),
+                pltpu.VMEM((KB * rows, BW), jnp.bfloat16),
+            ],
         ),
         compiler_params=pltpu.CompilerParams(dimension_semantics=("arbitrary",)),
     )(star_map, sel, loc, onehot, weight_c)
@@ -149,7 +151,9 @@
     omega_sq = (omega * omega)[:, None, None, None]
     diff = val_local[:, None, :] - cond_local[:, :, None]
     weight = 4.0 / KF * diff[None] / (diff[None] * diff[None] + omega_sq) * mask
-    weight_c = jnp.transpose(weight.reshape(NF, KF, c_loc * NV), (1, 2, 0))
+    weight_c = jnp.broadcast_to(
+        jnp.transpose(weight.reshape(NF, KF, c_loc * NV), (1, 2, 0)), (KF, c_loc * NV, GB)
+    )
 
     my_blocks = blocks[band_index, ga_index]
     perm_blocks = perm_lists.reshape(perm_lists.shape[0], NB, BW)

time: 117 us -> 117 us (level); the launches traced: 117 us -> 115 us
  local copies, waits for them, and re-layouts: 14.7 us -> 11.5 us
  other arithmetic: 21.6 us -> 19.9 us
  starting transfers between devices: 10.1 us -> 11.7 us
    mul x1, local copies, waits for them, and re-layouts: 4.52 us -> 0.7 us  [on_device(): weight = 4.0 / KF * diff[None] / (diff[None] * diff[None] + omega_sq) * mask]
    broadcast_in_dim x0 -> x1, local copies, waits for them, and re-layouts: none -> 2.57 us  [on_device(): jnp.broadcast_to(jnp.transpose(weight.reshape(NF, KF, c_loc * NV), (1, 2,...]
    all_to_all x1, waiting for transfers between devices: 0.01 us -> 2.14 us  [on_device(): recv = lax.all_to_all(send, 'band', 0, 0, tiled=False)]
    ppermute x1, starting transfers between devices: 2.87 us -> 4.49 us  [on_device(): lax.ppermute(slab, ('ka', 'band', 'ga'), slab_perm(ka_count, band_count,...]
    ppermute x1, waiting for transfers between devices: 9.91 us -> 8.61 us  [on_device(): lax.ppermute(slab, ('ka', 'band', 'ga'), slab_perm(ka_count, band_count,...]
    unnamed x15 -> x19, local copies, waits for them, and re-layouts: 2.24 us -> 0.94 us
  transfers between devices with their start and end apart: 2 -> 2, of which waited for: 1 -> 2; matrix products, arithmetic and copies ran while one was open for 27% -> 22% of each run, Pallas kernels for 0% -> 0%
where the time goes in v11:
time: 117 us; the launch traced here: 115 us
  blocking collectives  37.1 us (32%)
  Pallas kernels  23.7 us (20%)
  other arithmetic  19.9 us (17%)
  starting transfers between devices  11.7 us (10%)
  local copies, waits for them, and re-layouts  11.5 us (10%)
  waiting for transfers between devices  10.7 us (9%)
    all_to_all x1, blocking collectives, on_device(): got = lax.all_to_all(pieces, 'ka', 0, 0, tiled=False)  37.1 us
    pallas_call x1, Pallas kernels, chi_block(): pl.pallas_call(chi_kernel, out_shape=jax.ShapeDtypeStruct((pieces, NF, GB...  23.7 us
    select_n x1, other arithmetic, on_device(): jnp.where(jnp.where(is_row, row_side, col_side), jnp.bfloat16(1), jnp.bfl...  13.5 us
    ppermute x1, waiting for transfers between devices, on_device(): lax.ppermute(slab, ('ka', 'band', 'ga'), slab_perm(ka_count, band_count,...  8.61 us
    all_to_all x1, starting transfers between devices, on_device(): recv = lax.all_to_all(send, 'band', 0, 0, tiled=False)  7.18 us
    ppermute x1, starting transfers between devices, on_device(): lax.ppermute(slab, ('ka', 'band', 'ga'), slab_perm(ka_count, band_count,...  4.49 us
    broadcast_in_dim x1, local copies, waits for them, and re-layouts, on_device(): jnp.broadcast_to(jnp.transpose(weight.reshape(NF, KF, c_loc * NV), (1, 2,...  2.57 us
  transfers between devices with their start and end apart: 2, of which 2 were waited for; matrix products, arithmetic and copies ran while one was open for 22% of the time, Pallas kernels for 0%

profile of v11, /device:TPU:22, one launch (start us, length us, event | category | flops | bytes accessed | tf_op | source)
XLA Modules:
  0.0 114.8 jit_solution(9562824531472195795)
XLA Ops:
  0.1 0.7 pad_clamp_fusion.3
  0.8 0.3 copy-done
  1.1 2.0 %gather_fusion = bf16[16,8,2,8,512]{4,3,2,1,0:T(8,128)(2,1)} fusion(bf16[4,8,2,8,512]{4,3,0,2,1:T(8,128)(2,1)S(1)} %bitcast.18, s32[1024]{0:T(1024)S(1)} %pad_clamp_fusion.3), kind=kCustom, calls=%fused_computation | custom fusion | bytes 4194368 | tf_op jit(solution)/shard_map/jit(_take)/gather | solution.py:138
  3.1 7.2 %all-to-all-start = ((bf16[8,2,8,2,8,512]{5,4,3,2,1,0:T(8,128)(2,1)}), bf16[8,2,8,2,8,512]{5,4,3,2,1,0:T(8,128)(2,1)S(1)}, u32[]{:S(2)}, u32[]{:S(2)}) async-start(bf16[8,2,8,2,8,512]{5,4,3,2,1,0:T(8,128)(2,1)} %bitcast.20), calls=%async_computation | async-start | bytes 4194304 | tf_op jit(solution)/shard_map/all_to_all | solution.py:140
  10.3 0.7 fusion.8
  10.9 0.7 compare_and_fusion.2
  11.6 0.7 bitcast_multiply_fusion
  12.3 0.5 iota_compare_fusion.2
  12.8 0.6 compare_and_fusion
  13.4 1.3 %fusion.5.sel_ref = s32[2]{0:T(128)} fusion(s32[8,2,2]{2,1,0:T(2,128)} %constant.125.clone, s32[]{:T(128)S(6)} %select_n.112, s32[]{:T(128)S(6)} %select_n.113), kind=kLoop, calls=%fused_computation.34 | loop fusion | bytes 24 | tf_op jit(solution)/shard_map/squeeze | solution.py:172
  14.8 0.1 broadcast_in_dim.100
  14.9 0.1 mul.62
  15.0 0.6 fusion.7
  15.7 0.6 gather_fusion.4
  16.4 0.6 gather_fusion.3
  17.3 0.7 copy.18
  18.0 0.3 reshape.234
  18.3 0.9 gather_fusion.1
  19.2 0.8 broadcast_select_fusion
  20.0 0.2 copy.14
  20.2 0.6 gather_fusion.2
  20.8 0.2 copy.15
  21.0 0.2 gather.28
  21.2 0.7 select_subtract_fusion
  22.0 13.5 %fusion.1.onehot_ref = bf16[64,8,128,128]{3,2,1,0:T(8,128)(2,1)} fusion(s32[64,8,128]{2,1,0:T(8,128)S(1)} %select_subtract_fusion, pred[8]{0:T(512)(128)(4,1)} %iota_compare_fusion.2), kind=kLoop, calls=%fused_computation.8 | loop fusion | flops 33554432 | bytes 17039368 | tf_op jit(solution)/shard_map/jit(_where)/select_n | solution.py:169
  35.5 2.1 %all-to-all-done = bf16[8,2,8,2,8,512]{5,4,3,2,1,0:T(8,128)(2,1)S(1)} async-done(((bf16[8,2,8,2,8,512]{5,4,3,2,1,0:T(8,128)(2,1)}), bf16[8,2,8,2,8,512]{5,4,3,2,1,0:T(8,128)(2,1)S(1)}, u32[]{:S(2)}, u32[]{:S(2)}) %all-to-all-start) | async-done | bytes 2097184 | tf_op jit(solution)/shard_map/all_to_all | solution.py:140
  37.6 2.6 %broadcast_in_dim.114.w_ref = f32[64,128,128]{2,1,0:T(8,128)} broadcast(f32[64,128]{1,0:T(8,128)S(1)} %copy-done.4), dimensions={0,1} | broadcast | bytes 4227072 | tf_op jit(solution)/shard_map/broadcast_in_dim | solution.py:154
  40.2 23.7 %shard_map.100 = f32[16,1,128,128]{3,2,1,0:T(8,128)} custom-call(s32[64]{0:T(128)} %star_ref.1, s32[2]{0:T(128)} %fusion.5.sel_ref, bf16[8,2,8,16,512]{4,3,2,1,0:T(8,128)(2,1)} %bitcast.19, bf16[64,8,128,128]{3,2,1,0:T(8,128)(2,1)} %fusion.1.onehot_ref, f32[64,128,128]{2,1,0:T(8,128)} %broadcast_in_dim.114.w_ref), custom_call_target="tpu_custom_call" | custom-call | tf_op jit(solution)/shard_map/pallas_call | solution.py:86
  63.9 37.1 %all_to_all.10 = f32[16,1,128,128]{3,2,1,0:T(8,128)S(1)} all-to-all(f32[16,1,128,128]{3,2,1,0:T(8,128)} %shard_map.100), channel_id=1, replica_groups=mesh['ka'=16,'band'=8,'ga'=2] {'ka'}, dimensions={0} | all-to-all | bytes 2097152 | tf_op jit(solution)/shard_map/all_to_all | solution.py:175
  101.0 4.5 %collective-permute-start = (f32[1,128,128]{2,1,0:T(8,128)S(1)}, f32[1,128,128]{2,1,0:T(8,128)S(1)}, u32[]{:S(2)}, u32[]{:S(2)}) collective-permute-start(f32[1,128,128]{2,1,0:T(8,128)S(1)} %bitcast.22), channel_id=1, source_target_pairs={{0,0},{1,68},{2,136},{3,204},{4,64},{5,4},{6,128},{7,8},{8,192},{9... | collective-permute-start | bytes 196616 | tf_op jit(solution)/shard_map/ppermute | solution.py:177
  105.5 8.6 %collective-permute-done = f32[1,128,128]{2,1,0:T(8,128)S(1)} collective-permute-done((f32[1,128,128]{2,1,0:T(8,128)S(1)}, f32[1,128,128]{2,1,0:T(8,128)S(1)}, u32[]{:S(2)}, u32[]{:S(2)}) %collective-permute-start) | collective-permute-done | bytes 65568 | tf_op jit(solution)/shard_map/ppermute | solution.py:177
  114.1 0.6 copy.20
  (32 shorter events, 0.7 us)
Async XLA Ops:
  0.0 1.1 copy-start
  0.0 12.8 %copy-start.5 = (s32[64]{0:T(128)S(1)}, s32[64]{0:T(128)}, u32[]{:S(2)}) copy-start(s32[64]{0:T(128)} %star_ref.1) | copy-start | bytes 772
  0.0 12.8 %copy-start.7 = (s32[64]{0:T(128)S(1)}, s32[64]{0:T(128)}, u32[]{:S(2)}) copy-start(s32[64]{0:T(128)} %param.14) | copy-start | bytes 772
  0.0 15.6 %copy-start.6 = (f32[8,256]{1,0:T(8,128)S(1)}, f32[8,256]{1,0:T(8,128)}, u32[]{:S(2)}) copy-start(f32[8,256]{1,0:T(8,128)} %param.12) | copy-start | bytes 24580
  0.0 16.4 %copy-start.1 = (f32[8,8]{1,0:T(8,128)S(1)}, f32[8,8]{1,0:T(8,128)}, u32[]{:S(2)}) copy-start(f32[8,8]{1,0:T(8,128)} %param.11) | copy-start | bytes 772
  0.0 17.2 %copy-start.8 = (s32[64]{0:T(128)S(1)}, s32[64]{0:T(128)}, u32[]{:S(2)}) copy-start(s32[64]{0:T(128)} %param.16) | copy-start | bytes 772
  0.0 18.0 %copy-start.3 = (s32[48,2048]{1,0:T(8,128)S(1)}, s32[48,2048]{1,0:T(8,128)}, u32[]{:S(2)}) copy-start(s32[48,2048]{1,0:T(8,128)} %param.15) | copy-start | bytes 1179652
  3.1 34.5 %all-to-all-start = ((bf16[8,2,8,2,8,512]{5,4,3,2,1,0:T(8,128)(2,1)}), bf16[8,2,8,2,8,512]{5,4,3,2,1,0:T(8,128)(2,1)S(1)}, u32[]{:S(2)}, u32[]{:S(2)}) async-start(bf16[8,2,8,2,8,512]{5,4,3,2,1,0:T(8,128)(2,1)} %bitcast.20), calls=%async_computation | async-start | bytes 4194304 | tf_op jit(solution)/shard_map/all_to_all | solution.py:140
  21.9 15.7 %copy-start.4 = (f32[64,128]{1,0:T(8,128)S(1)}, f32[64,128]{1,0:T(8,128)}, u32[]{:S(2)}) copy-start(f32[64,128]{1,0:T(8,128)} %copy.18) | copy-start | bytes 98308
  37.6 2.6 %copy-start.2 = (bf16[8,2,8,2,8,512]{5,4,3,2,1,0:T(8,128)(2,1)}, bf16[8,2,8,2,8,512]{5,4,3,2,1,0:T(8,128)(2,1)S(1)}, u32[]{:S(2)}) copy-start(bf16[8,2,8,2,8,512]{5,4,3,2,1,0:T(8,128)(2,1)S(1)} %all-to-all-done) | copy-start | bytes 6291460
  101.0 13.1 %collective-permute-start = (f32[1,128,128]{2,1,0:T(8,128)S(1)}, f32[1,128,128]{2,1,0:T(8,128)S(1)}, u32[]{:S(2)}, u32[]{:S(2)}) collective-permute-start(f32[1,128,128]{2,1,0:T(8,128)S(1)} %bitcast.22), channel_id=1, source_target_pairs={{0,0},{1,68},{2,136},{3,204},{4,64},{5,4},{6,128},{7,8},{8,192},{9... | collective-permute-start | bytes 196616 | tf_op jit(solution)/shard_map/ppermute | solution.py:177

commit v12 on v10

--- a/solution.py
+++ b/solution.py
@@ -93,9 +93,9 @@
             num_scalar_prefetch=2,
             grid=(KF // KB,),
             in_specs=[
-                pl.BlockSpec(loc.shape, lambda st, sm, se: (0, 0, 0, 0, 0)),
+                pl.BlockSpec(memory_space=pltpu.VMEM),
                 pl.BlockSpec((KB, 2 * BW // GB, GB, GB), lambda st, sm, se: (st, 0, 0, 0)),
-                pl.BlockSpec((KB, rows, NF), lambda st, sm, se: (st, 0, 0)),
+                pl.BlockSpec((KB, rows, GB), lambda st, sm, se: (st, 0, 0)),
             ],
             out_specs=pl.BlockSpec((pieces, NF, GB, GB), lambda st, sm, se: (0, 0, 0, 0)),
             scratch_shapes=[pltpu.VMEM((NF, BW, BW), jnp.float32)],
@@ -149,7 +149,9 @@
     omega_sq = (omega * omega)[:, None, None, None]
     diff = val_local[:, None, :] - cond_local[:, :, None]
     weight = 4.0 / KF * diff[None] / (diff[None] * diff[None] + omega_sq) * mask
-    weight_c = jnp.transpose(weight.reshape(NF, KF, c_loc * NV), (1, 2, 0))
+    weight_c = jnp.broadcast_to(
+        jnp.transpose(weight.reshape(NF, KF, c_loc * NV), (1, 2, 0)), (KF, c_loc * NV, GB)
+    )
 
     my_blocks = blocks[band_index, ga_index]
     perm_blocks = perm_lists.reshape(perm_lists.shape[0], NB, BW)

time: 117 us -> 116 us (level); the launches traced: 117 us -> 114 us
  local copies, waits for them, and re-layouts: 14.7 us -> 11.5 us
  other arithmetic: 21.6 us -> 19.9 us
  starting transfers between devices: 10.1 us -> 11.7 us
    mul x1, local copies, waits for them, and re-layouts: 4.52 us -> 0.7 us  [on_device(): weight = 4.0 / KF * diff[None] / (diff[None] * diff[None] + omega_sq) * mask]
    broadcast_in_dim x0 -> x1, local copies, waits for them, and re-layouts: none -> 2.57 us  [on_device(): jnp.broadcast_to(jnp.transpose(weight.reshape(NF, KF, c_loc * NV), (1, 2,...]
    all_to_all x1, waiting for transfers between devices: 0.01 us -> 2.14 us  [on_device(): recv = lax.all_to_all(send, 'band', 0, 0, tiled=False)]
    ppermute x1, starting transfers between devices: 2.87 us -> 4.49 us  [on_device(): lax.ppermute(slab, ('ka', 'band', 'ga'), slab_perm(ka_count, band_count,...]
    ppermute x1, waiting for transfers between devices: 9.91 us -> 8.6 us  [on_device(): lax.ppermute(slab, ('ka', 'band', 'ga'), slab_perm(ka_count, band_count,...]
    unnamed x15 -> x19, local copies, waits for them, and re-layouts: 2.24 us -> 0.94 us
  transfers between devices with their start and end apart: 2 -> 2, of which waited for: 1 -> 2; matrix products, arithmetic and copies ran while one was open for 27% -> 22% of each run, Pallas kernels for 0% -> 0%
where the time goes in v12:
time: 116 us; the launch traced here: 114 us
  blocking collectives  37.1 us (32%)
  Pallas kernels  23.4 us (20%)
  other arithmetic  19.9 us (17%)
  starting transfers between devices  11.7 us (10%)
  local copies, waits for them, and re-layouts  11.5 us (10%)
  waiting for transfers between devices  10.7 us (9%)
    all_to_all x1, blocking collectives, on_device(): got = lax.all_to_all(pieces, 'ka', 0, 0, tiled=False)  37.1 us
    pallas_call x1, Pallas kernels, chi_block(): pl.pallas_call(chi_kernel, out_shape=jax.ShapeDtypeStruct((pieces, NF, GB...  23.4 us
    select_n x1, other arithmetic, on_device(): jnp.where(jnp.where(is_row, row_side, col_side), jnp.bfloat16(1), jnp.bfl...  13.5 us
    ppermute x1, waiting for transfers between devices, on_device(): lax.ppermute(slab, ('ka', 'band', 'ga'), slab_perm(ka_count, band_count,...  8.6 us
    all_to_all x1, starting transfers between devices, on_device(): recv = lax.all_to_all(send, 'band', 0, 0, tiled=False)  7.18 us
    ppermute x1, starting transfers between devices, on_device(): lax.ppermute(slab, ('ka', 'band', 'ga'), slab_perm(ka_count, band_count,...  4.49 us
    broadcast_in_dim x1, local copies, waits for them, and re-layouts, on_device(): jnp.broadcast_to(jnp.transpose(weight.reshape(NF, KF, c_loc * NV), (1, 2,...  2.57 us
  transfers between devices with their start and end apart: 2, of which 2 were waited for; matrix products, arithmetic and copies ran while one was open for 22% of the time, Pallas kernels for 0%

profile of v12, /device:TPU:22, one launch (start us, length us, event | category | flops | bytes accessed | tf_op | source)
XLA Modules:
  0.0 114.5 jit_solution(16071770260749145148)
XLA Ops:
  0.1 0.7 pad_clamp_fusion.3
  0.8 0.3 copy-done
  1.1 2.0 %gather_fusion = bf16[16,8,2,8,512]{4,3,2,1,0:T(8,128)(2,1)} fusion(bf16[4,8,2,8,512]{4,3,0,2,1:T(8,128)(2,1)S(1)} %bitcast.18, s32[1024]{0:T(1024)S(1)} %pad_clamp_fusion.3), kind=kCustom, calls=%fused_computation | custom fusion | bytes 4194368 | tf_op jit(solution)/shard_map/jit(_take)/gather | solution.py:136
  3.1 7.2 %all-to-all-start = ((bf16[8,2,8,2,8,512]{5,4,3,2,1,0:T(8,128)(2,1)}), bf16[8,2,8,2,8,512]{5,4,3,2,1,0:T(8,128)(2,1)S(1)}, u32[]{:S(2)}, u32[]{:S(2)}) async-start(bf16[8,2,8,2,8,512]{5,4,3,2,1,0:T(8,128)(2,1)} %bitcast.20), calls=%async_computation | async-start | bytes 4194304 | tf_op jit(solution)/shard_map/all_to_all | solution.py:138
  10.3 0.7 fusion.8
  10.9 0.7 compare_and_fusion.2
  11.6 0.7 bitcast_multiply_fusion
  12.3 0.5 iota_compare_fusion.2
  12.8 0.6 compare_and_fusion
  13.4 1.3 %fusion.5.sel_ref = s32[2]{0:T(128)} fusion(s32[8,2,2]{2,1,0:T(2,128)} %constant.125.clone, s32[]{:T(128)S(6)} %select_n.112, s32[]{:T(128)S(6)} %select_n.113), kind=kLoop, calls=%fused_computation.34 | loop fusion | bytes 24 | tf_op jit(solution)/shard_map/squeeze | solution.py:170
  14.8 0.1 broadcast_in_dim.100
  14.9 0.1 mul.62
  15.0 0.6 fusion.7
  15.7 0.6 gather_fusion.4
  16.4 0.6 gather_fusion.3
  17.3 0.7 copy.18
  18.0 0.3 reshape.234
  18.3 0.9 gather_fusion.1
  19.2 0.8 broadcast_select_fusion
  20.0 0.2 copy.14
  20.2 0.6 gather_fusion.2
  20.8 0.2 copy.15
  21.0 0.2 gather.28
  21.2 0.7 select_subtract_fusion
  22.0 13.5 %fusion.1.onehot_ref = bf16[64,8,128,128]{3,2,1,0:T(8,128)(2,1)} fusion(s32[64,8,128]{2,1,0:T(8,128)S(1)} %select_subtract_fusion, pred[8]{0:T(512)(128)(4,1)} %iota_compare_fusion.2), kind=kLoop, calls=%fused_computation.8 | loop fusion | flops 33554432 | bytes 17039368 | tf_op jit(solution)/shard_map/jit(_where)/select_n | solution.py:167
  35.5 2.1 %all-to-all-done = bf16[8,2,8,2,8,512]{5,4,3,2,1,0:T(8,128)(2,1)S(1)} async-done(((bf16[8,2,8,2,8,512]{5,4,3,2,1,0:T(8,128)(2,1)}), bf16[8,2,8,2,8,512]{5,4,3,2,1,0:T(8,128)(2,1)S(1)}, u32[]{:S(2)}, u32[]{:S(2)}) %all-to-all-start) | async-done | bytes 2097184 | tf_op jit(solution)/shard_map/all_to_all | solution.py:138
  37.6 2.6 %broadcast_in_dim.114.w_ref = f32[64,128,128]{2,1,0:T(8,128)} broadcast(f32[64,128]{1,0:T(8,128)S(1)} %copy-done.4), dimensions={0,1} | broadcast | bytes 4227072 | tf_op jit(solution)/shard_map/broadcast_in_dim | solution.py:152
  40.2 23.4 %shard_map.100 = f32[16,1,128,128]{3,2,1,0:T(8,128)} custom-call(s32[64]{0:T(128)} %star_ref.1, s32[2]{0:T(128)} %fusion.5.sel_ref, bf16[8,2,8,16,512]{4,3,2,1,0:T(8,128)(2,1)} %bitcast.19, bf16[64,8,128,128]{3,2,1,0:T(8,128)(2,1)} %fusion.1.onehot_ref, f32[64,128,128]{2,1,0:T(8,128)} %broadcast_in_dim.114.w_ref), custom_call_target="tpu_custom_call" | custom-call | tf_op jit(solution)/shard_map/pallas_call | solution.py:89
  63.6 37.1 %all_to_all.10 = f32[16,1,128,128]{3,2,1,0:T(8,128)S(1)} all-to-all(f32[16,1,128,128]{3,2,1,0:T(8,128)} %shard_map.100), channel_id=1, replica_groups=mesh['ka'=16,'band'=8,'ga'=2] {'ka'}, dimensions={0} | all-to-all | bytes 2097152 | tf_op jit(solution)/shard_map/all_to_all | solution.py:173
  100.7 4.5 %collective-permute-start = (f32[1,128,128]{2,1,0:T(8,128)S(1)}, f32[1,128,128]{2,1,0:T(8,128)S(1)}, u32[]{:S(2)}, u32[]{:S(2)}) collective-permute-start(f32[1,128,128]{2,1,0:T(8,128)S(1)} %bitcast.22), channel_id=1, source_target_pairs={{0,0},{1,68},{2,136},{3,204},{4,64},{5,4},{6,128},{7,8},{8,192},{9... | collective-permute-start | bytes 196616 | tf_op jit(solution)/shard_map/ppermute | solution.py:175
  105.2 8.6 %collective-permute-done = f32[1,128,128]{2,1,0:T(8,128)S(1)} collective-permute-done((f32[1,128,128]{2,1,0:T(8,128)S(1)}, f32[1,128,128]{2,1,0:T(8,128)S(1)}, u32[]{:S(2)}, u32[]{:S(2)}) %collective-permute-start) | collective-permute-done | bytes 65568 | tf_op jit(solution)/shard_map/ppermute | solution.py:175
  113.8 0.6 copy.20
  (32 shorter events, 0.7 us)
Async XLA Ops:
  0.0 1.1 copy-start
  0.0 12.8 %copy-start.5 = (s32[64]{0:T(128)S(1)}, s32[64]{0:T(128)}, u32[]{:S(2)}) copy-start(s32[64]{0:T(128)} %star_ref.1) | copy-start | bytes 772
  0.0 12.8 %copy-start.7 = (s32[64]{0:T(128)S(1)}, s32[64]{0:T(128)}, u32[]{:S(2)}) copy-start(s32[64]{0:T(128)} %param.14) | copy-start | bytes 772
  0.0 15.6 %copy-start.6 = (f32[8,256]{1,0:T(8,128)S(1)}, f32[8,256]{1,0:T(8,128)}, u32[]{:S(2)}) copy-start(f32[8,256]{1,0:T(8,128)} %param.12) | copy-start | bytes 24580
  0.0 16.4 %copy-start.1 = (f32[8,8]{1,0:T(8,128)S(1)}, f32[8,8]{1,0:T(8,128)}, u32[]{:S(2)}) copy-start(f32[8,8]{1,0:T(8,128)} %param.11) | copy-start | bytes 772
  0.0 17.2 %copy-start.8 = (s32[64]{0:T(128)S(1)}, s32[64]{0:T(128)}, u32[]{:S(2)}) copy-start(s32[64]{0:T(128)} %param.16) | copy-start | bytes 772
  0.0 18.0 %copy-start.3 = (s32[48,2048]{1,0:T(8,128)S(1)}, s32[48,2048]{1,0:T(8,128)}, u32[]{:S(2)}) copy-start(s32[48,2048]{1,0:T(8,128)} %param.15) | copy-start | bytes 1179652
  3.1 34.5 %all-to-all-start = ((bf16[8,2,8,2,8,512]{5,4,3,2,1,0:T(8,128)(2,1)}), bf16[8,2,8,2,8,512]{5,4,3,2,1,0:T(8,128)(2,1)S(1)}, u32[]{:S(2)}, u32[]{:S(2)}) async-start(bf16[8,2,8,2,8,512]{5,4,3,2,1,0:T(8,128)(2,1)} %bitcast.20), calls=%async_computation | async-start | bytes 4194304 | tf_op jit(solution)/shard_map/all_to_all | solution.py:138
  21.9 15.7 %copy-start.4 = (f32[64,128]{1,0:T(8,128)S(1)}, f32[64,128]{1,0:T(8,128)}, u32[]{:S(2)}) copy-start(f32[64,128]{1,0:T(8,128)} %copy.18) | copy-start | bytes 98308
  37.6 2.6 %copy-start.2 = (bf16[8,2,8,2,8,512]{5,4,3,2,1,0:T(8,128)(2,1)}, bf16[8,2,8,2,8,512]{5,4,3,2,1,0:T(8,128)(2,1)S(1)}, u32[]{:S(2)}) copy-start(bf16[8,2,8,2,8,512]{5,4,3,2,1,0:T(8,128)(2,1)S(1)} %all-to-all-done) | copy-start | bytes 6291460
  100.7 13.1 %collective-permute-start = (f32[1,128,128]{2,1,0:T(8,128)S(1)}, f32[1,128,128]{2,1,0:T(8,128)S(1)}, u32[]{:S(2)}, u32[]{:S(2)}) collective-permute-start(f32[1,128,128]{2,1,0:T(8,128)S(1)} %bitcast.22), channel_id=1, source_target_pairs={{0,0},{1,68},{2,136},{3,204},{4,64},{5,4},{6,128},{7,8},{8,192},{9... | collective-permute-start | bytes 196616 | tf_op jit(solution)/shard_map/ppermute | solution.py:175
